TPU v7x, 256 devices: a whole 4x4x8 slice. The times are simulated.
256 devices in a mesh: lat: 8 (over y_hi, x), lon: 32 (over y_lo, z, core).
Axes of the slice: x: 4, y: 4 (y_hi: 2, y_lo: 2; y = y_hi * 2 + y_lo), z: 8, core: 2. Of those that a mesh axis runs over, the one named last changes fastest.
Arguments:
- thickness: float32 [8, 256, 4096], P(None, 'lat', 'lon'), may hold values from 0.5 to 1.5
- winds: float32 [2, 8, 256, 4096], P(None, None, 'lat', 'lon'), may hold values from -2.5 to 2.5
- tracer_mass: float32 [8, 8, 256, 4096], P(None, None, 'lat', 'lon'), may hold values from -6 to 6
Outputs:
- thickness_out: float32 [8, 256, 4096], P(None, 'lat', 'lon')
- winds_out: float32 [2, 8, 256, 4096], P(None, None, 'lat', 'lon')
- tracer_out: float32 [8, 8, 256, 4096], P(None, None, 'lat', 'lon')
All inputs are finite; a program needn't handle non-finite values.
Results may differ from a plain program's by a relative error of at most 0.0003.
Values sent between devices are 32-bit elements; how exact they have to be, the bound alone decides.
No kernel may reach another device: no remote copies, remote signals or barrier semaphores. Data moves between devices by JAX's collectives and lax.ppermute only.
A program may use at most 64 MiB of HBM per device.

v0:
```python
import math

import jax
import jax.numpy as jnp
from jax import lax
from jax.sharding import PartitionSpec as P

SUBSTEPS = 2


COUR = 0.25
GRAV = 1.0
FCOR = 1.0


def padded_2(cells, sides, width, closed):
    for axis, dim in sides:
        count = lax.axis_size(axis)
        ends = count if closed else count - 1
        head = lax.slice_in_dim(cells, 0, width, axis=dim)
        tail = lax.slice_in_dim(cells, cells.shape[dim] - width, cells.shape[dim], axis=dim)
        cells = jnp.concatenate(
            [
                lax.ppermute(tail, axis, [(i, (i + 1) % count) for i in range(ends)]),
                cells,
                lax.ppermute(head, axis, [((i + 1) % count, i) for i in range(ends)]),
            ],
            axis=dim,
        )
    return cells


def shifted(block, axis, distance):
    devices = range(lax.axis_size(axis))
    route = [((i - distance) % len(devices), i) for i in devices]
    return lax.ppermute(block, axis, route)


def geopot(thick):
    return GRAV * jnp.flip(jnp.cumsum(jnp.flip(thick, 0), 0), 0)


def upwind(face_speed, behind, centre, forward, beyond):
    return (
        face_speed
        * jnp.where(
            face_speed >= 0.0,
            5.0 * centre + 2.0 * forward - behind,
            5.0 * forward + 2.0 * centre - beyond,
        )
        / 6.0
    )


def advance(padded, potential, row_start, spacing):
    height = padded.shape[-2]
    columns = padded.shape[-1]
    row_index = (jnp.arange(height) + row_start).astype(jnp.float32)
    center_lat = (row_index[2 : height - 2] + 0.5) * spacing - 0.5 * math.pi
    face_lat = (row_index[1 : height - 2] + 1.0) * spacing - 0.5 * math.pi
    center_cos = jnp.cos(center_lat)[:, None]
    face_cos = jnp.abs(jnp.cos(face_lat))[:, None]
    coriolis = FCOR * jnp.sin(center_lat)[:, None] * jnp.where(center_cos >= 0.0, 1.0, -1.0)
    band_rows = padded[..., 2 : height - 2, :]
    zonal_wind = band_rows[1]
    face_speed = COUR * 0.5 * (zonal_wind[..., 1 : columns - 2] + zonal_wind[..., 2 : columns - 1])
    zonal_flux = upwind(
        face_speed,
        band_rows[..., 0 : columns - 3],
        band_rows[..., 1 : columns - 2],
        band_rows[..., 2 : columns - 1],
        band_rows[..., 3:columns],
    )
    zonal_div = zonal_flux[..., 1:] - zonal_flux[..., :-1]
    column_strip = padded[..., 2 : columns - 2]
    merid_wind = column_strip[2]
    merid_speed = (
        COUR
        * 0.5
        * (merid_wind[..., 1 : height - 2, :] + merid_wind[..., 2 : height - 1, :])
        * face_cos
    )
    merid_flux = upwind(
        merid_speed,
        column_strip[..., 0 : height - 3, :],
        column_strip[..., 1 : height - 2, :],
        column_strip[..., 2 : height - 1, :],
        column_strip[..., 3:height, :],
    )
    merid_div = (merid_flux[..., 1:, :] - merid_flux[..., :-1, :]) / jnp.abs(center_cos)
    center = padded[..., 2 : height - 2, 2 : columns - 2]
    advected = center - zonal_div - merid_div
    push_x = (
        COUR
        * 0.5
        * (
            potential[..., 2 : height - 2, 3 : columns - 1]
            - potential[..., 2 : height - 2, 1 : columns - 3]
        )
    )
    push_y = (
        COUR
        * 0.5
        * (
            potential[..., 3 : height - 1, 2 : columns - 2]
            - potential[..., 1 : height - 3, 2 : columns - 2]
        )
    )
    east_wind = advected[1] - push_x + COUR * coriolis * center[2]
    north_wind = advected[2] - push_y - COUR * coriolis * center[1]
    return jnp.concatenate([advected[0:1], east_wind[None], north_wind[None], advected[3:]], 0)


def extend(fields, margin, band_index):
    local_rows = fields.shape[2]
    last_band = lax.axis_size("lat") - 1
    lat_padded = padded_2(fields, (("lat", 2),), margin, False)
    sign_vector = jnp.where(jnp.arange(fields.shape[0]) == 2, -1.0, 1.0).astype(jnp.float32)[
        :, None, None, None
    ]
    south_rows = jnp.flip(fields[:, :, 0:margin], 2)
    north_rows = jnp.flip(fields[:, :, local_rows - margin :], 2)
    outgoing = jnp.where(band_index == 0, south_rows, north_rows) * sign_vector
    received = shifted(outgoing, "lon", lax.axis_size("lon") // 2)
    lat_padded = lat_padded.at[:, :, 0:margin].set(
        jnp.where(band_index == 0, received, lat_padded[:, :, 0:margin])
    )
    lat_padded = lat_padded.at[:, :, local_rows + margin :].set(
        jnp.where(band_index == last_band, received, lat_padded[:, :, local_rows + margin :])
    )
    return padded_2(lat_padded, (("lon", 3),), margin, True)


def shards(thickness, winds, tracer_mass):
    fields = jnp.concatenate([thickness[None], winds, tracer_mass], 0)
    local_rows = thickness.shape[1]
    spacing = math.pi / (local_rows * lax.axis_size("lat"))
    band_index = lax.axis_index("lat")
    for substep in range(SUBSTEPS):
        padded = extend(fields, 2, band_index)
        fields = advance(padded, geopot(padded[0]), band_index * local_rows - 2, spacing)
    return (fields[0], fields[1:3], fields[3:])


def solution(mesh):
    return jax.shard_map(
        shards,
        mesh=mesh,
        in_specs=(P(None, "lat", "lon"), P(None, None, "lat", "lon"), P(None, None, "lat", "lon")),
        out_specs=(P(None, "lat", "lon"), P(None, None, "lat", "lon"), P(None, None, "lat", "lon")),
        check_vma=False,
    )
```

profile of v0, /device:TPU:103, one launch (start us, length us, event | category | flops | bytes accessed | tf_op | source)
XLA Modules:
  0.0 93.4 jit_solution(12643360513912589225)
XLA Ops:
  0.6 1.4 %pad_maximum_fusion.6 = f32[11,8,32,128]{3,2,1,0:T(8,128)S(1)} fusion(f32[8,8,32,128]{3,2,1,0:T(8,128)} %param.13, f32[2,8,32,128]{3,2,1,0:T(8,128)} %param.12, f32[1,8,32,128]{3,2,1,0:T(8,128)} %bitcast.79), kind=kLoop, calls=%fused_computation.48 | loop fusion | flops 720896 | bytes 2883584 | tf_op jit(solution)/shard_map/concatenate | solution.py:135
  3.0 4.7 %collective-permute-start = (f32[11,8,2,128]{3,1,2,0:T(8,128)S(1)}, f32[11,8,2,128]{3,1,2,0:T(8,128)S(1)}, u32[]{:S(2)}, u32[]{:S(2)}) collective-permute-start(f32[11,8,2,128]{3,1,2,0:T(8,128)S(1)} %get-tuple-element.78), channel_id=1, source_target_pairs={{0,32},{32,64},{64,96},{96,128},{128,160},{160,192},{192,224},{1,3... | collective-permute-start | bytes 270344 | tf_op jit(solution)/shard_map/ppermute | solution.py:24
  7.8 1.9 %collective-permute-start.1 = (f32[11,8,2,128]{3,1,2,0:T(8,128)S(1)}, f32[11,8,2,128]{3,1,2,0:T(8,128)S(1)}, u32[]{:S(2)}, u32[]{:S(2)}) collective-permute-start(f32[11,8,2,128]{3,1,2,0:T(8,128)S(1)} %get-tuple-element.79), channel_id=1, source_target_pairs={{32,0},{64,32},{96,64},{128,96},{160,128},{192,160},{224,192},{33,... | collective-permute-start | bytes 270344 | tf_op jit(solution)/shard_map/ppermute | solution.py:26
  10.5 6.2 %collective-permute-done.1 = f32[11,8,2,128]{3,1,2,0:T(8,128)S(1)} collective-permute-done((f32[11,8,2,128]{3,1,2,0:T(8,128)S(1)}, f32[11,8,2,128]{3,1,2,0:T(8,128)S(1)}, u32[]{:S(2)}, u32[]{:S(2)}) %collective-permute-start.1) | collective-permute-done | bytes 90144 | tf_op jit(solution)/shard_map/ppermute | solution.py:26
  17.0 1.7 %fusion.59 = (f32[11,8,36,2]{3,1,2,0:T(8,128)}, f32[11,8,36,2]{3,1,2,0:T(8,128)S(1)}) fusion(f32[11,8,36,128]{3,1,2,0:T(8,128)S(1)} %fusion.49), kind=kLoop, calls=%fused_computation.119 | loop fusion | bytes 101376 | tf_op jit(solution)/shard_map/slice | solution.py:21
  18.7 2.1 %copy.41 = f32[11,8,36,2]{2,1,3,0:T(8,128)S(1)} copy(f32[11,8,36,2]{3,1,2,0:T(8,128)} %get-tuple-element.74) | data formatting | bytes 50688 | tf_op jit(solution)/shard_map/slice | solution.py:21
  20.9 4.8 %collective-permute-start.3 = (f32[11,8,36,2]{2,1,3,0:T(8,128)S(1)}, f32[11,8,36,2]{2,1,3,0:T(8,128)}, u32[]{:S(2)}, u32[]{:S(2)}) collective-permute-start(f32[11,8,36,2]{2,1,3,0:T(8,128)S(1)} %copy.41), channel_id=1, source_target_pairs={{0,1},{1,2},{2,3},{3,4},{4,5},{5,6},{6,7},{7,8},{8,9},{9,10},{10,1... | collective-permute-start | bytes 76040 | tf_op jit(solution)/shard_map/ppermute | solution.py:24
  25.6 1.4 %copy.42 = f32[11,8,36,2]{2,1,3,0:T(8,128)} copy(f32[11,8,36,2]{3,1,2,0:T(8,128)S(1)} %get-tuple-element.75) | data formatting | bytes 50688 | tf_op jit(solution)/shard_map/slice | solution.py:20
  27.1 1.6 %fusion.19 = f32[11,8,33,128]{3,1,2,0:T(8,128)} fusion(f32[11,8,36,128]{3,1,2,0:T(8,128)S(1)} %fusion.49, f32[8,33,128]{2,0,1:T(8,128)S(1)} %get-tuple-element.67, pred[8,33,128]{2,0,1:T(8,128)(4,1)S(1)} %get-tuple-element.66), kind=kLoop, calls=%fused_computation.36 | loop fusion | flops 4088832 | bytes 7603200 | tf_op jit(solution)/shard_map/div | solution.py:45
  28.7 1.6 %copy.43 = f32[11,8,36,2]{3,1,2,0:T(8,128)S(1)} copy(f32[11,8,36,2]{2,1,3,0:T(8,128)} %collective-permute-done.3) | data formatting | bytes 50688 | tf_op jit(solution)/shard_map/ppermute | solution.py:24
  30.3 2.2 %collective-permute-done.4 = f32[11,8,36,2]{2,1,3,0:T(8,128)} collective-permute-done((f32[11,8,36,2]{2,1,3,0:T(8,128)}, f32[11,8,36,2]{2,1,3,0:T(8,128)}, u32[]{:S(2)}, u32[]{:S(2)}) %collective-permute-start.4) | collective-permute-done | bytes 25376 | tf_op jit(solution)/shard_map/ppermute | solution.py:26
  32.5 2.8 %copy.44 = f32[11,8,36,2]{3,1,2,0:T(8,128)} copy(f32[11,8,36,2]{2,1,3,0:T(8,128)} %collective-permute-done.4) | data formatting | bytes 50688 | tf_op jit(solution)/shard_map/ppermute | solution.py:26
  35.3 1.2 %fusion.27 = f32[8,36,132]{2,0,1:T(8,128)S(1)} fusion(f32[11,8,36,2]{3,1,2,0:T(8,128)} %copy.44, f32[11,8,36,128]{3,1,2,0:T(8,128)S(1)} %fusion.49, f32[11,8,36,2]{3,1,2,0:T(8,128)S(1)} %copy.43), kind=kLoop, calls=%fused_computation.53 | loop fusion | flops 76032 | bytes 1824768 | tf_op jit(solution)/shard_map/squeeze | solution.py:141
  37.2 3.2 %fusion.12 = f32[11,8,32,129]{3,1,2,0:T(8,128)S(1)} fusion(f32[11,8,36,2]{3,1,2,0:T(8,128)S(1)} %copy-done, f32[11,8,36,128]{3,1,2,0:T(8,128)S(1)} %fusion.49, f32[11,8,36,2]{3,1,2,0:T(8,128)S(1)} %copy.43, f32[8,32,129]{2,0,1:T(8,128)S(1)} %get-tuple-element.65, pred[8,32,129]{2,0,1:T(8,128)(4,1)S(1)} %get-tuple-element.64), kind=kLoop, calls=%fused_computation.23 | loop fusion | flops 5448960 | bytes 3290880 | tf_op jit(solution)/shard_map/div | solution.py:45
  42.9 1.2 %reduce_window_sum.17 = f32[8,36,132]{2,0,1:T(8,128)S(1)} reduce-window(f32[8,36,132]{2,0,1:T(8,128)} %rev.24, f32[]{:T(128)} %constant.143.clone.1), window={size=8x1x1 pad=7_0x0_0x0_0}, to_apply=%region_0.1 | reduce-window | flops 266112 | bytes 304132 | tf_op jit(solution)/shard_map/jit(cumsum)/reduce_window_sum | solution.py:40
  47.0 3.7 %collective-permute-start.5 = (f32[11,8,2,128]{3,1,2,0:T(8,128)S(1)}, f32[11,8,2,128]{3,1,2,0:T(8,128)S(1)}, u32[]{:S(2)}, u32[]{:S(2)}) collective-permute-start(f32[11,8,2,128]{3,1,2,0:T(8,128)S(1)} %get-tuple-element.76), channel_id=1, source_target_pairs={{0,32},{32,64},{64,96},{96,128},{128,160},{160,192},{192,224},{1,3... | collective-permute-start | bytes 270344 | tf_op jit(solution)/shard_map/ppermute | solution.py:24
  50.8 1.9 %collective-permute-start.6 = (f32[11,8,2,128]{3,1,2,0:T(8,128)S(1)}, f32[11,8,2,128]{3,1,2,0:T(8,128)S(1)}, u32[]{:S(2)}, u32[]{:S(2)}) collective-permute-start(f32[11,8,2,128]{3,1,2,0:T(8,128)S(1)} %get-tuple-element.77), channel_id=1, source_target_pairs={{32,0},{64,32},{96,64},{128,96},{160,128},{192,160},{224,192},{33,... | collective-permute-start | bytes 270344 | tf_op jit(solution)/shard_map/ppermute | solution.py:26
  53.3 6.4 %collective-permute-done.6 = f32[11,8,2,128]{3,1,2,0:T(8,128)S(1)} collective-permute-done((f32[11,8,2,128]{3,1,2,0:T(8,128)S(1)}, f32[11,8,2,128]{3,1,2,0:T(8,128)S(1)}, u32[]{:S(2)}, u32[]{:S(2)}) %collective-permute-start.6) | collective-permute-done | bytes 90144 | tf_op jit(solution)/shard_map/ppermute | solution.py:26
  59.8 1.7 %fusion.58 = (f32[11,8,36,2]{3,1,2,0:T(8,128)}, f32[11,8,36,2]{3,1,2,0:T(8,128)S(1)}) fusion(f32[11,8,36,128]{3,1,2,0:T(8,128)S(1)} %fusion.48), kind=kLoop, calls=%fused_computation.118 | loop fusion | bytes 101376 | tf_op jit(solution)/shard_map/slice | solution.py:21
  61.6 2.1 %copy.47 = f32[11,8,36,2]{2,1,3,0:T(8,128)S(1)} copy(f32[11,8,36,2]{3,1,2,0:T(8,128)} %get-tuple-element.72) | data formatting | bytes 50688 | tf_op jit(solution)/shard_map/slice | solution.py:21
  63.7 2.5 %collective-permute-start.8 = (f32[11,8,36,2]{2,1,3,0:T(8,128)S(1)}, f32[11,8,36,2]{2,1,3,0:T(8,128)}, u32[]{:S(2)}, u32[]{:S(2)}) collective-permute-start(f32[11,8,36,2]{2,1,3,0:T(8,128)S(1)} %copy.47), channel_id=1, source_target_pairs={{0,1},{1,2},{2,3},{3,4},{4,5},{5,6},{6,7},{7,8},{8,9},{9,10},{10,1... | collective-permute-start | bytes 76040 | tf_op jit(solution)/shard_map/ppermute | solution.py:24
  66.2 1.4 %copy.48 = f32[11,8,36,2]{2,1,3,0:T(8,128)} copy(f32[11,8,36,2]{3,1,2,0:T(8,128)S(1)} %get-tuple-element.73) | data formatting | bytes 50688 | tf_op jit(solution)/shard_map/slice | solution.py:20
  67.7 1.6 %fusion.16 = f32[11,8,33,128]{3,1,2,0:T(8,128)} fusion(f32[11,8,36,128]{3,1,2,0:T(8,128)S(1)} %fusion.48, f32[8,33,128]{2,0,1:T(8,128)S(1)} %get-tuple-element.63, pred[8,33,128]{2,0,1:T(8,128)(4,1)S(1)} %get-tuple-element.62), kind=kLoop, calls=%fused_computation.31 | loop fusion | flops 4088832 | bytes 7603200 | tf_op jit(solution)/shard_map/div | solution.py:45
  69.3 1.6 %copy.49 = f32[11,8,36,2]{3,1,2,0:T(8,128)S(1)} copy(f32[11,8,36,2]{2,1,3,0:T(8,128)} %collective-permute-done.8) | data formatting | bytes 50688 | tf_op jit(solution)/shard_map/ppermute | solution.py:24
  70.9 2.2 %collective-permute-done.9 = f32[11,8,36,2]{2,1,3,0:T(8,128)} collective-permute-done((f32[11,8,36,2]{2,1,3,0:T(8,128)}, f32[11,8,36,2]{2,1,3,0:T(8,128)}, u32[]{:S(2)}, u32[]{:S(2)}) %collective-permute-start.9) | collective-permute-done | bytes 25376 | tf_op jit(solution)/shard_map/ppermute | solution.py:26
  73.0 2.8 %copy.50 = f32[11,8,36,2]{3,1,2,0:T(8,128)} copy(f32[11,8,36,2]{2,1,3,0:T(8,128)} %collective-permute-done.9) | data formatting | bytes 50688 | tf_op jit(solution)/shard_map/ppermute | solution.py:26
  75.9 1.2 %fusion.26 = f32[8,36,132]{2,0,1:T(8,128)S(1)} fusion(f32[11,8,36,2]{3,1,2,0:T(8,128)} %copy.50, f32[11,8,36,128]{3,1,2,0:T(8,128)S(1)} %fusion.48, f32[11,8,36,2]{3,1,2,0:T(8,128)S(1)} %copy.49), kind=kLoop, calls=%fused_computation.50 | loop fusion | flops 76032 | bytes 1824768 | tf_op jit(solution)/shard_map/squeeze | solution.py:141
  77.8 3.2 %fusion.7 = f32[11,8,32,129]{3,1,2,0:T(8,128)S(1)} fusion(f32[11,8,36,2]{3,1,2,0:T(8,128)S(1)} %copy-done.1, f32[11,8,36,128]{3,1,2,0:T(8,128)S(1)} %fusion.48, f32[11,8,36,2]{3,1,2,0:T(8,128)S(1)} %copy.49, f32[8,32,129]{2,0,1:T(8,128)S(1)} %get-tuple-element.61, pred[8,32,129]{2,0,1:T(8,128)(4,1)S(1)} %get-tuple-element.60), kind=kLoop, calls=%fused_computation.16 | loop fusion | flops 5448960 | bytes 3290880 | tf_op jit(solution)/shard_map/div | solution.py:45
  84.0 1.2 %reduce_window_sum.18 = f32[8,36,132]{2,0,1:T(8,128)S(1)} reduce-window(f32[8,36,132]{2,0,1:T(8,128)} %rev.27, f32[]{:T(128)} %constant.143.clone.1), window={size=8x1x1 pad=7_0x0_0x0_0}, to_apply=%region_1.2 | reduce-window | flops 266112 | bytes 304132 | tf_op jit(solution)/shard_map/jit(cumsum)/reduce_window_sum | solution.py:40
  88.0 1.6 %slice.455 = f32[8,32,128]{2,0,1:T(8,128)} reverse(f32[8,32,128]{2,0,1:T(8,128)} %get-tuple-element.81), dimensions={0} | reverse | bytes 262144 | tf_op jit(solution)/shard_map/slice | solution.py:106
  89.5 1.1 %fusion.38 = (f32[1,8,32,128]{3,1,2,0:T(8,128)S(1)}, f32[1,8,32,128]{3,1,2,0:T(8,128)S(1)}) fusion(f32[11,8,36,128]{3,1,2,0:T(8,128)S(1)} %fusion.48, f32[11,8,32,128]{3,1,2,0:T(8,128)S(1)} %fusion.21, f32[8,32,128]{2,0,1:T(8,128)S(1)} %slice.447, f32[8,32,128]{2,0,1:T(8,128)S(1)} %slice.449, f32[32]{0:T(128)S(1)} %get-tuple-element.88, ...), kind=kLoop, calls=%fused_computation.77 | loop fusion | flops 327680 | bytes 1310848 | tf_op jit(solution)/shard_map/broadcast_in_dim | solution.py:111
  90.8 1.2 %copy.56 = f32[8,8,32,128]{3,2,1,0:T(8,128)} copy(f32[8,8,32,128]{3,1,2,0:T(8,128)S(1)} %copy-done.5) | data formatting | bytes 2097152
  (69 shorter events, 16.9 us)
Async XLA Ops:
  3.0 7.5 %collective-permute-start = (f32[11,8,2,128]{3,1,2,0:T(8,128)S(1)}, f32[11,8,2,128]{3,1,2,0:T(8,128)S(1)}, u32[]{:S(2)}, u32[]{:S(2)}) collective-permute-start(f32[11,8,2,128]{3,1,2,0:T(8,128)S(1)} %get-tuple-element.78), channel_id=1, source_target_pairs={{0,32},{32,64},{64,96},{96,128},{128,160},{160,192},{192,224},{1,3... | collective-permute-start | bytes 270344 | tf_op jit(solution)/shard_map/ppermute | solution.py:24
  7.8 9.0 %collective-permute-start.1 = (f32[11,8,2,128]{3,1,2,0:T(8,128)S(1)}, f32[11,8,2,128]{3,1,2,0:T(8,128)S(1)}, u32[]{:S(2)}, u32[]{:S(2)}) collective-permute-start(f32[11,8,2,128]{3,1,2,0:T(8,128)S(1)} %get-tuple-element.79), channel_id=1, source_target_pairs={{32,0},{64,32},{96,64},{128,96},{160,128},{192,160},{224,192},{33,... | collective-permute-start | bytes 270344 | tf_op jit(solution)/shard_map/ppermute | solution.py:26
  9.8 7.1 %collective-permute-start.2 = (f32[11,8,2,128]{3,1,2,0:T(8,128)S(1)}, f32[11,8,2,128]{3,1,2,0:T(8,128)S(1)}, u32[]{:S(2)}, u32[]{:S(2)}) collective-permute-start(f32[11,8,2,128]{3,1,2,0:T(8,128)S(1)} %select_multiply_fusion.1), channel_id=1, source_target_pairs={{16,0},{17,1},{18,2},{19,3},{20,4},{21,5},{22,6},{23,7},{24,8},{25... | collective-permute-start | bytes 270344 | tf_op jit(solution)/shard_map/ppermute | solution.py:36
  20.9 7.8 %collective-permute-start.3 = (f32[11,8,36,2]{2,1,3,0:T(8,128)S(1)}, f32[11,8,36,2]{2,1,3,0:T(8,128)}, u32[]{:S(2)}, u32[]{:S(2)}) collective-permute-start(f32[11,8,36,2]{2,1,3,0:T(8,128)S(1)} %copy.41), channel_id=1, source_target_pairs={{0,1},{1,2},{2,3},{3,4},{4,5},{5,6},{6,7},{7,8},{8,9},{9,10},{10,1... | collective-permute-start | bytes 76040 | tf_op jit(solution)/shard_map/ppermute | solution.py:24
  27.0 5.5 %collective-permute-start.4 = (f32[11,8,36,2]{2,1,3,0:T(8,128)}, f32[11,8,36,2]{2,1,3,0:T(8,128)}, u32[]{:S(2)}, u32[]{:S(2)}) collective-permute-start(f32[11,8,36,2]{2,1,3,0:T(8,128)} %copy.42), channel_id=1, source_target_pairs={{1,0},{2,1},{3,2},{4,3},{5,4},{6,5},{7,6},{8,7},{9,8},{10,9},{11,1... | collective-permute-start | bytes 76040 | tf_op jit(solution)/shard_map/ppermute | solution.py:26
  35.3 1.5 %copy-start = (f32[11,8,36,2]{3,1,2,0:T(8,128)S(1)}, f32[11,8,36,2]{3,1,2,0:T(8,128)}, u32[]{:S(2)}) copy-start(f32[11,8,36,2]{3,1,2,0:T(8,128)} %copy.44) | copy-start | bytes 76036
  37.2 3.2 %copy-start.3 = (f32[11,8,33,128]{3,1,2,0:T(8,128)S(1)}, f32[11,8,33,128]{3,1,2,0:T(8,128)}, u32[]{:S(2)}) copy-start(f32[11,8,33,128]{3,1,2,0:T(8,128)} %fusion.19) | copy-start | bytes 4460548
  41.0 1.1 %copy-start.4 = (f32[11,8,32,128]{3,1,2,0:T(8,128)}, f32[11,8,32,128]{3,1,2,0:T(8,128)S(1)}, u32[]{:S(2)}) copy-start(f32[11,8,32,128]{3,1,2,0:T(8,128)S(1)} %fusion.24) | copy-start | bytes 4325380
  47.0 6.2 %collective-permute-start.5 = (f32[11,8,2,128]{3,1,2,0:T(8,128)S(1)}, f32[11,8,2,128]{3,1,2,0:T(8,128)S(1)}, u32[]{:S(2)}, u32[]{:S(2)}) collective-permute-start(f32[11,8,2,128]{3,1,2,0:T(8,128)S(1)} %get-tuple-element.76), channel_id=1, source_target_pairs={{0,32},{32,64},{64,96},{96,128},{128,160},{160,192},{192,224},{1,3... | collective-permute-start | bytes 270344 | tf_op jit(solution)/shard_map/ppermute | solution.py:24
  50.8 8.9 %collective-permute-start.6 = (f32[11,8,2,128]{3,1,2,0:T(8,128)S(1)}, f32[11,8,2,128]{3,1,2,0:T(8,128)S(1)}, u32[]{:S(2)}, u32[]{:S(2)}) collective-permute-start(f32[11,8,2,128]{3,1,2,0:T(8,128)S(1)} %get-tuple-element.77), channel_id=1, source_target_pairs={{32,0},{64,32},{96,64},{128,96},{160,128},{192,160},{224,192},{33,... | collective-permute-start | bytes 270344 | tf_op jit(solution)/shard_map/ppermute | solution.py:26
  52.8 7.0 %collective-permute-start.7 = (f32[11,8,2,128]{3,1,2,0:T(8,128)S(1)}, f32[11,8,2,128]{3,1,2,0:T(8,128)S(1)}, u32[]{:S(2)}, u32[]{:S(2)}) collective-permute-start(f32[11,8,2,128]{3,1,2,0:T(8,128)S(1)} %select_multiply_fusion), channel_id=1, source_target_pairs={{16,0},{17,1},{18,2},{19,3},{20,4},{21,5},{22,6},{23,7},{24,8},{25... | collective-permute-start | bytes 270344 | tf_op jit(solution)/shard_map/ppermute | solution.py:36
  63.7 5.5 %collective-permute-start.8 = (f32[11,8,36,2]{2,1,3,0:T(8,128)S(1)}, f32[11,8,36,2]{2,1,3,0:T(8,128)}, u32[]{:S(2)}, u32[]{:S(2)}) collective-permute-start(f32[11,8,36,2]{2,1,3,0:T(8,128)S(1)} %copy.47), channel_id=1, source_target_pairs={{0,1},{1,2},{2,3},{3,4},{4,5},{5,6},{6,7},{7,8},{8,9},{9,10},{10,1... | collective-permute-start | bytes 76040 | tf_op jit(solution)/shard_map/ppermute | solution.py:24
  67.6 5.5 %collective-permute-start.9 = (f32[11,8,36,2]{2,1,3,0:T(8,128)}, f32[11,8,36,2]{2,1,3,0:T(8,128)}, u32[]{:S(2)}, u32[]{:S(2)}) collective-permute-start(f32[11,8,36,2]{2,1,3,0:T(8,128)} %copy.48), channel_id=1, source_target_pairs={{1,0},{2,1},{3,2},{4,3},{5,4},{6,5},{7,6},{8,7},{9,8},{10,9},{11,1... | collective-permute-start | bytes 76040 | tf_op jit(solution)/shard_map/ppermute | solution.py:26
  75.9 1.5 %copy-start.1 = (f32[11,8,36,2]{3,1,2,0:T(8,128)S(1)}, f32[11,8,36,2]{3,1,2,0:T(8,128)}, u32[]{:S(2)}) copy-start(f32[11,8,36,2]{3,1,2,0:T(8,128)} %copy.50) | copy-start | bytes 76036
  77.8 3.2 %copy-start.2 = (f32[11,8,33,128]{3,1,2,0:T(8,128)S(1)}, f32[11,8,33,128]{3,1,2,0:T(8,128)}, u32[]{:S(2)}) copy-start(f32[11,8,33,128]{3,1,2,0:T(8,128)} %fusion.16) | copy-start | bytes 4460548
  89.5 1.3 %copy-start.5 = (f32[8,8,32,128]{3,1,2,0:T(8,128)S(1)}, f32[8,8,32,128]{3,1,2,0:T(8,128)}, u32[]{:S(2)}) copy-start(f32[8,8,32,128]{3,1,2,0:T(8,128)} %slice.521) | copy-start | bytes 3145732
  90.6 1.3 %copy-start.6 = (f32[8,32,128]{2,0,1:T(8,128)S(1)}, f32[8,32,128]{2,0,1:T(8,128)}, u32[]{:S(2)}) copy-start(f32[8,32,128]{2,0,1:T(8,128)} %slice_bitcast_fusion.6) | copy-start | bytes 393220
where the time goes:
time: 94 us; the launch traced here: 93.4 us
  local copies, waits for them, and re-layouts  33.4 us (36%)
  other arithmetic  21.4 us (23%)
  starting transfers between devices  20.5 us (22%)
  waiting for transfers between devices  16.9 us (18%)
  between operations  1.03 us (1%)
    ppermute x4, waiting for transfers between devices, padded_2(): lax.ppermute(head, axis, [((i + 1) % count, i) for i in range(ends)])  16.9 us
    ppermute x4, starting transfers between devices, padded_2(): lax.ppermute(tail, axis, [(i, (i + 1) % count) for i in range(ends)])  15.7 us
    div x4, other arithmetic, upwind(): face_speed * jnp.where(face_speed >= 0.0, 5.0 * centre + 2.0 * forward -...  9.5 us
    slice x5, local copies, waits for them, and re-layouts, padded_2(): lax.slice_in_dim(cells, cells.shape[dim] - width, cells.shape[dim], axis=...  7.78 us
    ppermute x2, local copies, waits for them, and re-layouts, padded_2(): lax.ppermute(head, axis, [((i + 1) % count, i) for i in range(ends)])  5.64 us
    ppermute x4, starting transfers between devices, padded_2(): lax.ppermute(head, axis, [((i + 1) % count, i) for i in range(ends)])  3.85 us
    unnamed x16, local copies, waits for them, and re-layouts  3.56 us
    ppermute x2, local copies, waits for them, and re-layouts, padded_2(): lax.ppermute(tail, axis, [(i, (i + 1) % count) for i in range(ends)])  3.27 us
  transfers between devices with their start and end apart: 10, of which 4 were waited for; matrix products, arithmetic and copies ran while one was open for 11% of the time, Pallas kernels for 0%

commit v1 on v0

v1 whole, which is shorter than its diff:
```python
import math

import jax
import jax.numpy as jnp
from jax import lax
from jax.experimental import pallas as pl
from jax.experimental.pallas import tpu as pltpu
from jax.sharding import PartitionSpec as P

SUBSTEPS = 2
COUR = 0.25
GRAV = 1.0
FCOR = 1.0

HALO = 2 * SUBSTEPS
STRIP = 4 * HALO


def _lroll(x, k):
    n = x.shape[-1]
    return pltpu.roll(x, k % n, x.ndim - 1)


def _rroll(x, k):
    n = x.shape[-2]
    return pltpu.roll(x, k % n, x.ndim - 2)


def _upwind(speed, pos, behind, centre, forward, beyond):
    return (
        speed
        * jnp.where(pos, 5.0 * centre + 2.0 * forward - behind, 5.0 * forward + 2.0 * centre - beyond)
        / 6.0
    )


def _substep(load, store, nf, pot, fcos, acos, cor):
    u = load(1)
    v = load(2)
    fs = COUR * 0.5 * (u + _lroll(u, -1))
    ms = COUR * 0.5 * (v + _rroll(v, -1)) * fcos
    fpos = fs >= 0.0
    mpos = ms >= 0.0
    for f in range(nf):
        x = u if f == 1 else (v if f == 2 else load(f))
        zf = _upwind(fs, fpos, _lroll(x, 1), x, _lroll(x, -1), _lroll(x, -2))
        mf = _upwind(ms, mpos, _rroll(x, 1), x, _rroll(x, -1), _rroll(x, -2))
        new = x - (zf - _lroll(zf, 1)) - (mf - _rroll(mf, 1)) / acos
        if f == 1:
            new = new - COUR * 0.5 * (_lroll(pot, -1) - _lroll(pot, 1)) + COUR * cor * v
        elif f == 2:
            new = new - COUR * 0.5 * (_rroll(pot, -1) - _rroll(pot, 1)) - COUR * cor * u
        store(f, new)


def _suffix_packed(h, group, ngroups):
    s = h
    k = 1
    while k < ngroups:
        s = s + jnp.where(group + k < ngroups, _lroll(s, -STRIP * k), 0.0)
        k *= 2
    return GRAV * s


def _fix_edges(x, g, lev, lane):
    w = x.shape[-1]
    base = STRIP * lev
    lo = _lroll(g, -(base + HALO))
    hi = _lroll(g, (w - 2) - (base + 2 * HALO + 2))
    return jnp.where(lane < 2, lo, jnp.where(lane >= w - 2, hi, x))


def _kernel(s_ref, g_ref, fcos_ref, acos_ref, cor_ref, thk_ref, wind_ref, trc_ref, s1_ref, g1_ref, p_ref):
    nf, nlev, rows, w = s_ref.shape
    fcos = fcos_ref[...]
    acos = acos_ref[...]
    cor = cor_ref[...]
    lane = lax.broadcasted_iota(jnp.int32, (rows, w), 1)
    group = lane // STRIP
    kk = lane % STRIP

    def set_g1(f, x):
        g1_ref[f] = x

    def potential(src):
        acc = None
        for lev in reversed(range(nlev)):
            acc = src[0, lev] if acc is None else acc + src[0, lev]
            p_ref[lev] = GRAV * acc

    _substep(lambda f: g_ref[f], set_g1, nf, _suffix_packed(g_ref[0], group, nlev), fcos, acos, cor)
    potential(s_ref)
    for lev in range(nlev):

        def store1(f, x, lev=lev):
            s1_ref[f, lev] = _fix_edges(x, g1_ref[f], lev, lane)

        _substep(lambda f, lev=lev: s_ref[f, lev], store1, nf, p_ref[lev], fcos, acos, cor)
    lo_mask = (kk >= HALO) & (kk < 2 * HALO)
    hi_mask = (kk >= 2 * HALO) & (kk < 3 * HALO)
    for f in range(nf):
        g = g1_ref[f]
        for lev in range(nlev):
            m = s1_ref[f, lev]
            base = STRIP * lev
            g = jnp.where((group == lev) & lo_mask, _lroll(m, base + HALO), g)
            g = jnp.where((group == lev) & hi_mask, _lroll(m, base + 2 * HALO - (w - HALO)), g)
        g1_ref[f] = g
    _substep(lambda f: g1_ref[f], set_g1, nf, _suffix_packed(g1_ref[0], group, nlev), fcos, acos, cor)
    potential(s1_ref)
    inner = rows - 2 * HALO
    for lev in range(nlev):

        def store2(f, x, lev=lev):
            x = _fix_edges(x, g1_ref[f], lev, lane)
            x = _rroll(x, -HALO)[:inner]
            if f == 0:
                thk_ref[lev] = x
            elif f < 3:
                wind_ref[f - 1, lev] = x
            else:
                trc_ref[f - 3, lev] = x

        _substep(lambda f, lev=lev: s1_ref[f, lev], store2, nf, p_ref[lev], fcos, acos, cor)


def _shift_pairs(n, d, closed):
    return [(i, (i + d) % n) for i in range(n) if closed or 0 <= i + d < n]


def shards(thickness, winds, tracer_mass):
    fields = jnp.concatenate([thickness[None], winds, tracer_mass], 0)
    nf, nlev, rows, w = fields.shape
    nlat = lax.axis_size("lat")
    nlon = lax.axis_size("lon")
    band = lax.axis_index("lat")
    spacing = math.pi / (rows * nlat)

    top = fields[:, :, rows - HALO :]
    bottom = fields[:, :, :HALO]
    from_south = lax.ppermute(top, "lat", _shift_pairs(nlat, 1, False))
    from_north = lax.ppermute(bottom, "lat", _shift_pairs(nlat, -1, False))
    half = nlon // 2
    pole_pairs = []
    for b in (0, nlat - 1):
        for s in range(nlon):
            pole_pairs.append((b * nlon + s, b * nlon + (s + half) % nlon))
    pole_out = jnp.where(band == 0, bottom, top)
    pole_in = lax.ppermute(pole_out, ("lat", "lon"), pole_pairs)
    sign = jnp.where(jnp.arange(nf) == 2, -1.0, 1.0).astype(jnp.float32)[:, None, None, None]
    mirrored = jnp.flip(pole_in, 2) * sign
    south = jnp.where(band == 0, mirrored, from_south)
    north = jnp.where(band == nlat - 1, mirrored, from_north)
    padded = jnp.concatenate([south, fields, north], 2)

    west_cols = padded[..., :HALO]
    east_cols = padded[..., w - HALO :]
    from_west = lax.ppermute(east_cols, "lon", _shift_pairs(nlon, 1, True))
    from_east = lax.ppermute(west_cols, "lon", _shift_pairs(nlon, -1, True))
    strip = jnp.concatenate([from_west, west_cols, east_cols, from_east], -1)
    tall = rows + 2 * HALO
    packed = jnp.transpose(strip, (0, 2, 1, 3)).reshape(nf, tall, nlev * STRIP)

    row_index = (jnp.arange(tall) + (band * rows - HALO)).astype(jnp.float32)
    center_lat = (row_index + 0.5) * spacing - 0.5 * math.pi
    face_lat = (row_index + 1.0) * spacing - 0.5 * math.pi
    center_cos = jnp.cos(center_lat)
    fcos = jnp.broadcast_to(jnp.abs(jnp.cos(face_lat))[:, None], (tall, w))
    acos = jnp.broadcast_to(jnp.abs(center_cos)[:, None], (tall, w))
    cor = jnp.broadcast_to(
        (FCOR * jnp.sin(center_lat) * jnp.where(center_cos >= 0.0, 1.0, -1.0))[:, None], (tall, w)
    )

    vmem = pl.BlockSpec(memory_space=pltpu.VMEM)
    return pl.pallas_call(
        _kernel,
        out_shape=(
            jax.ShapeDtypeStruct(thickness.shape, jnp.float32),
            jax.ShapeDtypeStruct(winds.shape, jnp.float32),
            jax.ShapeDtypeStruct(tracer_mass.shape, jnp.float32),
        ),
        in_specs=[vmem] * 5,
        out_specs=(vmem, vmem, vmem),
        scratch_shapes=[
            pltpu.VMEM(padded.shape, jnp.float32),
            pltpu.VMEM(packed.shape, jnp.float32),
            pltpu.VMEM((nlev, tall, w), jnp.float32),
        ],
    )(padded, packed, fcos, acos, cor)


def solution(mesh):
    return jax.shard_map(
        shards,
        mesh=mesh,
        in_specs=(P(None, "lat", "lon"), P(None, None, "lat", "lon"), P(None, None, "lat", "lon")),
        out_specs=(P(None, "lat", "lon"), P(None, None, "lat", "lon"), P(None, None, "lat", "lon")),
        check_vma=False,
    )
```

time: 94 us -> 63 us (0.67)
  the two profiles are of different devices: /device:TPU:103 before, /device:TPU:6 now
where the time goes in v1:
time: 63 us; the launch traced here: 62.7 us
  Pallas kernels  23.1 us (37%)
  waiting for transfers between devices  13.4 us (21%)
  starting transfers between devices  11.9 us (19%)
  local copies, waits for them, and re-layouts  11.5 us (18%)
  other arithmetic  2.03 us (3%)
  between operations  0.8 us (1%)
    pallas_call x1, Pallas kernels, shards(): pl.pallas_call(_kernel, out_shape=(jax.ShapeDtypeStruct(thickness.shape,...  23.1 us
    ppermute x1, waiting for transfers between devices, shards(): from_north = lax.ppermute(bottom, 'lat', _shift_pairs(nlat, -1, False))  7.73 us
    slice x3, local copies, waits for them, and re-layouts, shards(): east_cols = padded[..., w - HALO:]  6.85 us
    ppermute x1, starting transfers between devices, shards(): from_south = lax.ppermute(top, 'lat', _shift_pairs(nlat, 1, False))  5.02 us
    ppermute x1, starting transfers between devices, shards(): from_east = lax.ppermute(west_cols, 'lon', _shift_pairs(nlon, -1, True))  4.29 us
    ppermute x1, waiting for transfers between devices, shards(): from_west = lax.ppermute(east_cols, 'lon', _shift_pairs(nlon, 1, True))  3.97 us
    ppermute x1, starting transfers between devices, shards(): from_north = lax.ppermute(bottom, 'lat', _shift_pairs(nlat, -1, False))  1.92 us
    ppermute x1, waiting for transfers between devices, shards(): from_south = lax.ppermute(top, 'lat', _shift_pairs(nlat, 1, False))  1.56 us
  transfers between devices with their start and end apart: 5, of which 4 were waited for; matrix products, arithmetic and copies ran while one was open for 5% of the time, Pallas kernels for 0%

profile of v1, /device:TPU:6, one launch (start us, length us, event | category | flops | bytes accessed | tf_op | source)
XLA Modules:
  0.0 62.7 jit_solution(11683571130551124938)
XLA Ops:
  0.6 0.0 copy-start.2
  0.7 1.3 %broadcast_select_fusion = (f32[11,8,4,128]{3,2,1,0:T(4,128)S(1)}, f32[11,8,4,128]{3,2,1,0:T(4,128)S(1)}, f32[11,8,4,128]{3,2,1,0:T(4,128)S(1)}) fusion(pred[]{:T(512)S(6)} %eq.14, f32[8,8,32,128]{3,2,1,0:T(8,128)} %param.5, f32[2,8,32,128]{3,2,1,0:T(8,128)} %param.4, f32[1,8,32,128]{3,2,1,0:T(8,128)} %bitcast.5), kind=kLoop, calls=%fused_computation.7 | loop fusion | flops 225280 | bytes 1982465 | tf_op jit(solution)/shard_map/jit(_where)/select_n | solution.py:148
  1.9 0.7 %collective-permute-start = (f32[11,8,4,128]{3,2,1,0:T(4,128)S(1)}, f32[11,8,4,128]{3,2,1,0:T(4,128)S(1)}, u32[]{:S(2)}, u32[]{:S(2)}) collective-permute-start(f32[11,8,4,128]{3,2,1,0:T(4,128)S(1)} %get-tuple-element.3), channel_id=1, source_target_pairs={{0,16},{1,17},{2,18},{3,19},{4,20},{5,21},{6,22},{7,23},{8,24},{9,... | collective-permute-start | bytes 540680 | tf_op jit(solution)/shard_map/ppermute | solution.py:149
  2.6 5.0 %collective-permute-start.1 = (f32[11,8,4,128]{3,2,1,0:T(4,128)S(1)}, f32[11,8,4,128]{3,2,1,0:T(4,128)S(1)}, u32[]{:S(2)}, u32[]{:S(2)}) collective-permute-start(f32[11,8,4,128]{3,2,1,0:T(4,128)S(1)} %get-tuple-element.4), channel_id=1, source_target_pairs={{0,32},{32,64},{64,96},{96,128},{128,160},{160,192},{192,224},{1,3... | collective-permute-start | bytes 540680 | tf_op jit(solution)/shard_map/ppermute | solution.py:141
  7.6 1.9 %collective-permute-start.2 = (f32[11,8,4,128]{3,2,1,0:T(4,128)S(1)}, f32[11,8,4,128]{3,2,1,0:T(4,128)S(1)}, u32[]{:S(2)}, u32[]{:S(2)}) collective-permute-start(f32[11,8,4,128]{3,2,1,0:T(4,128)S(1)} %get-tuple-element.5), channel_id=1, source_target_pairs={{32,0},{64,32},{96,64},{128,96},{160,128},{192,160},{224,192},{33,... | collective-permute-start | bytes 540680 | tf_op jit(solution)/shard_map/ppermute | solution.py:142
  9.6 0.1 fusion
  9.6 0.0 collective-permute-done
  9.7 0.2 rev.4
  9.9 1.6 %collective-permute-done.1 = f32[11,8,4,128]{3,2,1,0:T(4,128)S(1)} collective-permute-done((f32[11,8,4,128]{3,2,1,0:T(4,128)S(1)}, f32[11,8,4,128]{3,2,1,0:T(4,128)S(1)}, u32[]{:S(2)}, u32[]{:S(2)}) %collective-permute-start.1) | collective-permute-done | bytes 180256 | tf_op jit(solution)/shard_map/ppermute | solution.py:141
  11.4 7.7 %collective-permute-done.2 = f32[11,8,4,128]{3,2,1,0:T(4,128)S(1)} collective-permute-done((f32[11,8,4,128]{3,2,1,0:T(4,128)S(1)}, f32[11,8,4,128]{3,2,1,0:T(4,128)S(1)}, u32[]{:S(2)}, u32[]{:S(2)}) %collective-permute-start.2) | collective-permute-done | bytes 180256 | tf_op jit(solution)/shard_map/ppermute | solution.py:142
  19.2 0.1 multiply_select_fusion.1
  19.3 0.0 copy-done.2
  19.3 0.0 copy-done.3
  19.3 0.0 copy-done.4
  19.3 0.3 pad_maximum_fusion.s_ref
  19.6 0.0 copy-start
  19.7 2.4 %fusion.3 = (f32[11,8,40,4]{3,2,1,0:T(8,128)}, f32[11,8,40,4]{3,2,1,0:T(8,128)}) fusion(f32[11,8,40,128]{3,2,1,0:T(8,128)S(1)} %pad_maximum_fusion.s_ref), kind=kLoop, calls=%fused_computation.16 | loop fusion | bytes 225280 | tf_op jit(solution)/shard_map/slice | solution.py:157
  22.1 2.3 %copy.9 = f32[11,8,40,4]{2,1,3,0:T(8,128)S(1)} copy(f32[11,8,40,4]{3,2,1,0:T(8,128)} %get-tuple-element.6) | data formatting | bytes 112640 | tf_op jit(solution)/shard_map/slice | solution.py:157
  24.4 0.0 copy-done.1
  24.4 0.7 %copy.10 = f32[11,8,40,4]{2,1,3,0:T(8,128)S(1)} copy(f32[11,8,40,4]{3,2,1,0:T(8,128)S(1)} %copy-done.1) | data formatting | bytes 112640 | tf_op jit(solution)/shard_map/slice | solution.py:156
  25.1 4.3 %collective-permute-start.4 = (f32[11,8,40,4]{2,1,3,0:T(8,128)S(1)}, f32[11,8,40,4]{2,1,3,0:T(8,128)S(1)}, u32[]{:S(2)}, u32[]{:S(2)}) collective-permute-start(f32[11,8,40,4]{2,1,3,0:T(8,128)S(1)} %copy.10), channel_id=1, source_target_pairs={{0,31},{1,0},{2,1},{3,2},{4,3},{5,4},{6,5},{7,6},{8,7},{9,8},{10,9... | collective-permute-start | bytes 168968 | tf_op jit(solution)/shard_map/ppermute | solution.py:159
  29.4 0.0 collective-permute-start.3
  29.4 2.1 %copy.13 = f32[11,8,40,4]{2,3,1,0:T(4,128)S(1)} copy(f32[11,8,40,4]{3,2,1,0:T(8,128)} %get-tuple-element.6) | data formatting | bytes 112640 | tf_op jit(solution)/shard_map/slice | solution.py:157
  31.5 0.7 %copy.12 = f32[11,8,40,4]{2,3,1,0:T(4,128)S(1)} copy(f32[11,8,40,4]{3,2,1,0:T(8,128)S(1)} %copy-done.1) | data formatting | bytes 112640 | tf_op jit(solution)/shard_map/slice | solution.py:156
  32.2 0.1 collective-permute-done.4
  32.4 4.0 %collective-permute-done.3 = f32[11,8,40,4]{2,1,3,0:T(8,128)S(1)} collective-permute-done((f32[11,8,40,4]{2,1,3,0:T(8,128)S(1)}, f32[11,8,40,4]{2,1,3,0:T(8,128)S(1)}, u32[]{:S(2)}, u32[]{:S(2)}) %collective-permute-start.3) | collective-permute-done | bytes 56352 | tf_op jit(solution)/shard_map/ppermute | solution.py:158
  36.4 0.2 pad_maximum_fusion.1
  36.7 0.9 %copy.15.g_ref = f32[11,40,128]{2,1,0:T(8,128)} copy(f32[11,40,128]{1,2,0:T(8,128)S(1)} %bitcast.4) | data formatting | bytes 450560 | tf_op jit(solution)/shard_map/reshape | solution.py:162
  37.6 0.7 %broadcast_in_dim.42.cor_ref = f32[40,128]{1,0:T(8,128)} broadcast(f32[40]{0:T(128)S(1)} %get-tuple-element.10), dimensions={0} | broadcast | bytes 20640 | tf_op jit(solution)/shard_map/broadcast_in_dim | solution.py:170
  38.3 0.7 %broadcast_in_dim.40.acos_ref = f32[40,128]{1,0:T(8,128)} broadcast(f32[40]{0:T(128)S(1)} %fusion.2), dimensions={0} | broadcast | bytes 20640 | tf_op jit(solution)/shard_map/broadcast_in_dim | solution.py:169
  39.0 0.7 %broadcast_in_dim.39.fcos_ref = f32[40,128]{1,0:T(8,128)} broadcast(f32[40]{0:T(128)S(1)} %get-tuple-element.11), dimensions={0} | broadcast | bytes 20640 | tf_op jit(solution)/shard_map/broadcast_in_dim | solution.py:168
  39.6 23.1 %shard_map.58 = (f32[8,32,128]{2,1,0:T(8,128)}, f32[2,8,32,128]{3,2,1,0:T(8,128)}, f32[8,8,32,128]{3,2,1,0:T(8,128)}) custom-call(f32[11,8,40,128]{3,2,1,0:T(8,128)} %copy-done, f32[11,40,128]{2,1,0:T(8,128)} %copy.15.g_ref, f32[40,128]{1,0:T(8,128)} %broadcast_in_dim.39.fcos_ref, f32[40,128]{1,0:T(8,128)} %broadcast_in_dim.40.acos_ref, ...), custom_call_target="tpu_custom_call" | custom-call | tf_op jit(solution)/shard_map/pallas_call | solution.py:175
  (8 shorter events, 0.2 us)
Async XLA Ops:
  0.6 18.7 %copy-start.2 = (f32[8,8,32,128]{3,2,1,0:T(8,128)S(1)}, f32[8,8,32,128]{3,2,1,0:T(8,128)}, u32[]{:S(2)}) copy-start(f32[8,8,32,128]{3,2,1,0:T(8,128)} %param.5) | copy-start | bytes 3145732
  0.6 18.7 %copy-start.3 = (f32[2,8,32,128]{3,2,1,0:T(8,128)S(1)}, f32[2,8,32,128]{3,2,1,0:T(8,128)}, u32[]{:S(2)}) copy-start(f32[2,8,32,128]{3,2,1,0:T(8,128)} %param.4) | copy-start | bytes 786436
  0.7 18.7 %copy-start.4 = (f32[8,32,128]{2,1,0:T(8,128)S(1)}, f32[8,32,128]{2,1,0:T(8,128)}, u32[]{:S(2)}) copy-start(f32[8,32,128]{2,1,0:T(8,128)} %param.3) | copy-start | bytes 393220
  1.9 7.7 %collective-permute-start = (f32[11,8,4,128]{3,2,1,0:T(4,128)S(1)}, f32[11,8,4,128]{3,2,1,0:T(4,128)S(1)}, u32[]{:S(2)}, u32[]{:S(2)}) collective-permute-start(f32[11,8,4,128]{3,2,1,0:T(4,128)S(1)} %get-tuple-element.3), channel_id=1, source_target_pairs={{0,16},{1,17},{2,18},{3,19},{4,20},{5,21},{6,22},{7,23},{8,24},{9,... | collective-permute-start | bytes 540680 | tf_op jit(solution)/shard_map/ppermute | solution.py:149
  2.6 8.8 %collective-permute-start.1 = (f32[11,8,4,128]{3,2,1,0:T(4,128)S(1)}, f32[11,8,4,128]{3,2,1,0:T(4,128)S(1)}, u32[]{:S(2)}, u32[]{:S(2)}) collective-permute-start(f32[11,8,4,128]{3,2,1,0:T(4,128)S(1)} %get-tuple-element.4), channel_id=1, source_target_pairs={{0,32},{32,64},{64,96},{96,128},{128,160},{160,192},{192,224},{1,3... | collective-permute-start | bytes 540680 | tf_op jit(solution)/shard_map/ppermute | solution.py:141
  7.6 11.5 %collective-permute-start.2 = (f32[11,8,4,128]{3,2,1,0:T(4,128)S(1)}, f32[11,8,4,128]{3,2,1,0:T(4,128)S(1)}, u32[]{:S(2)}, u32[]{:S(2)}) collective-permute-start(f32[11,8,4,128]{3,2,1,0:T(4,128)S(1)} %get-tuple-element.5), channel_id=1, source_target_pairs={{32,0},{64,32},{96,64},{128,96},{160,128},{192,160},{224,192},{33,... | collective-permute-start | bytes 540680 | tf_op jit(solution)/shard_map/ppermute | solution.py:142
  19.6 2.4 %copy-start = (f32[11,8,40,128]{3,2,1,0:T(8,128)}, f32[11,8,40,128]{3,2,1,0:T(8,128)S(1)}, u32[]{:S(2)}) copy-start(f32[11,8,40,128]{3,2,1,0:T(8,128)S(1)} %pad_maximum_fusion.s_ref) | copy-start | bytes 5406724
  22.1 2.3 %copy-start.1 = (f32[11,8,40,4]{3,2,1,0:T(8,128)S(1)}, f32[11,8,40,4]{3,2,1,0:T(8,128)}, u32[]{:S(2)}) copy-start(f32[11,8,40,4]{3,2,1,0:T(8,128)} %get-tuple-element.7) | copy-start | bytes 168964
  25.1 7.3 %collective-permute-start.4 = (f32[11,8,40,4]{2,1,3,0:T(8,128)S(1)}, f32[11,8,40,4]{2,1,3,0:T(8,128)S(1)}, u32[]{:S(2)}, u32[]{:S(2)}) collective-permute-start(f32[11,8,40,4]{2,1,3,0:T(8,128)S(1)} %copy.10), channel_id=1, source_target_pairs={{0,31},{1,0},{2,1},{3,2},{4,3},{5,4},{6,5},{7,6},{8,7},{9,8},{10,9... | collective-permute-start | bytes 168968 | tf_op jit(solution)/shard_map/ppermute | solution.py:159
  29.4 7.0 %collective-permute-start.3 = (f32[11,8,40,4]{2,1,3,0:T(8,128)S(1)}, f32[11,8,40,4]{2,1,3,0:T(8,128)S(1)}, u32[]{:S(2)}, u32[]{:S(2)}) collective-permute-start(f32[11,8,40,4]{2,1,3,0:T(8,128)S(1)} %copy.9), channel_id=1, source_target_pairs={{0,1},{1,2},{2,3},{3,4},{4,5},{5,6},{6,7},{7,8},{8,9},{9,10},{10,1... | collective-permute-start | bytes 168968 | tf_op jit(solution)/shard_map/ppermute | solution.py:158

commit v2 on v1

v2 whole, which is shorter than its diff:
```python
import math

import jax
import jax.numpy as jnp
from jax import lax
from jax.experimental import pallas as pl
from jax.experimental.pallas import tpu as pltpu
from jax.sharding import PartitionSpec as P

SUBSTEPS = 2
COUR = 0.25
GRAV = 1.0
FCOR = 1.0

HALO = 2 * SUBSTEPS
STRIP = 4 * HALO


def _lroll(x, k):
    n = x.shape[-1]
    return pltpu.roll(x, k % n, x.ndim - 1)


def _rroll(x, k):
    n = x.shape[-2]
    return pltpu.roll(x, k % n, x.ndim - 2)


def _upwind(speed, pos, behind, centre, forward, beyond):
    return speed * jnp.where(pos, 5.0 * centre + 2.0 * forward - behind, 5.0 * forward + 2.0 * centre - beyond)


def _substep(load, store, nf, pot, rv):
    fcos, inv_acos, cor = rv
    u = load(1)
    v = load(2)
    fs = (COUR * 0.5 / 6.0) * (u + _lroll(u, -1))
    ms = (COUR * 0.5 / 6.0) * (v + _rroll(v, -1)) * fcos
    fpos = fs >= 0.0
    mpos = ms >= 0.0
    for f in range(nf):
        x = u if f == 1 else (v if f == 2 else load(f))
        zf = _upwind(fs, fpos, _lroll(x, 1), x, _lroll(x, -1), _lroll(x, -2))
        mf = _upwind(ms, mpos, _rroll(x, 1), x, _rroll(x, -1), _rroll(x, -2))
        new = x - (zf - _lroll(zf, 1)) - (mf - _rroll(mf, 1)) * inv_acos
        if f == 1:
            new = new - COUR * 0.5 * (_lroll(pot, -1) - _lroll(pot, 1)) + cor * v
        elif f == 2:
            new = new - COUR * 0.5 * (_rroll(pot, -1) - _rroll(pot, 1)) - cor * u
        store(f, new)


def _suffix_packed(h, group, ngroups):
    s = h
    k = 1
    while k < ngroups:
        s = s + jnp.where(group + k < ngroups, _lroll(s, -STRIP * k), 0.0)
        k *= 2
    return GRAV * s


def _fix_edges(x, g, lev, lane):
    w = x.shape[-1]
    base = STRIP * lev
    lo = _lroll(g, -(base + HALO))
    hi = _lroll(g, (w - 2) - (base + 2 * HALO + 2))
    return jnp.where(lane < 2, lo, jnp.where(lane >= w - 2, hi, x))


def _lanes(rows, w):
    lane = lax.broadcasted_iota(jnp.int32, (rows, w), 1)
    return lane, lane // STRIP, lane % STRIP


def _pack_edges(get, nlev, rows, w, init):
    lane, group, kk = _lanes(rows, w)
    lo_mask = (kk >= HALO) & (kk < 2 * HALO)
    hi_mask = (kk >= 2 * HALO) & (kk < 3 * HALO)
    g = init
    for lev in range(nlev):
        m = get(lev)
        base = STRIP * lev
        g = jnp.where((group == lev) & lo_mask, _lroll(m, base + HALO), g)
        g = jnp.where((group == lev) & hi_mask, _lroll(m, base + 2 * HALO - (w - HALO)), g)
    return g


def _potential(src, p_ref, nlev):
    acc = None
    for lev in reversed(range(nlev)):
        acc = src[0, lev] if acc is None else acc + src[0, lev]
        p_ref[lev] = GRAV * acc


def _edge_kernel(s_ref, e_ref):
    nf, nlev, rows, w = s_ref.shape
    for f in range(nf):
        e_ref[f] = _pack_edges(lambda lev: s_ref[f, lev], nlev, rows, w, jnp.zeros((rows, w), jnp.float32))


def _main1_kernel(s_ref, rv_ref, o_ref, p_ref):
    nf, nlev, rows, w = s_ref.shape
    rv = (rv_ref[0], rv_ref[1], rv_ref[2])
    _potential(s_ref, p_ref, nlev)
    for lev in range(nlev):

        def store(f, x, lev=lev):
            o_ref[f, lev] = x

        _substep(lambda f, lev=lev: s_ref[f, lev], store, nf, p_ref[lev], rv)


def _final_kernel(s1_ref, e_ref, ew_ref, ee_ref, rv_ref, thk_ref, wind_ref, trc_ref, s_ref, g_ref, p_ref):
    nf, nlev, rows, w = s1_ref.shape
    rv = (rv_ref[0], rv_ref[1], rv_ref[2])
    lane, group, kk = _lanes(rows, w)

    def set_g(f, x):
        g_ref[f] = x

    for f in range(nf):
        g_ref[f] = jnp.where(
            kk < HALO, _lroll(ew_ref[f], -2 * HALO), jnp.where(kk >= 3 * HALO, _lroll(ee_ref[f], 2 * HALO), e_ref[f])
        )
    _substep(lambda f: g_ref[f], set_g, nf, _suffix_packed(g_ref[0], group, nlev), rv)
    for f in range(nf):
        g = g_ref[f]
        for lev in range(nlev):
            s_ref[f, lev] = _fix_edges(s1_ref[f, lev], g, lev, lane)
    for f in range(nf):
        g_ref[f] = _pack_edges(lambda lev: s_ref[f, lev], nlev, rows, w, g_ref[f])
    _substep(lambda f: g_ref[f], set_g, nf, _suffix_packed(g_ref[0], group, nlev), rv)
    _potential(s_ref, p_ref, nlev)
    inner = rows - 2 * HALO
    for lev in range(nlev):

        def store2(f, x, lev=lev):
            x = _fix_edges(x, g_ref[f], lev, lane)
            x = _rroll(x, -HALO)[:inner]
            if f == 0:
                thk_ref[lev] = x
            elif f < 3:
                wind_ref[f - 1, lev] = x
            else:
                trc_ref[f - 3, lev] = x

        _substep(lambda f, lev=lev: s_ref[f, lev], store2, nf, p_ref[lev], rv)


def _shift_pairs(n, d, closed):
    return [(i, (i + d) % n) for i in range(n) if closed or 0 <= i + d < n]


def _vmem_call(kernel, out_shape, n_in, scratch, flops, nbytes):
    vmem = pl.BlockSpec(memory_space=pltpu.VMEM)
    return pl.pallas_call(
        kernel,
        out_shape=out_shape,
        in_specs=[vmem] * n_in,
        out_specs=tuple(vmem for _ in out_shape) if isinstance(out_shape, tuple) else vmem,
        scratch_shapes=scratch,
        cost_estimate=pl.CostEstimate(flops=flops, bytes_accessed=nbytes, transcendentals=0),
    )


def shards(thickness, winds, tracer_mass):
    fields = jnp.concatenate([thickness[None], winds, tracer_mass], 0)
    nf, nlev, rows, w = fields.shape
    nlat = lax.axis_size("lat")
    nlon = lax.axis_size("lon")
    band = lax.axis_index("lat")
    spacing = math.pi / (rows * nlat)
    tall = rows + 2 * HALO

    row_index = (jnp.arange(tall) + (band * rows - HALO)).astype(jnp.float32)
    center_lat = (row_index + 0.5) * spacing - 0.5 * math.pi
    face_lat = (row_index + 1.0) * spacing - 0.5 * math.pi
    center_cos = jnp.cos(center_lat)
    rowvec = jnp.stack(
        [
            jnp.abs(jnp.cos(face_lat)),
            1.0 / jnp.abs(center_cos),
            COUR * FCOR * jnp.sin(center_lat) * jnp.where(center_cos >= 0.0, 1.0, -1.0),
        ]
    )
    rowvec = jnp.broadcast_to(rowvec[:, :, None], (3, tall, w))

    top = fields[:, :, rows - HALO :]
    bottom = fields[:, :, :HALO]
    from_south = lax.ppermute(top, "lat", _shift_pairs(nlat, 1, False))
    from_north = lax.ppermute(bottom, "lat", _shift_pairs(nlat, -1, False))
    half = nlon // 2
    pole_pairs = []
    for b in (0, nlat - 1):
        for s in range(nlon):
            pole_pairs.append((b * nlon + s, b * nlon + (s + half) % nlon))
    pole_out = jnp.where(band == 0, bottom, top)
    pole_in = lax.ppermute(pole_out, ("lat", "lon"), pole_pairs)
    sign = jnp.where(jnp.arange(nf) == 2, -1.0, 1.0).astype(jnp.float32)[:, None, None, None]
    mirrored = jnp.flip(pole_in, 2) * sign
    south = jnp.where(band == 0, mirrored, from_south)
    north = jnp.where(band == nlat - 1, mirrored, from_north)
    padded = jnp.concatenate([south, fields, north], 2)

    slab = nf * tall * w * 4
    edges = _vmem_call(_edge_kernel, jax.ShapeDtypeStruct((nf, tall, w), jnp.float32), 1, [], 0, slab * (nlev + 1))(
        padded
    )
    from_west = lax.ppermute(edges, "lon", _shift_pairs(nlon, 1, True))
    from_east = lax.ppermute(edges, "lon", _shift_pairs(nlon, -1, True))

    step_flops = 60 * nf * nlev * tall * w
    main1 = _vmem_call(
        _main1_kernel,
        jax.ShapeDtypeStruct(padded.shape, jnp.float32),
        2,
        [pltpu.VMEM((nlev, tall, w), jnp.float32)],
        step_flops,
        2 * slab * nlev,
    )(padded, rowvec)

    return _vmem_call(
        _final_kernel,
        (
            jax.ShapeDtypeStruct(thickness.shape, jnp.float32),
            jax.ShapeDtypeStruct(winds.shape, jnp.float32),
            jax.ShapeDtypeStruct(tracer_mass.shape, jnp.float32),
        ),
        5,
        [
            pltpu.VMEM(padded.shape, jnp.float32),
            pltpu.VMEM(edges.shape, jnp.float32),
            pltpu.VMEM((nlev, tall, w), jnp.float32),
        ],
        step_flops + 3 * step_flops // nlev,
        2 * slab * nlev,
    )(main1, edges, from_west, from_east, rowvec)


def solution(mesh):
    return jax.shard_map(
        shards,
        mesh=mesh,
        in_specs=(P(None, "lat", "lon"), P(None, None, "lat", "lon"), P(None, None, "lat", "lon")),
        out_specs=(P(None, "lat", "lon"), P(None, None, "lat", "lon"), P(None, None, "lat", "lon")),
        check_vma=False,
    )
```

time: 63 us -> 56.1 us (0.89)
  local copies, waits for them, and re-layouts: 11.5 us -> 2.33 us
  Pallas kernels: 23.1 us -> 28.6 us
  waiting for transfers between devices: 13.4 us -> 9.3 us
  other arithmetic: 2.03 us -> 3.04 us
    slice x5 -> x0, local copies, waits for them, and re-layouts: 8.2 us -> none  [the longest x3 6.85 us: shards(): east_cols = padded[..., w - HALO:]]
    pallas_call x1 -> x3, Pallas kernels: 23.1 us -> 28.6 us  [the longest x1 15.3 us: shards(): _vmem_call(_final_kernel, (jax.ShapeDtypeStruct(thickness.shape, jnp.floa...]
    ppermute x2, waiting for transfers between devices: 4.11 us -> 0.01 us  [the longest x1 0.01 us: shards(): from_east = lax.ppermute(edges, 'lon', _shift_pairs(nlon, -1, True))]
    unnamed x10, local copies, waits for them, and re-layouts: 0.02 us -> 1.4 us
    broadcast_in_dim x3 -> x1, local copies, waits for them, and re-layouts: 2.02 us -> 0.72 us  [shards(): rowvec = jnp.broadcast_to(rowvec[:, :, None], (3, tall, w))]
    concatenate x1, other arithmetic: 0.3 us -> 1.52 us  [shards(): padded = jnp.concatenate([south, fields, north], 2)]
    reshape x1 -> x0, local copies, waits for them, and re-layouts: 0.94 us -> none  [shards(): packed = jnp.transpose(strip, (0, 2, 1, 3)).reshape(nf, tall, nlev * STRIP)]
  transfers between devices with their start and end apart: 5 -> 5, of which waited for: 4 -> 2; matrix products, arithmetic and copies ran while one was open for 5% -> 2% of each run, Pallas kernels for 0% -> 18%
where the time goes in v2:
time: 56.1 us; the launch traced here: 55.9 us
  Pallas kernels  28.6 us (51%)
  starting transfers between devices  11.8 us (21%)
  waiting for transfers between devices  9.3 us (17%)
  other arithmetic  3.04 us (5%)
  local copies, waits for them, and re-layouts  2.33 us (4%)
  between operations  0.77 us (1%)
    pallas_call x1, Pallas kernels, shards(): _vmem_call(_final_kernel, (jax.ShapeDtypeStruct(thickness.shape, jnp.floa...  15.3 us
    pallas_call x1, Pallas kernels, shards(): _vmem_call(_main1_kernel, jax.ShapeDtypeStruct(padded.shape, jnp.float32)...  10.1 us
    ppermute x1, waiting for transfers between devices, shards(): from_north = lax.ppermute(bottom, 'lat', _shift_pairs(nlat, -1, False))  7.73 us
    ppermute x1, starting transfers between devices, shards(): from_south = lax.ppermute(top, 'lat', _shift_pairs(nlat, 1, False))  5.02 us
    ppermute x1, starting transfers between devices, shards(): from_east = lax.ppermute(edges, 'lon', _shift_pairs(nlon, -1, True))  4.22 us
    pallas_call x1, Pallas kernels, shards(): _vmem_call(_edge_kernel, jax.ShapeDtypeStruct((nf, tall, w), jnp.float32)...  3.17 us
    ppermute x1, starting transfers between devices, shards(): from_north = lax.ppermute(bottom, 'lat', _shift_pairs(nlat, -1, False))  1.92 us
    ppermute x1, waiting for transfers between devices, shards(): from_south = lax.ppermute(top, 'lat', _shift_pairs(nlat, 1, False))  1.56 us
  transfers between devices with their start and end apart: 5, of which 2 were waited for; matrix products, arithmetic and copies ran while one was open for 2% of the time, Pallas kernels for 18%

profile of v2, /device:TPU:6, one launch (start us, length us, event | category | flops | bytes accessed | tf_op | source)
XLA Modules:
  0.0 55.9 jit_solution(8262754161449902104)
XLA Ops:
  0.6 0.0 copy-start
  0.6 0.0 copy-start.1
  0.7 0.0 copy-start.2
  0.7 1.3 %broadcast_select_fusion = (f32[11,8,4,128]{3,2,1,0:T(4,128)S(1)}, f32[11,8,4,128]{3,2,1,0:T(4,128)S(1)}, f32[11,8,4,128]{3,2,1,0:T(4,128)S(1)}) fusion(pred[]{:T(512)S(6)} %eq.14, f32[8,8,32,128]{3,2,1,0:T(8,128)} %param.5, f32[2,8,32,128]{3,2,1,0:T(8,128)} %param.4, f32[1,8,32,128]{3,2,1,0:T(8,128)} %bitcast.1), kind=kLoop, calls=%fused_computation.6 | loop fusion | flops 225280 | bytes 1982465 | tf_op jit(solution)/shard_map/jit(_where)/select_n | solution.py:197
  1.9 0.7 %collective-permute-start = (f32[11,8,4,128]{3,2,1,0:T(4,128)S(1)}, f32[11,8,4,128]{3,2,1,0:T(4,128)S(1)}, u32[]{:S(2)}, u32[]{:S(2)}) collective-permute-start(f32[11,8,4,128]{3,2,1,0:T(4,128)S(1)} %get-tuple-element.3), channel_id=1, source_target_pairs={{0,16},{1,17},{2,18},{3,19},{4,20},{5,21},{6,22},{7,23},{8,24},{9,... | collective-permute-start | bytes 540680 | tf_op jit(solution)/shard_map/ppermute | solution.py:198
  2.6 5.0 %collective-permute-start.1 = (f32[11,8,4,128]{3,2,1,0:T(4,128)S(1)}, f32[11,8,4,128]{3,2,1,0:T(4,128)S(1)}, u32[]{:S(2)}, u32[]{:S(2)}) collective-permute-start(f32[11,8,4,128]{3,2,1,0:T(4,128)S(1)} %get-tuple-element.4), channel_id=1, source_target_pairs={{0,32},{32,64},{64,96},{96,128},{128,160},{160,192},{192,224},{1,3... | collective-permute-start | bytes 540680 | tf_op jit(solution)/shard_map/ppermute | solution.py:190
  7.6 1.9 %collective-permute-start.2 = (f32[11,8,4,128]{3,2,1,0:T(4,128)S(1)}, f32[11,8,4,128]{3,2,1,0:T(4,128)S(1)}, u32[]{:S(2)}, u32[]{:S(2)}) collective-permute-start(f32[11,8,4,128]{3,2,1,0:T(4,128)S(1)} %get-tuple-element.5), channel_id=1, source_target_pairs={{32,0},{64,32},{96,64},{128,96},{160,128},{192,160},{224,192},{33,... | collective-permute-start | bytes 540680 | tf_op jit(solution)/shard_map/ppermute | solution.py:191
  9.6 0.1 fusion
  9.6 0.0 collective-permute-done
  9.6 0.2 rev.4
  9.9 1.6 %collective-permute-done.1 = f32[11,8,4,128]{3,2,1,0:T(4,128)S(1)} collective-permute-done((f32[11,8,4,128]{3,2,1,0:T(4,128)S(1)}, f32[11,8,4,128]{3,2,1,0:T(4,128)S(1)}, u32[]{:S(2)}, u32[]{:S(2)}) %collective-permute-start.1) | collective-permute-done | bytes 180256 | tf_op jit(solution)/shard_map/ppermute | solution.py:190
  11.4 7.7 %collective-permute-done.2 = f32[11,8,4,128]{3,2,1,0:T(4,128)S(1)} collective-permute-done((f32[11,8,4,128]{3,2,1,0:T(4,128)S(1)}, f32[11,8,4,128]{3,2,1,0:T(4,128)S(1)}, u32[]{:S(2)}, u32[]{:S(2)}) %collective-permute-start.2) | collective-permute-done | bytes 180256 | tf_op jit(solution)/shard_map/ppermute | solution.py:191
  19.2 0.1 multiply_select_fusion.1
  19.3 0.0 copy-done
  19.3 0.0 copy-done.1
  19.3 0.0 copy-done.2
  19.3 1.5 %pad_maximum_fusion.s_ref = f32[11,8,40,128]{3,2,1,0:T(8,128)} fusion(f32[11,8,4,128]{3,2,1,0:T(4,128)S(1)} %get-tuple-element.7, f32[8,8,32,128]{3,2,1,0:T(8,128)S(1)} %copy-done, f32[2,8,32,128]{3,2,1,0:T(8,128)S(1)} %copy-done.1, f32[1,8,32,128]{3,2,1,0:T(8,128)S(1)} %bitcast.2, f32[11,8,4,128]{3,2,1,0:T(4,128)S(1)} %get-tuple-element.6), kind=kLoop, calls=%fused_computation | loop fusion | flops 1802240 | bytes 3604480 | tf_op jit(solution)/shard_map/concatenate | solution.py:203
  20.9 3.2 %shard_map.59.e_ref = f32[11,40,128]{2,1,0:T(8,128)} custom-call(f32[11,8,40,128]{3,2,1,0:T(8,128)} %pad_maximum_fusion.s_ref), custom_call_target="tpu_custom_call" | custom-call | bytes 2027520 | tf_op jit(solution)/shard_map/pallas_call | solution.py:206
  24.0 4.2 %collective-permute-start.4 = (f32[11,40,128]{2,1,0:T(8,128)}, f32[11,40,128]{2,1,0:T(8,128)S(1)}, u32[]{:S(2)}, u32[]{:S(2)}) collective-permute-start(f32[11,40,128]{2,1,0:T(8,128)} %shard_map.59.e_ref), channel_id=1, source_target_pairs={{0,31},{1,0},{2,1},{3,2},{4,3},{5,4},{6,5},{7,6},{8,7},{9,8},{10,9... | collective-permute-start | bytes 675848 | tf_op jit(solution)/shard_map/ppermute | solution.py:210
  28.3 0.0 collective-permute-start.3
  28.3 0.7 %broadcast_in_dim.28.rv_ref = f32[3,40,128]{2,1,0:T(8,128)} broadcast(f32[3,40]{1,0:T(4,128)S(1)} %pad_maximum_fusion.4), dimensions={0,1} | broadcast | bytes 61920 | tf_op jit(solution)/shard_map/broadcast_in_dim | solution.py:186
  29.0 10.1 %shard_map.58.s1_ref = f32[11,8,40,128]{3,2,1,0:T(8,128)} custom-call(f32[11,8,40,128]{3,2,1,0:T(8,128)} %pad_maximum_fusion.s_ref, f32[3,40,128]{2,1,0:T(8,128)} %broadcast_in_dim.28.rv_ref), custom_call_target="tpu_custom_call" | custom-call | flops 27033600 | bytes 3604480 | tf_op jit(solution)/shard_map/pallas_call | solution.py:213
  39.1 0.0 collective-permute-done.4.ee_ref
  39.1 0.0 copy-start.3
  39.1 0.0 collective-permute-done.3.ew_ref
  39.1 0.7 %copy-done.3 = f32[11,40,128]{2,1,0:T(8,128)} copy-done((f32[11,40,128]{2,1,0:T(8,128)}, f32[11,40,128]{2,1,0:T(8,128)S(1)}, u32[]{:S(2)}) %copy-start.3) | copy-done | bytes 225304
  39.8 0.0 copy-start.4
  39.8 0.7 %copy-done.4 = f32[11,40,128]{2,1,0:T(8,128)} copy-done((f32[11,40,128]{2,1,0:T(8,128)}, f32[11,40,128]{2,1,0:T(8,128)S(1)}, u32[]{:S(2)}) %copy-start.4) | copy-done | bytes 225304
  40.5 15.3 %shard_map.60 = (f32[8,32,128]{2,1,0:T(8,128)}, f32[2,8,32,128]{3,2,1,0:T(8,128)}, f32[8,8,32,128]{3,2,1,0:T(8,128)}) custom-call(f32[11,8,40,128]{3,2,1,0:T(8,128)} %shard_map.58.s1_ref, f32[11,40,128]{2,1,0:T(8,128)} %shard_map.59.e_ref, f32[11,40,128]{2,1,0:T(8,128)} %copy-done.4, f32[11,40,128]{2,1,0:T(8,128)} %copy-done.3, ...), custom_call_target="tpu_custom_call" | custom-call | flops 37171200 | bytes 3604480 | tf_op jit(solution)/shard_map/pallas_call | solution.py:222
  (3 shorter events, 0.1 us)
Async XLA Ops:
  0.6 18.7 %copy-start = (f32[8,8,32,128]{3,2,1,0:T(8,128)S(1)}, f32[8,8,32,128]{3,2,1,0:T(8,128)}, u32[]{:S(2)}) copy-start(f32[8,8,32,128]{3,2,1,0:T(8,128)} %param.5) | copy-start | bytes 3145732
  0.6 18.7 %copy-start.1 = (f32[2,8,32,128]{3,2,1,0:T(8,128)S(1)}, f32[2,8,32,128]{3,2,1,0:T(8,128)}, u32[]{:S(2)}) copy-start(f32[2,8,32,128]{3,2,1,0:T(8,128)} %param.4) | copy-start | bytes 786436
  0.7 18.7 %copy-start.2 = (f32[8,32,128]{2,1,0:T(8,128)S(1)}, f32[8,32,128]{2,1,0:T(8,128)}, u32[]{:S(2)}) copy-start(f32[8,32,128]{2,1,0:T(8,128)} %param.3) | copy-start | bytes 393220
  1.9 7.7 %collective-permute-start = (f32[11,8,4,128]{3,2,1,0:T(4,128)S(1)}, f32[11,8,4,128]{3,2,1,0:T(4,128)S(1)}, u32[]{:S(2)}, u32[]{:S(2)}) collective-permute-start(f32[11,8,4,128]{3,2,1,0:T(4,128)S(1)} %get-tuple-element.3), channel_id=1, source_target_pairs={{0,16},{1,17},{2,18},{3,19},{4,20},{5,21},{6,22},{7,23},{8,24},{9,... | collective-permute-start | bytes 540680 | tf_op jit(solution)/shard_map/ppermute | solution.py:198
  2.6 8.8 %collective-permute-start.1 = (f32[11,8,4,128]{3,2,1,0:T(4,128)S(1)}, f32[11,8,4,128]{3,2,1,0:T(4,128)S(1)}, u32[]{:S(2)}, u32[]{:S(2)}) collective-permute-start(f32[11,8,4,128]{3,2,1,0:T(4,128)S(1)} %get-tuple-element.4), channel_id=1, source_target_pairs={{0,32},{32,64},{64,96},{96,128},{128,160},{160,192},{192,224},{1,3... | collective-permute-start | bytes 540680 | tf_op jit(solution)/shard_map/ppermute | solution.py:190
  7.6 11.5 %collective-permute-start.2 = (f32[11,8,4,128]{3,2,1,0:T(4,128)S(1)}, f32[11,8,4,128]{3,2,1,0:T(4,128)S(1)}, u32[]{:S(2)}, u32[]{:S(2)}) collective-permute-start(f32[11,8,4,128]{3,2,1,0:T(4,128)S(1)} %get-tuple-element.5), channel_id=1, source_target_pairs={{32,0},{64,32},{96,64},{128,96},{160,128},{192,160},{224,192},{33,... | collective-permute-start | bytes 540680 | tf_op jit(solution)/shard_map/ppermute | solution.py:191
  24.0 15.1 %collective-permute-start.4 = (f32[11,40,128]{2,1,0:T(8,128)}, f32[11,40,128]{2,1,0:T(8,128)S(1)}, u32[]{:S(2)}, u32[]{:S(2)}) collective-permute-start(f32[11,40,128]{2,1,0:T(8,128)} %shard_map.59.e_ref), channel_id=1, source_target_pairs={{0,31},{1,0},{2,1},{3,2},{4,3},{5,4},{6,5},{7,6},{8,7},{9,8},{10,9... | collective-permute-start | bytes 675848 | tf_op jit(solution)/shard_map/ppermute | solution.py:210
  28.3 10.9 %collective-permute-start.3 = (f32[11,40,128]{2,1,0:T(8,128)}, f32[11,40,128]{2,1,0:T(8,128)S(1)}, u32[]{:S(2)}, u32[]{:S(2)}) collective-permute-start(f32[11,40,128]{2,1,0:T(8,128)} %shard_map.59.e_ref), channel_id=1, source_target_pairs={{0,1},{1,2},{2,3},{3,4},{4,5},{5,6},{6,7},{7,8},{8,9},{9,10},{10,1... | collective-permute-start | bytes 675848 | tf_op jit(solution)/shard_map/ppermute | solution.py:209
  39.1 0.7 %copy-start.3 = (f32[11,40,128]{2,1,0:T(8,128)}, f32[11,40,128]{2,1,0:T(8,128)S(1)}, u32[]{:S(2)}) copy-start(f32[11,40,128]{2,1,0:T(8,128)S(1)} %collective-permute-done.4.ee_ref) | copy-start | bytes 675844
  39.8 0.7 %copy-start.4 = (f32[11,40,128]{2,1,0:T(8,128)}, f32[11,40,128]{2,1,0:T(8,128)S(1)}, u32[]{:S(2)}) copy-start(f32[11,40,128]{2,1,0:T(8,128)S(1)} %collective-permute-done.3.ew_ref) | copy-start | bytes 675844

commit v3 on v2

--- a/solution.py
+++ b/solution.py
@@ -14,6 +14,7 @@
 
 HALO = 2 * SUBSTEPS
 STRIP = 4 * HALO
+MARGIN = 8
 
 
 def _lroll(x, k):
@@ -21,32 +22,33 @@
     return pltpu.roll(x, k % n, x.ndim - 1)
 
 
-def _rroll(x, k):
-    n = x.shape[-2]
-    return pltpu.roll(x, k % n, x.ndim - 2)
-
-
-def _upwind(speed, pos, behind, centre, forward, beyond):
-    return speed * jnp.where(pos, 5.0 * centre + 2.0 * forward - behind, 5.0 * forward + 2.0 * centre - beyond)
-
-
-def _substep(load, store, nf, pot, rv):
+def _face(pos, behind, centre, forward, beyond):
+    p = jnp.where(pos, centre, forward)
+    q = jnp.where(pos, forward, centre)
+    r = jnp.where(pos, behind, beyond)
+    return 5.0 * p + 2.0 * q - r
+
+
+def _substep(load, store, nf, pot, rv, mf_ref):
     fcos, inv_acos, cor = rv
-    u = load(1)
-    v = load(2)
+    u = load(1, 0)
+    v = load(2, 0)
+    n = u.shape[0]
     fs = (COUR * 0.5 / 6.0) * (u + _lroll(u, -1))
-    ms = (COUR * 0.5 / 6.0) * (v + _rroll(v, -1)) * fcos
+    ms = (COUR * 0.5 / 6.0) * (v + load(2, 1)) * fcos
     fpos = fs >= 0.0
     mpos = ms >= 0.0
     for f in range(nf):
-        x = u if f == 1 else (v if f == 2 else load(f))
-        zf = _upwind(fs, fpos, _lroll(x, 1), x, _lroll(x, -1), _lroll(x, -2))
-        mf = _upwind(ms, mpos, _rroll(x, 1), x, _rroll(x, -1), _rroll(x, -2))
-        new = x - (zf - _lroll(zf, 1)) - (mf - _rroll(mf, 1)) * inv_acos
+        x = u if f == 1 else (v if f == 2 else load(f, 0))
+        zf = fs * _face(fpos, _lroll(x, 1), x, _lroll(x, -1), _lroll(x, -2))
+        mf = ms * _face(mpos, load(f, -1), x, load(f, 1), load(f, 2))
+        mf_ref[f, pl.ds(MARGIN, n)] = mf
+        new = x - (zf - _lroll(zf, 1)) - (mf - mf_ref[f, pl.ds(MARGIN - 1, n)]) * inv_acos
         if f == 1:
-            new = new - COUR * 0.5 * (_lroll(pot, -1) - _lroll(pot, 1)) + cor * v
+            p0 = pot(0)
+            new = new - COUR * 0.5 * (_lroll(p0, -1) - _lroll(p0, 1)) + cor * v
         elif f == 2:
-            new = new - COUR * 0.5 * (_rroll(pot, -1) - _rroll(pot, 1)) - cor * u
+            new = new - COUR * 0.5 * (pot(1) - pot(-1)) - cor * u
         store(f, new)
 
 
@@ -85,58 +87,96 @@
     return g
 
 
-def _potential(src, p_ref, nlev):
+def _potential(thick, p_ref, nlev, n):
     acc = None
     for lev in reversed(range(nlev)):
-        acc = src[0, lev] if acc is None else acc + src[0, lev]
-        p_ref[lev] = GRAV * acc
+        acc = thick(lev) if acc is None else acc + thick(lev)
+        p_ref[lev, pl.ds(MARGIN, n)] = GRAV * acc
 
 
 def _edge_kernel(s_ref, e_ref):
-    nf, nlev, rows, w = s_ref.shape
+    nf, nlev, _, w = s_ref.shape
+    rows = e_ref.shape[1]
     for f in range(nf):
         e_ref[f] = _pack_edges(lambda lev: s_ref[f, lev], nlev, rows, w, jnp.zeros((rows, w), jnp.float32))
 
 
-def _main1_kernel(s_ref, rv_ref, o_ref, p_ref):
+def _main1_kernel(s_ref, rv_ref, o_ref, p_ref, mf_ref, sp_ref):
     nf, nlev, rows, w = s_ref.shape
     rv = (rv_ref[0], rv_ref[1], rv_ref[2])
-    _potential(s_ref, p_ref, nlev)
+    win = pl.ds(MARGIN, rows)
+    _potential(lambda lev: s_ref[0, lev], p_ref, nlev, rows)
     for lev in range(nlev):
+        sp = sp_ref.at[lev % 2]
+        for f in range(nf):
+            sp[f, win] = s_ref[f, lev]
 
         def store(f, x, lev=lev):
-            o_ref[f, lev] = x
-
-        _substep(lambda f, lev=lev: s_ref[f, lev], store, nf, p_ref[lev], rv)
-
-
-def _final_kernel(s1_ref, e_ref, ew_ref, ee_ref, rv_ref, thk_ref, wind_ref, trc_ref, s_ref, g_ref, p_ref):
-    nf, nlev, rows, w = s1_ref.shape
-    rv = (rv_ref[0], rv_ref[1], rv_ref[2])
+            o_ref[f, lev, win] = x
+
+        _substep(
+            lambda f, d, sp=sp: sp[f, pl.ds(MARGIN + d, rows)],
+            store,
+            nf,
+            lambda d, lev=lev: p_ref[lev, pl.ds(MARGIN + d, rows)],
+            rv,
+            mf_ref,
+        )
+
+
+def _final_kernel(
+    s1_ref, e_ref, ew_ref, ee_ref, rv_ref, thk_ref, wind_ref, trc_ref, s_ref, g0_ref, g1_ref, g2_ref, p_ref, pg_ref, mf_ref, o2_ref
+):
+    nf, nlev, _, w = s1_ref.shape
+    rows = rv_ref.shape[1]
+    inner = rows - 2 * HALO
+    rv1 = (rv_ref[0], rv_ref[1], rv_ref[2])
     lane, group, kk = _lanes(rows, w)
-
-    def set_g(f, x):
-        g_ref[f] = x
-
-    for f in range(nf):
-        g_ref[f] = jnp.where(
+    win = pl.ds(MARGIN, rows)
+
+    for f in range(nf):
+        g0_ref[f, win] = jnp.where(
             kk < HALO, _lroll(ew_ref[f], -2 * HALO), jnp.where(kk >= 3 * HALO, _lroll(ee_ref[f], 2 * HALO), e_ref[f])
         )
-    _substep(lambda f: g_ref[f], set_g, nf, _suffix_packed(g_ref[0], group, nlev), rv)
-    for f in range(nf):
-        g = g_ref[f]
+    pg_ref[win] = _suffix_packed(g0_ref[0, win], group, nlev)
+
+    def set_g1(f, x):
+        g1_ref[f, win] = x
+
+    _substep(
+        lambda f, d: g0_ref[f, pl.ds(MARGIN + d, rows)],
+        set_g1,
+        nf,
+        lambda d: pg_ref[pl.ds(MARGIN + d, rows)],
+        rv1,
+        mf_ref,
+    )
+    for f in range(nf):
+        g = g1_ref[f, win]
         for lev in range(nlev):
-            s_ref[f, lev] = _fix_edges(s1_ref[f, lev], g, lev, lane)
-    for f in range(nf):
-        g_ref[f] = _pack_edges(lambda lev: s_ref[f, lev], nlev, rows, w, g_ref[f])
-    _substep(lambda f: g_ref[f], set_g, nf, _suffix_packed(g_ref[0], group, nlev), rv)
-    _potential(s_ref, p_ref, nlev)
-    inner = rows - 2 * HALO
+            s_ref[f, lev, win] = _fix_edges(s1_ref[f, lev, win], g, lev, lane)
+    for f in range(nf):
+        g1_ref[f, win] = _pack_edges(lambda lev: s_ref[f, lev, win], nlev, rows, w, g1_ref[f, win])
+    pg_ref[win] = _suffix_packed(g1_ref[0, win], group, nlev)
+
+    def set_g2(f, x):
+        g2_ref[f, win] = x
+
+    _substep(
+        lambda f, d: g1_ref[f, pl.ds(MARGIN + d, rows)],
+        set_g2,
+        nf,
+        lambda d: pg_ref[pl.ds(MARGIN + d, rows)],
+        rv1,
+        mf_ref,
+    )
+    _potential(lambda lev: s_ref[0, lev, win], p_ref, nlev, rows)
+    inner_rows = pl.ds(MARGIN + HALO, inner)
     for lev in range(nlev):
 
         def store2(f, x, lev=lev):
-            x = _fix_edges(x, g_ref[f], lev, lane)
-            x = _rroll(x, -HALO)[:inner]
+            o2_ref[f, win] = _fix_edges(x, g2_ref[f, win], lev, lane)
+            x = o2_ref[f, inner_rows]
             if f == 0:
                 thk_ref[lev] = x
             elif f < 3:
@@ -144,7 +184,14 @@
             else:
                 trc_ref[f - 3, lev] = x
 
-        _substep(lambda f, lev=lev: s_ref[f, lev], store2, nf, p_ref[lev], rv)
+        _substep(
+            lambda f, d, lev=lev: s_ref[f, lev, pl.ds(MARGIN + d, rows)],
+            store2,
+            nf,
+            lambda d, lev=lev: p_ref[lev, pl.ds(MARGIN + d, rows)],
+            rv1,
+            mf_ref,
+        )
 
 
 def _shift_pairs(n, d, closed):
@@ -203,18 +250,23 @@
     padded = jnp.concatenate([south, fields, north], 2)
 
     slab = nf * tall * w * 4
-    edges = _vmem_call(_edge_kernel, jax.ShapeDtypeStruct((nf, tall, w), jnp.float32), 1, [], 0, slab * (nlev + 1))(
+    edges = _vmem_call(_edge_kernel, jax.ShapeDtypeStruct((nf, tall, w), jnp.float32), 1, [], 0, 2 * slab * nlev)(
         padded
     )
     from_west = lax.ppermute(edges, "lon", _shift_pairs(nlon, 1, True))
     from_east = lax.ppermute(edges, "lon", _shift_pairs(nlon, -1, True))
 
     step_flops = 60 * nf * nlev * tall * w
+    deep = tall + 2 * MARGIN
     main1 = _vmem_call(
         _main1_kernel,
-        jax.ShapeDtypeStruct(padded.shape, jnp.float32),
+        jax.ShapeDtypeStruct((nf, nlev, deep, w), jnp.float32),
         2,
-        [pltpu.VMEM((nlev, tall, w), jnp.float32)],
+        [
+            pltpu.VMEM((nlev, deep, w), jnp.float32),
+            pltpu.VMEM((nf, deep, w), jnp.float32),
+            pltpu.VMEM((2, nf, deep, w), jnp.float32),
+        ],
         step_flops,
         2 * slab * nlev,
     )(padded, rowvec)
@@ -228,9 +280,14 @@
         ),
         5,
         [
-            pltpu.VMEM(padded.shape, jnp.float32),
-            pltpu.VMEM(edges.shape, jnp.float32),
-            pltpu.VMEM((nlev, tall, w), jnp.float32),
+            pltpu.VMEM((nf, nlev, deep, w), jnp.float32),
+            pltpu.VMEM((nf, tall + 2 * MARGIN, w), jnp.float32),
+            pltpu.VMEM((nf, tall + 2 * MARGIN, w), jnp.float32),
+            pltpu.VMEM((nf, tall + 2 * MARGIN, w), jnp.float32),
+            pltpu.VMEM((nlev, tall + 2 * MARGIN, w), jnp.float32),
+            pltpu.VMEM((tall + 2 * MARGIN, w), jnp.float32),
+            pltpu.VMEM((nf, tall + 2 * MARGIN, w), jnp.float32),
+            pltpu.VMEM((nf, tall + 2 * MARGIN, w), jnp.float32),
         ],
         step_flops + 3 * step_flops // nlev,
         2 * slab * nlev,

time: 56.1 us -> 57.2 us (1.020)
  Pallas kernels: 28.6 us -> 29.7 us
    pallas_call x1, Pallas kernels: 15.3 us -> 15.9 us  [shards(): _vmem_call(_final_kernel, (jax.ShapeDtypeStruct(thickness.shape, jnp.floa...]
  transfers between devices with their start and end apart: 5 -> 5, of which waited for: 2 -> 2; matrix products, arithmetic and copies ran while one was open for 2% -> 2% of each run, Pallas kernels for 18% -> 19%
where the time goes in v3:
time: 57.2 us; the launch traced here: 57 us
  Pallas kernels  29.7 us (52%)
  starting transfers between devices  11.8 us (21%)
  waiting for transfers between devices  9.3 us (16%)
  other arithmetic  3.05 us (5%)
  local copies, waits for them, and re-layouts  2.3 us (4%)
  between operations  0.77 us (1%)
    pallas_call x1, Pallas kernels, shards(): _vmem_call(_final_kernel, (jax.ShapeDtypeStruct(thickness.shape, jnp.floa...  15.9 us
    pallas_call x1, Pallas kernels, shards(): _vmem_call(_main1_kernel, jax.ShapeDtypeStruct((nf, nlev, deep, w), jnp.f...  10.6 us
    ppermute x1, waiting for transfers between devices, shards(): from_north = lax.ppermute(bottom, 'lat', _shift_pairs(nlat, -1, False))  7.73 us
    ppermute x1, starting transfers between devices, shards(): from_south = lax.ppermute(top, 'lat', _shift_pairs(nlat, 1, False))  5.02 us
    ppermute x1, starting transfers between devices, shards(): from_east = lax.ppermute(edges, 'lon', _shift_pairs(nlon, -1, True))  4.22 us
    pallas_call x1, Pallas kernels, shards(): _vmem_call(_edge_kernel, jax.ShapeDtypeStruct((nf, tall, w), jnp.float32)...  3.18 us
    ppermute x1, starting transfers between devices, shards(): from_north = lax.ppermute(bottom, 'lat', _shift_pairs(nlat, -1, False))  1.92 us
    ppermute x1, waiting for transfers between devices, shards(): from_south = lax.ppermute(top, 'lat', _shift_pairs(nlat, 1, False))  1.56 us
  transfers between devices with their start and end apart: 5, of which 2 were waited for; matrix products, arithmetic and copies ran while one was open for 2% of the time, Pallas kernels for 19%

profile of v3, /device:TPU:6, one launch (start us, length us, event | category | flops | bytes accessed | tf_op | source)
XLA Modules:
  0.0 57.0 jit_solution(16789699670063610659)
XLA Ops:
  0.6 0.0 copy-start.2
  0.6 0.0 copy-start.1
  0.7 0.0 copy-start
  0.7 1.3 %broadcast_select_fusion = (f32[11,8,4,128]{3,2,1,0:T(4,128)S(1)}, f32[11,8,4,128]{3,2,1,0:T(4,128)S(1)}, f32[11,8,4,128]{3,2,1,0:T(4,128)S(1)}) fusion(pred[]{:T(512)S(6)} %eq.14, f32[8,8,32,128]{3,2,1,0:T(8,128)} %param.5, f32[2,8,32,128]{3,2,1,0:T(8,128)} %param.4, f32[1,8,32,128]{3,2,1,0:T(8,128)} %bitcast.1), kind=kLoop, calls=%fused_computation.6 | loop fusion | flops 225280 | bytes 1982465 | tf_op jit(solution)/shard_map/jit(_where)/select_n | solution.py:244
  1.9 0.7 %collective-permute-start = (f32[11,8,4,128]{3,2,1,0:T(4,128)S(1)}, f32[11,8,4,128]{3,2,1,0:T(4,128)S(1)}, u32[]{:S(2)}, u32[]{:S(2)}) collective-permute-start(f32[11,8,4,128]{3,2,1,0:T(4,128)S(1)} %get-tuple-element.3), channel_id=1, source_target_pairs={{0,16},{1,17},{2,18},{3,19},{4,20},{5,21},{6,22},{7,23},{8,24},{9,... | collective-permute-start | bytes 540680 | tf_op jit(solution)/shard_map/ppermute | solution.py:245
  2.6 5.0 %collective-permute-start.1 = (f32[11,8,4,128]{3,2,1,0:T(4,128)S(1)}, f32[11,8,4,128]{3,2,1,0:T(4,128)S(1)}, u32[]{:S(2)}, u32[]{:S(2)}) collective-permute-start(f32[11,8,4,128]{3,2,1,0:T(4,128)S(1)} %get-tuple-element.4), channel_id=1, source_target_pairs={{0,32},{32,64},{64,96},{96,128},{128,160},{160,192},{192,224},{1,3... | collective-permute-start | bytes 540680 | tf_op jit(solution)/shard_map/ppermute | solution.py:237
  7.6 1.9 %collective-permute-start.2 = (f32[11,8,4,128]{3,2,1,0:T(4,128)S(1)}, f32[11,8,4,128]{3,2,1,0:T(4,128)S(1)}, u32[]{:S(2)}, u32[]{:S(2)}) collective-permute-start(f32[11,8,4,128]{3,2,1,0:T(4,128)S(1)} %get-tuple-element.5), channel_id=1, source_target_pairs={{32,0},{64,32},{96,64},{128,96},{160,128},{192,160},{224,192},{33,... | collective-permute-start | bytes 540680 | tf_op jit(solution)/shard_map/ppermute | solution.py:238
  9.6 0.1 fusion
  9.6 0.0 collective-permute-done
  9.7 0.2 rev.4
  9.9 1.6 %collective-permute-done.1 = f32[11,8,4,128]{3,2,1,0:T(4,128)S(1)} collective-permute-done((f32[11,8,4,128]{3,2,1,0:T(4,128)S(1)}, f32[11,8,4,128]{3,2,1,0:T(4,128)S(1)}, u32[]{:S(2)}, u32[]{:S(2)}) %collective-permute-start.1) | collective-permute-done | bytes 180256 | tf_op jit(solution)/shard_map/ppermute | solution.py:237
  11.4 7.7 %collective-permute-done.2 = f32[11,8,4,128]{3,2,1,0:T(4,128)S(1)} collective-permute-done((f32[11,8,4,128]{3,2,1,0:T(4,128)S(1)}, f32[11,8,4,128]{3,2,1,0:T(4,128)S(1)}, u32[]{:S(2)}, u32[]{:S(2)}) %collective-permute-start.2) | collective-permute-done | bytes 180256 | tf_op jit(solution)/shard_map/ppermute | solution.py:238
  19.2 0.1 multiply_select_fusion.1
  19.3 0.0 copy-done.2
  19.3 0.0 copy-done.1
  19.3 0.0 copy-done
  19.3 1.5 %pad_maximum_fusion.s_ref = f32[11,8,40,128]{3,2,1,0:T(8,128)} fusion(f32[11,8,4,128]{3,2,1,0:T(4,128)S(1)} %get-tuple-element.7, f32[8,8,32,128]{3,2,1,0:T(8,128)S(1)} %copy-done, f32[2,8,32,128]{3,2,1,0:T(8,128)S(1)} %copy-done.1, f32[1,8,32,128]{3,2,1,0:T(8,128)S(1)} %bitcast.2, f32[11,8,4,128]{3,2,1,0:T(4,128)S(1)} %get-tuple-element.6), kind=kLoop, calls=%fused_computation | loop fusion | flops 1802240 | bytes 3604480 | tf_op jit(solution)/shard_map/concatenate | solution.py:250
  20.9 3.2 %shard_map.59.e_ref = f32[11,40,128]{2,1,0:T(8,128)} custom-call(f32[11,8,40,128]{3,2,1,0:T(8,128)} %pad_maximum_fusion.s_ref), custom_call_target="tpu_custom_call" | custom-call | bytes 3604480 | tf_op jit(solution)/shard_map/pallas_call | solution.py:253
  24.1 0.0 collective-permute-start.3
  24.1 4.2 %collective-permute-start.4 = (f32[11,40,128]{2,1,0:T(8,128)}, f32[11,40,128]{2,1,0:T(8,128)S(1)}, u32[]{:S(2)}, u32[]{:S(2)}) collective-permute-start(f32[11,40,128]{2,1,0:T(8,128)} %shard_map.59.e_ref), channel_id=1, source_target_pairs={{0,31},{1,0},{2,1},{3,2},{4,3},{5,4},{6,5},{7,6},{8,7},{9,8},{10,9... | collective-permute-start | bytes 675848 | tf_op jit(solution)/shard_map/ppermute | solution.py:257
  28.3 0.7 %broadcast_in_dim.28.rv_ref = f32[3,40,128]{2,1,0:T(8,128)} broadcast(f32[3,40]{1,0:T(4,128)S(1)} %pad_maximum_fusion.4), dimensions={0,1} | broadcast | bytes 61920 | tf_op jit(solution)/shard_map/broadcast_in_dim | solution.py:233
  29.0 10.6 %shard_map.58.s1_ref = f32[11,8,56,128]{3,2,1,0:T(8,128)} custom-call(f32[11,8,40,128]{3,2,1,0:T(8,128)} %pad_maximum_fusion.s_ref, f32[3,40,128]{2,1,0:T(8,128)} %broadcast_in_dim.28.rv_ref), custom_call_target="tpu_custom_call" | custom-call | flops 27033600 | bytes 3604480 | tf_op jit(solution)/shard_map/pallas_call | solution.py:261
  39.6 0.0 collective-permute-done.3.ew_ref
  39.6 0.0 copy-start.3
  39.6 0.0 collective-permute-done.4.ee_ref
  39.6 0.7 %copy-done.3 = f32[11,40,128]{2,1,0:T(8,128)} copy-done((f32[11,40,128]{2,1,0:T(8,128)}, f32[11,40,128]{2,1,0:T(8,128)S(1)}, u32[]{:S(2)}) %copy-start.3) | copy-done | bytes 225304
  40.3 0.0 copy-start.4
  40.3 0.7 %copy-done.4 = f32[11,40,128]{2,1,0:T(8,128)} copy-done((f32[11,40,128]{2,1,0:T(8,128)}, f32[11,40,128]{2,1,0:T(8,128)S(1)}, u32[]{:S(2)}) %copy-start.4) | copy-done | bytes 225304
  41.0 15.9 %shard_map.60 = (f32[8,32,128]{2,1,0:T(8,128)}, f32[2,8,32,128]{3,2,1,0:T(8,128)}, f32[8,8,32,128]{3,2,1,0:T(8,128)}) custom-call(f32[11,8,56,128]{3,2,1,0:T(8,128)} %shard_map.58.s1_ref, f32[11,40,128]{2,1,0:T(8,128)} %shard_map.59.e_ref, f32[11,40,128]{2,1,0:T(8,128)} %copy-done.3, f32[11,40,128]{2,1,0:T(8,128)} %copy-done.4, ...), custom_call_target="tpu_custom_call" | custom-call | flops 37171200 | bytes 3604480 | tf_op jit(solution)/shard_map/pallas_call | solution.py:274
  (3 shorter events, 0.1 us)
Async XLA Ops:
  0.6 18.7 %copy-start.2 = (f32[8,32,128]{2,1,0:T(8,128)S(1)}, f32[8,32,128]{2,1,0:T(8,128)}, u32[]{:S(2)}) copy-start(f32[8,32,128]{2,1,0:T(8,128)} %param.3) | copy-start | bytes 393220
  0.6 18.7 %copy-start.1 = (f32[2,8,32,128]{3,2,1,0:T(8,128)S(1)}, f32[2,8,32,128]{3,2,1,0:T(8,128)}, u32[]{:S(2)}) copy-start(f32[2,8,32,128]{3,2,1,0:T(8,128)} %param.4) | copy-start | bytes 786436
  0.7 18.7 %copy-start = (f32[8,8,32,128]{3,2,1,0:T(8,128)S(1)}, f32[8,8,32,128]{3,2,1,0:T(8,128)}, u32[]{:S(2)}) copy-start(f32[8,8,32,128]{3,2,1,0:T(8,128)} %param.5) | copy-start | bytes 3145732
  1.9 7.7 %collective-permute-start = (f32[11,8,4,128]{3,2,1,0:T(4,128)S(1)}, f32[11,8,4,128]{3,2,1,0:T(4,128)S(1)}, u32[]{:S(2)}, u32[]{:S(2)}) collective-permute-start(f32[11,8,4,128]{3,2,1,0:T(4,128)S(1)} %get-tuple-element.3), channel_id=1, source_target_pairs={{0,16},{1,17},{2,18},{3,19},{4,20},{5,21},{6,22},{7,23},{8,24},{9,... | collective-permute-start | bytes 540680 | tf_op jit(solution)/shard_map/ppermute | solution.py:245
  2.6 8.8 %collective-permute-start.1 = (f32[11,8,4,128]{3,2,1,0:T(4,128)S(1)}, f32[11,8,4,128]{3,2,1,0:T(4,128)S(1)}, u32[]{:S(2)}, u32[]{:S(2)}) collective-permute-start(f32[11,8,4,128]{3,2,1,0:T(4,128)S(1)} %get-tuple-element.4), channel_id=1, source_target_pairs={{0,32},{32,64},{64,96},{96,128},{128,160},{160,192},{192,224},{1,3... | collective-permute-start | bytes 540680 | tf_op jit(solution)/shard_map/ppermute | solution.py:237
  7.6 11.5 %collective-permute-start.2 = (f32[11,8,4,128]{3,2,1,0:T(4,128)S(1)}, f32[11,8,4,128]{3,2,1,0:T(4,128)S(1)}, u32[]{:S(2)}, u32[]{:S(2)}) collective-permute-start(f32[11,8,4,128]{3,2,1,0:T(4,128)S(1)} %get-tuple-element.5), channel_id=1, source_target_pairs={{32,0},{64,32},{96,64},{128,96},{160,128},{192,160},{224,192},{33,... | collective-permute-start | bytes 540680 | tf_op jit(solution)/shard_map/ppermute | solution.py:238
  24.1 15.6 %collective-permute-start.3 = (f32[11,40,128]{2,1,0:T(8,128)}, f32[11,40,128]{2,1,0:T(8,128)S(1)}, u32[]{:S(2)}, u32[]{:S(2)}) collective-permute-start(f32[11,40,128]{2,1,0:T(8,128)} %shard_map.59.e_ref), channel_id=1, source_target_pairs={{0,1},{1,2},{2,3},{3,4},{4,5},{5,6},{6,7},{7,8},{8,9},{9,10},{10,1... | collective-permute-start | bytes 675848 | tf_op jit(solution)/shard_map/ppermute | solution.py:256
  24.1 15.6 %collective-permute-start.4 = (f32[11,40,128]{2,1,0:T(8,128)}, f32[11,40,128]{2,1,0:T(8,128)S(1)}, u32[]{:S(2)}, u32[]{:S(2)}) collective-permute-start(f32[11,40,128]{2,1,0:T(8,128)} %shard_map.59.e_ref), channel_id=1, source_target_pairs={{0,31},{1,0},{2,1},{3,2},{4,3},{5,4},{6,5},{7,6},{8,7},{9,8},{10,9... | collective-permute-start | bytes 675848 | tf_op jit(solution)/shard_map/ppermute | solution.py:257
  39.6 0.7 %copy-start.3 = (f32[11,40,128]{2,1,0:T(8,128)}, f32[11,40,128]{2,1,0:T(8,128)S(1)}, u32[]{:S(2)}) copy-start(f32[11,40,128]{2,1,0:T(8,128)S(1)} %collective-permute-done.3.ew_ref) | copy-start | bytes 675844
  40.3 0.7 %copy-start.4 = (f32[11,40,128]{2,1,0:T(8,128)}, f32[11,40,128]{2,1,0:T(8,128)S(1)}, u32[]{:S(2)}) copy-start(f32[11,40,128]{2,1,0:T(8,128)S(1)} %collective-permute-done.4.ee_ref) | copy-start | bytes 675844

commit v4 on v3

--- a/solution.py
+++ b/solution.py
@@ -94,34 +94,54 @@
         p_ref[lev, pl.ds(MARGIN, n)] = GRAV * acc
 
 
-def _edge_kernel(s_ref, e_ref):
-    nf, nlev, _, w = s_ref.shape
-    rows = e_ref.shape[1]
-    for f in range(nf):
-        e_ref[f] = _pack_edges(lambda lev: s_ref[f, lev], nlev, rows, w, jnp.zeros((rows, w), jnp.float32))
-
-
-def _main1_kernel(s_ref, rv_ref, o_ref, p_ref, mf_ref, sp_ref):
-    nf, nlev, rows, w = s_ref.shape
+def _edge_inner_kernel(thk_ref, wind_ref, trc_ref, e_ref):
+    nlev, rows, w = thk_ref.shape
+    zeros = jnp.zeros((rows, w), jnp.float32)
+    for f in range(e_ref.shape[0]):
+        if f == 0:
+            get = lambda lev: thk_ref[lev]
+        elif f < 3:
+            get = lambda lev, f=f: wind_ref[f - 1, lev]
+        else:
+            get = lambda lev, f=f: trc_ref[f - 3, lev]
+        e_ref[f] = _pack_edges(get, nlev, rows, w, zeros)
+
+
+def _edge_kernel(south_ref, inner_ref, north_ref, e_ref):
+    nf, nlev, halo, w = south_ref.shape
+    rows = inner_ref.shape[1]
+    zeros = jnp.zeros((halo, w), jnp.float32)
+    for f in range(nf):
+        e_ref[f, pl.ds(0, halo)] = _pack_edges(lambda lev: south_ref[f, lev], nlev, halo, w, zeros)
+        e_ref[f, pl.ds(halo, rows)] = inner_ref[f]
+        e_ref[f, pl.ds(halo + rows, halo)] = _pack_edges(lambda lev: north_ref[f, lev], nlev, halo, w, zeros)
+
+
+def _main1_kernel(s_ref, th_ref, rv_ref, o_ref, p_ref, mf_ref, sp_ref):
+    nf, _, rows, w = s_ref.shape
+    nlev = th_ref.shape[1]
+    lev = pl.program_id(0)
+    win = pl.ds(MARGIN, rows)
+
+    @pl.when(lev == 0)
+    def _():
+        _potential(lambda l: th_ref[0, l], p_ref, nlev, rows)
+
     rv = (rv_ref[0], rv_ref[1], rv_ref[2])
-    win = pl.ds(MARGIN, rows)
-    _potential(lambda lev: s_ref[0, lev], p_ref, nlev, rows)
-    for lev in range(nlev):
-        sp = sp_ref.at[lev % 2]
-        for f in range(nf):
-            sp[f, win] = s_ref[f, lev]
-
-        def store(f, x, lev=lev):
-            o_ref[f, lev, win] = x
-
-        _substep(
-            lambda f, d, sp=sp: sp[f, pl.ds(MARGIN + d, rows)],
-            store,
-            nf,
-            lambda d, lev=lev: p_ref[lev, pl.ds(MARGIN + d, rows)],
-            rv,
-            mf_ref,
-        )
+    for f in range(nf):
+        sp_ref[f, win] = s_ref[f, 0]
+
+    def store(f, x):
+        o_ref[f, 0, win] = x
+
+    _substep(
+        lambda f, d: sp_ref[f, pl.ds(MARGIN + d, rows)],
+        store,
+        nf,
+        lambda d: p_ref[lev, pl.ds(MARGIN + d, rows)],
+        rv,
+        mf_ref,
+    )
 
 
 def _final_kernel(
@@ -231,6 +251,10 @@
         ]
     )
     rowvec = jnp.broadcast_to(rowvec[:, :, None], (3, tall, w))
+
+    inner_edges = _vmem_call(
+        _edge_inner_kernel, jax.ShapeDtypeStruct((nf, rows, w), jnp.float32), 3, [], 0, nf * nlev * rows * w * 4
+    )(thickness, winds, tracer_mass)
 
     top = fields[:, :, rows - HALO :]
     bottom = fields[:, :, :HALO]
@@ -250,26 +274,32 @@
     padded = jnp.concatenate([south, fields, north], 2)
 
     slab = nf * tall * w * 4
-    edges = _vmem_call(_edge_kernel, jax.ShapeDtypeStruct((nf, tall, w), jnp.float32), 1, [], 0, 2 * slab * nlev)(
-        padded
-    )
+    edges = _vmem_call(
+        _edge_kernel, jax.ShapeDtypeStruct((nf, tall, w), jnp.float32), 3, [], 0, 2 * slab
+    )(south, inner_edges, north)
     from_west = lax.ppermute(edges, "lon", _shift_pairs(nlon, 1, True))
     from_east = lax.ppermute(edges, "lon", _shift_pairs(nlon, -1, True))
 
     step_flops = 60 * nf * nlev * tall * w
     deep = tall + 2 * MARGIN
-    main1 = _vmem_call(
+    main1 = pl.pallas_call(
         _main1_kernel,
-        jax.ShapeDtypeStruct((nf, nlev, deep, w), jnp.float32),
-        2,
-        [
+        out_shape=jax.ShapeDtypeStruct((nf, nlev, deep, w), jnp.float32),
+        grid=(nlev,),
+        in_specs=[
+            pl.BlockSpec((nf, 1, tall, w), lambda l: (0, l, 0, 0)),
+            pl.BlockSpec((1, nlev, tall, w), lambda l: (0, 0, 0, 0)),
+            pl.BlockSpec((3, tall, w), lambda l: (0, 0, 0)),
+        ],
+        out_specs=pl.BlockSpec((nf, 1, deep, w), lambda l: (0, l, 0, 0)),
+        scratch_shapes=[
             pltpu.VMEM((nlev, deep, w), jnp.float32),
             pltpu.VMEM((nf, deep, w), jnp.float32),
-            pltpu.VMEM((2, nf, deep, w), jnp.float32),
+            pltpu.VMEM((nf, deep, w), jnp.float32),
         ],
-        step_flops,
-        2 * slab * nlev,
-    )(padded, rowvec)
+        compiler_params=pltpu.CompilerParams(dimension_semantics=("arbitrary",)),
+        cost_estimate=pl.CostEstimate(flops=step_flops, bytes_accessed=2 * slab * nlev, transcendentals=0),
+    )(padded, padded, rowvec)
 
     return _vmem_call(
         _final_kernel,

time: 57.2 us -> 55.9 us (0.977)
  waiting for transfers between devices: 9.3 us -> 6.24 us
  other arithmetic: 3.05 us -> 4.66 us
    ppermute x1, waiting for transfers between devices: 1.56 us -> 0.01 us  [shards(): from_south = lax.ppermute(top, 'lat', _shift_pairs(nlat, 1, False))]
    ppermute x1, waiting for transfers between devices: 7.73 us -> 6.23 us  [shards(): from_north = lax.ppermute(bottom, 'lat', _shift_pairs(nlat, -1, False))]
    concatenate x1, other arithmetic: 1.54 us -> 2.52 us  [shards(): padded = jnp.concatenate([south, fields, north], 2)]
    pallas_call x1, Pallas kernels: 3.18 us -> 2.22 us  [shards(): _vmem_call(_edge_kernel, jax.ShapeDtypeStruct((nf, tall, w), jnp.float32)...]
    pallas_call x1 -> x2, Pallas kernels: 10.6 us -> 11.5 us  [the longest x1 8.55 us: shards(): pl.pallas_call(_main1_kernel, out_shape=jax.ShapeDtypeStruct((nf, nlev, d...]
    select_n x1, other arithmetic: 0.14 us -> 0.87 us  [shards(): south = jnp.where(band == 0, mirrored, from_south)]
  transfers between devices with their start and end apart: 5 -> 5, of which waited for: 2 -> 1; matrix products, arithmetic and copies ran while one was open for 2% -> 6% of each run, Pallas kernels for 19% -> 21%
where the time goes in v4:
time: 55.9 us; the launch traced here: 55.5 us
  Pallas kernels  29.7 us (53%)
  starting transfers between devices  11.8 us (21%)
  waiting for transfers between devices  6.24 us (11%)
  other arithmetic  4.66 us (8%)
  local copies, waits for them, and re-layouts  2.3 us (4%)
  between operations  0.76 us (1%)
    pallas_call x1, Pallas kernels, shards(): _vmem_call(_final_kernel, (jax.ShapeDtypeStruct(thickness.shape, jnp.floa...  15.9 us
    pallas_call x1, Pallas kernels, shards(): pl.pallas_call(_main1_kernel, out_shape=jax.ShapeDtypeStruct((nf, nlev, d...  8.55 us
    ppermute x1, waiting for transfers between devices, shards(): from_north = lax.ppermute(bottom, 'lat', _shift_pairs(nlat, -1, False))  6.23 us
    ppermute x1, starting transfers between devices, shards(): from_south = lax.ppermute(top, 'lat', _shift_pairs(nlat, 1, False))  5.02 us
    ppermute x1, starting transfers between devices, shards(): from_east = lax.ppermute(edges, 'lon', _shift_pairs(nlon, -1, True))  4.22 us
    pallas_call x1, Pallas kernels, shards(): _vmem_call(_edge_inner_kernel, jax.ShapeDtypeStruct((nf, rows, w), jnp.fl...  2.97 us
    concatenate x1, other arithmetic, shards(): padded = jnp.concatenate([south, fields, north], 2)  2.52 us
    pallas_call x1, Pallas kernels, shards(): _vmem_call(_edge_kernel, jax.ShapeDtypeStruct((nf, tall, w), jnp.float32)...  2.22 us
  transfers between devices with their start and end apart: 5, of which 1 were waited for; matrix products, arithmetic and copies ran while one was open for 6% of the time, Pallas kernels for 21%

profile of v4, /device:TPU:6, one launch (start us, length us, event | category | flops | bytes accessed | tf_op | source)
XLA Modules:
  0.0 55.5 jit_solution(4541026120195345042)
XLA Ops:
  0.6 1.2 %broadcast_select_fusion = (f32[11,8,4,128]{3,2,1,0:T(4,128)S(1)}, f32[11,8,4,128]{3,2,1,0:T(4,128)S(1)}, f32[11,8,4,128]{3,2,1,0:T(4,128)S(1)}) fusion(pred[]{:T(512)S(6)} %eq.14, f32[8,8,32,128]{3,2,1,0:T(8,128)} %trc_ref.1, f32[2,8,32,128]{3,2,1,0:T(8,128)} %wind_ref.1, f32[1,8,32,128]{3,2,1,0:T(8,128)} %bitcast.1), kind=kLoop, calls=%fused_computation.6 | loop fusion | flops 225280 | bytes 1982465 | tf_op jit(solution)/shard_map/jit(_where)/select_n | solution.py:268
  1.8 0.7 %collective-permute-start = (f32[11,8,4,128]{3,2,1,0:T(4,128)S(1)}, f32[11,8,4,128]{3,2,1,0:T(4,128)S(1)}, u32[]{:S(2)}, u32[]{:S(2)}) collective-permute-start(f32[11,8,4,128]{3,2,1,0:T(4,128)S(1)} %get-tuple-element.3), channel_id=1, source_target_pairs={{0,16},{1,17},{2,18},{3,19},{4,20},{5,21},{6,22},{7,23},{8,24},{9,... | collective-permute-start | bytes 540680 | tf_op jit(solution)/shard_map/ppermute | solution.py:269
  2.5 5.0 %collective-permute-start.1 = (f32[11,8,4,128]{3,2,1,0:T(4,128)S(1)}, f32[11,8,4,128]{3,2,1,0:T(4,128)S(1)}, u32[]{:S(2)}, u32[]{:S(2)}) collective-permute-start(f32[11,8,4,128]{3,2,1,0:T(4,128)S(1)} %get-tuple-element.4), channel_id=1, source_target_pairs={{0,32},{32,64},{64,96},{96,128},{128,160},{160,192},{192,224},{1,3... | collective-permute-start | bytes 540680 | tf_op jit(solution)/shard_map/ppermute | solution.py:261
  7.5 1.9 %collective-permute-start.2 = (f32[11,8,4,128]{3,2,1,0:T(4,128)S(1)}, f32[11,8,4,128]{3,2,1,0:T(4,128)S(1)}, u32[]{:S(2)}, u32[]{:S(2)}) collective-permute-start(f32[11,8,4,128]{3,2,1,0:T(4,128)S(1)} %get-tuple-element.5), channel_id=1, source_target_pairs={{32,0},{64,32},{96,64},{128,96},{160,128},{192,160},{224,192},{33,... | collective-permute-start | bytes 540680 | tf_op jit(solution)/shard_map/ppermute | solution.py:262
  9.4 0.0 copy-start
  9.5 0.0 copy-start.1
  9.5 0.0 copy-start.2
  9.5 3.0 %shard_map.59.inner_ref = f32[11,32,128]{2,1,0:T(8,128)} custom-call(f32[8,32,128]{2,1,0:T(8,128)} %thk_ref.1, f32[2,8,32,128]{3,2,1,0:T(8,128)} %wind_ref.1, f32[8,8,32,128]{3,2,1,0:T(8,128)} %trc_ref.1), custom_call_target="tpu_custom_call" | custom-call | bytes 1441792 | tf_op jit(solution)/shard_map/pallas_call | solution.py:255
  12.6 0.0 collective-permute-done
  12.6 0.2 rev.4
  12.8 0.0 collective-permute-done.1
  12.8 6.2 %collective-permute-done.2 = f32[11,8,4,128]{3,2,1,0:T(4,128)S(1)} collective-permute-done((f32[11,8,4,128]{3,2,1,0:T(4,128)S(1)}, f32[11,8,4,128]{3,2,1,0:T(4,128)S(1)}, u32[]{:S(2)}, u32[]{:S(2)}) %collective-permute-start.2) | collective-permute-done | bytes 180256 | tf_op jit(solution)/shard_map/ppermute | solution.py:262
  19.0 0.9 %multiply_select_fusion.1 = (f32[11,8,4,128]{3,2,1,0:T(4,128)}, f32[11,8,4,128]{3,2,1,0:T(4,128)}) fusion(f32[11,8,4,128]{3,2,1,0:T(4,128)S(1)} %collective-permute-done.1, f32[11,8,4,128]{3,2,1,0:T(4,128)S(1)} %rev.4, f32[11]{0:T(128)S(1)} %compare_select_fusion.1, pred[]{:T(512)S(6)} %eq.14, f32[11,8,4,128]{3,2,1,0:T(4,128)S(1)} %collective-permute-done.2, ...), kind=kLoop, calls=%fused_computation.5 | loop fusion | flops 135168 | bytes 901166 | tf_op jit(solution)/shard_map/jit(_where)/select_n | solution.py:272
  19.9 2.2 %shard_map.60.e_ref = f32[11,40,128]{2,1,0:T(8,128)} custom-call(f32[11,8,4,128]{3,2,1,0:T(4,128)} %get-tuple-element.6.south_ref, f32[11,32,128]{2,1,0:T(8,128)} %shard_map.59.inner_ref, f32[11,8,4,128]{3,2,1,0:T(4,128)} %get-tuple-element.7.north_ref), custom_call_target="tpu_custom_call" | custom-call | bytes 450560 | tf_op jit(solution)/shard_map/pallas_call | solution.py:277
  22.1 0.0 collective-permute-start.3
  22.1 4.2 %collective-permute-start.4 = (f32[11,40,128]{2,1,0:T(8,128)}, f32[11,40,128]{2,1,0:T(8,128)S(1)}, u32[]{:S(2)}, u32[]{:S(2)}) collective-permute-start(f32[11,40,128]{2,1,0:T(8,128)} %shard_map.60.e_ref), channel_id=1, source_target_pairs={{0,31},{1,0},{2,1},{3,2},{4,3},{5,4},{6,5},{7,6},{8,7},{9,8},{10,9... | collective-permute-start | bytes 675848 | tf_op jit(solution)/shard_map/ppermute | solution.py:281
  26.4 0.0 copy-done
  26.4 0.0 copy-done.1
  26.4 0.0 copy-done.2
  26.4 2.5 %pad_maximum_fusion.s_ref.th_ref = f32[11,8,40,128]{3,2,1,0:T(8,128)} fusion(f32[11,8,4,128]{3,2,1,0:T(4,128)} %get-tuple-element.7.north_ref, f32[8,8,32,128]{3,2,1,0:T(8,128)S(1)} %copy-done, f32[2,8,32,128]{3,2,1,0:T(8,128)S(1)} %copy-done.1, f32[1,8,32,128]{3,2,1,0:T(8,128)S(1)} %bitcast.2, f32[11,8,4,128]{3,2,1,0:T(4,128)} %get-tuple-element.6.south_ref), kind=kLoop, calls=%fused_computation | loop fusion | flops 1802240 | bytes 3604480 | tf_op jit(solution)/shard_map/concatenate | solution.py:274
  28.9 0.7 %broadcast_in_dim.28.rv_ref = f32[3,40,128]{2,1,0:T(8,128)} broadcast(f32[3,40]{1,0:T(4,128)S(1)} %pad_maximum_fusion.4), dimensions={0,1} | broadcast | bytes 61920 | tf_op jit(solution)/shard_map/broadcast_in_dim | solution.py:253
  29.6 8.5 %shard_map.58.s1_ref = f32[11,8,56,128]{3,2,1,0:T(8,128)} custom-call(f32[11,8,40,128]{3,2,1,0:T(8,128)} %pad_maximum_fusion.s_ref.th_ref, f32[11,8,40,128]{3,2,1,0:T(8,128)} %pad_maximum_fusion.s_ref.th_ref, f32[3,40,128]{2,1,0:T(8,128)} %broadcast_in_dim.28.rv_ref), custom_call_target="tpu_custom_call" | custom-call | flops 27033600 | bytes 3604480 | tf_op jit(solution)/shard_map/pallas_call | solution.py:285
  38.1 0.0 collective-permute-done.3.ew_ref
  38.2 0.0 copy-start.3
  38.2 0.0 collective-permute-done.4.ee_ref
  38.2 0.7 %copy-done.3 = f32[11,40,128]{2,1,0:T(8,128)} copy-done((f32[11,40,128]{2,1,0:T(8,128)}, f32[11,40,128]{2,1,0:T(8,128)S(1)}, u32[]{:S(2)}) %copy-start.3) | copy-done | bytes 225304
  38.8 0.0 copy-start.4
  38.8 0.7 %copy-done.4 = f32[11,40,128]{2,1,0:T(8,128)} copy-done((f32[11,40,128]{2,1,0:T(8,128)}, f32[11,40,128]{2,1,0:T(8,128)S(1)}, u32[]{:S(2)}) %copy-start.4) | copy-done | bytes 225304
  39.5 15.9 %shard_map.61 = (f32[8,32,128]{2,1,0:T(8,128)}, f32[2,8,32,128]{3,2,1,0:T(8,128)}, f32[8,8,32,128]{3,2,1,0:T(8,128)}) custom-call(f32[11,8,56,128]{3,2,1,0:T(8,128)} %shard_map.58.s1_ref, f32[11,40,128]{2,1,0:T(8,128)} %shard_map.60.e_ref, f32[11,40,128]{2,1,0:T(8,128)} %copy-done.3, f32[11,40,128]{2,1,0:T(8,128)} %copy-done.4, ...), custom_call_target="tpu_custom_call" | custom-call | flops 37171200 | bytes 3604480 | tf_op jit(solution)/shard_map/pallas_call | solution.py:304
  (4 shorter events, 0.1 us)
Async XLA Ops:
  1.8 10.8 %collective-permute-start = (f32[11,8,4,128]{3,2,1,0:T(4,128)S(1)}, f32[11,8,4,128]{3,2,1,0:T(4,128)S(1)}, u32[]{:S(2)}, u32[]{:S(2)}) collective-permute-start(f32[11,8,4,128]{3,2,1,0:T(4,128)S(1)} %get-tuple-element.3), channel_id=1, source_target_pairs={{0,16},{1,17},{2,18},{3,19},{4,20},{5,21},{6,22},{7,23},{8,24},{9,... | collective-permute-start | bytes 540680 | tf_op jit(solution)/shard_map/ppermute | solution.py:269
  2.5 10.3 %collective-permute-start.1 = (f32[11,8,4,128]{3,2,1,0:T(4,128)S(1)}, f32[11,8,4,128]{3,2,1,0:T(4,128)S(1)}, u32[]{:S(2)}, u32[]{:S(2)}) collective-permute-start(f32[11,8,4,128]{3,2,1,0:T(4,128)S(1)} %get-tuple-element.4), channel_id=1, source_target_pairs={{0,32},{32,64},{64,96},{96,128},{128,160},{160,192},{192,224},{1,3... | collective-permute-start | bytes 540680 | tf_op jit(solution)/shard_map/ppermute | solution.py:261
  7.5 11.5 %collective-permute-start.2 = (f32[11,8,4,128]{3,2,1,0:T(4,128)S(1)}, f32[11,8,4,128]{3,2,1,0:T(4,128)S(1)}, u32[]{:S(2)}, u32[]{:S(2)}) collective-permute-start(f32[11,8,4,128]{3,2,1,0:T(4,128)S(1)} %get-tuple-element.5), channel_id=1, source_target_pairs={{32,0},{64,32},{96,64},{128,96},{160,128},{192,160},{224,192},{33,... | collective-permute-start | bytes 540680 | tf_op jit(solution)/shard_map/ppermute | solution.py:262
  9.4 16.9 %copy-start = (f32[8,8,32,128]{3,2,1,0:T(8,128)S(1)}, f32[8,8,32,128]{3,2,1,0:T(8,128)}, u32[]{:S(2)}) copy-start(f32[8,8,32,128]{3,2,1,0:T(8,128)} %trc_ref.1) | copy-start | bytes 3145732
  9.5 16.9 %copy-start.1 = (f32[2,8,32,128]{3,2,1,0:T(8,128)S(1)}, f32[2,8,32,128]{3,2,1,0:T(8,128)}, u32[]{:S(2)}) copy-start(f32[2,8,32,128]{3,2,1,0:T(8,128)} %wind_ref.1) | copy-start | bytes 786436
  9.5 16.9 %copy-start.2 = (f32[8,32,128]{2,1,0:T(8,128)S(1)}, f32[8,32,128]{2,1,0:T(8,128)}, u32[]{:S(2)}) copy-start(f32[8,32,128]{2,1,0:T(8,128)} %thk_ref.1) | copy-start | bytes 393220
  22.1 16.0 %collective-permute-start.3 = (f32[11,40,128]{2,1,0:T(8,128)}, f32[11,40,128]{2,1,0:T(8,128)S(1)}, u32[]{:S(2)}, u32[]{:S(2)}) collective-permute-start(f32[11,40,128]{2,1,0:T(8,128)} %shard_map.60.e_ref), channel_id=1, source_target_pairs={{0,1},{1,2},{2,3},{3,4},{4,5},{5,6},{6,7},{7,8},{8,9},{9,10},{10,1... | collective-permute-start | bytes 675848 | tf_op jit(solution)/shard_map/ppermute | solution.py:280
  22.1 16.0 %collective-permute-start.4 = (f32[11,40,128]{2,1,0:T(8,128)}, f32[11,40,128]{2,1,0:T(8,128)S(1)}, u32[]{:S(2)}, u32[]{:S(2)}) collective-permute-start(f32[11,40,128]{2,1,0:T(8,128)} %shard_map.60.e_ref), channel_id=1, source_target_pairs={{0,31},{1,0},{2,1},{3,2},{4,3},{5,4},{6,5},{7,6},{8,7},{9,8},{10,9... | collective-permute-start | bytes 675848 | tf_op jit(solution)/shard_map/ppermute | solution.py:281
  38.2 0.7 %copy-start.3 = (f32[11,40,128]{2,1,0:T(8,128)}, f32[11,40,128]{2,1,0:T(8,128)S(1)}, u32[]{:S(2)}) copy-start(f32[11,40,128]{2,1,0:T(8,128)S(1)} %collective-permute-done.3.ew_ref) | copy-start | bytes 675844
  38.8 0.7 %copy-start.4 = (f32[11,40,128]{2,1,0:T(8,128)}, f32[11,40,128]{2,1,0:T(8,128)S(1)}, u32[]{:S(2)}) copy-start(f32[11,40,128]{2,1,0:T(8,128)S(1)} %collective-permute-done.4.ee_ref) | copy-start | bytes 675844

commit v5 on v4

--- a/solution.py
+++ b/solution.py
@@ -117,36 +117,60 @@
         e_ref[f, pl.ds(halo + rows, halo)] = _pack_edges(lambda lev: north_ref[f, lev], nlev, halo, w, zeros)
 
 
-def _main1_kernel(s_ref, th_ref, rv_ref, o_ref, p_ref, mf_ref, sp_ref):
-    nf, _, rows, w = s_ref.shape
-    nlev = th_ref.shape[1]
+def _main1_kernel(south_ref, thk_ref, wind_ref, trc_ref, north_ref, tall_ref, sall_ref, nall_ref, rv_ref, o_ref, p_ref, mf_ref, sp_ref):
+    nf, _, halo, w = south_ref.shape
+    nlev, rows = tall_ref.shape[0], tall_ref.shape[1]
     lev = pl.program_id(0)
-    win = pl.ds(MARGIN, rows)
+    tall = rows + 2 * halo
+    win = pl.ds(MARGIN, tall)
+    top = pl.ds(MARGIN, halo)
+    mid = pl.ds(MARGIN + halo, rows)
+    bot = pl.ds(MARGIN + halo + rows, halo)
 
     @pl.when(lev == 0)
     def _():
-        _potential(lambda l: th_ref[0, l], p_ref, nlev, rows)
+        acc = None
+        for l in reversed(range(nlev)):
+            part = (sall_ref[0, l], tall_ref[l], nall_ref[0, l])
+            acc = part if acc is None else tuple(x + y for x, y in zip(acc, part))
+            p_ref[l, top] = GRAV * acc[0]
+            p_ref[l, mid] = GRAV * acc[1]
+            p_ref[l, bot] = GRAV * acc[2]
 
     rv = (rv_ref[0], rv_ref[1], rv_ref[2])
     for f in range(nf):
-        sp_ref[f, win] = s_ref[f, 0]
+        sp_ref[f, top] = south_ref[f, 0]
+        if f == 0:
+            sp_ref[f, mid] = thk_ref[0]
+        elif f < 3:
+            sp_ref[f, mid] = wind_ref[f - 1, 0]
+        else:
+            sp_ref[f, mid] = trc_ref[f - 3, 0]
+        sp_ref[f, bot] = north_ref[f, 0]
 
     def store(f, x):
         o_ref[f, 0, win] = x
 
     _substep(
-        lambda f, d: sp_ref[f, pl.ds(MARGIN + d, rows)],
+        lambda f, d: sp_ref[f, pl.ds(MARGIN + d, tall)],
         store,
         nf,
-        lambda d: p_ref[lev, pl.ds(MARGIN + d, rows)],
+        lambda d: p_ref[lev, pl.ds(MARGIN + d, tall)],
         rv,
         mf_ref,
     )
 
 
 def _final_kernel(
-    s1_ref, e_ref, ew_ref, ee_ref, rv_ref, thk_ref, wind_ref, trc_ref, s_ref, g0_ref, g1_ref, g2_ref, p_ref, pg_ref, mf_ref, o2_ref
+    s1_ref, e_ref, ew_hbm, ee_hbm, rv_ref, thk_ref, wind_ref, trc_ref, s_ref, g0_ref, g1_ref, g2_ref, p_ref, pg_ref, mf_ref, o2_ref, nb_ref, sem
 ):
+    copies = [pltpu.make_async_copy(src, nb_ref.at[i], sem.at[i]) for i, src in enumerate((ew_hbm, ee_hbm))]
+    for c in copies:
+        c.start()
+    for c in copies:
+        c.wait()
+    ew_ref = nb_ref.at[0]
+    ee_ref = nb_ref.at[1]
     nf, nlev, _, w = s1_ref.shape
     rows = rv_ref.shape[1]
     inner = rows - 2 * HALO
@@ -271,7 +295,6 @@
     mirrored = jnp.flip(pole_in, 2) * sign
     south = jnp.where(band == 0, mirrored, from_south)
     north = jnp.where(band == nlat - 1, mirrored, from_north)
-    padded = jnp.concatenate([south, fields, north], 2)
 
     slab = nf * tall * w * 4
     edges = _vmem_call(
@@ -287,8 +310,14 @@
         out_shape=jax.ShapeDtypeStruct((nf, nlev, deep, w), jnp.float32),
         grid=(nlev,),
         in_specs=[
-            pl.BlockSpec((nf, 1, tall, w), lambda l: (0, l, 0, 0)),
-            pl.BlockSpec((1, nlev, tall, w), lambda l: (0, 0, 0, 0)),
+            pl.BlockSpec((nf, 1, HALO, w), lambda l: (0, l, 0, 0)),
+            pl.BlockSpec((1, rows, w), lambda l: (l, 0, 0)),
+            pl.BlockSpec((2, 1, rows, w), lambda l: (0, l, 0, 0)),
+            pl.BlockSpec((nf - 3, 1, rows, w), lambda l: (0, l, 0, 0)),
+            pl.BlockSpec((nf, 1, HALO, w), lambda l: (0, l, 0, 0)),
+            pl.BlockSpec((nlev, rows, w), lambda l: (0, 0, 0)),
+            pl.BlockSpec((1, nlev, HALO, w), lambda l: (0, 0, 0, 0)),
+            pl.BlockSpec((1, nlev, HALO, w), lambda l: (0, 0, 0, 0)),
             pl.BlockSpec((3, tall, w), lambda l: (0, 0, 0)),
         ],
         out_specs=pl.BlockSpec((nf, 1, deep, w), lambda l: (0, l, 0, 0)),
@@ -299,28 +328,34 @@
         ],
         compiler_params=pltpu.CompilerParams(dimension_semantics=("arbitrary",)),
         cost_estimate=pl.CostEstimate(flops=step_flops, bytes_accessed=2 * slab * nlev, transcendentals=0),
-    )(padded, padded, rowvec)
-
-    return _vmem_call(
+    )(south, thickness, winds, tracer_mass, north, thickness, south, north, rowvec)
+
+    vmem = pl.BlockSpec(memory_space=pltpu.VMEM)
+    anywhere = pl.BlockSpec(memory_space=pl.ANY)
+    return pl.pallas_call(
         _final_kernel,
-        (
+        out_shape=(
             jax.ShapeDtypeStruct(thickness.shape, jnp.float32),
             jax.ShapeDtypeStruct(winds.shape, jnp.float32),
             jax.ShapeDtypeStruct(tracer_mass.shape, jnp.float32),
         ),
-        5,
-        [
+        in_specs=[vmem, vmem, anywhere, anywhere, vmem],
+        out_specs=(vmem, vmem, vmem),
+        scratch_shapes=[
             pltpu.VMEM((nf, nlev, deep, w), jnp.float32),
-            pltpu.VMEM((nf, tall + 2 * MARGIN, w), jnp.float32),
-            pltpu.VMEM((nf, tall + 2 * MARGIN, w), jnp.float32),
-            pltpu.VMEM((nf, tall + 2 * MARGIN, w), jnp.float32),
-            pltpu.VMEM((nlev, tall + 2 * MARGIN, w), jnp.float32),
-            pltpu.VMEM((tall + 2 * MARGIN, w), jnp.float32),
-            pltpu.VMEM((nf, tall + 2 * MARGIN, w), jnp.float32),
-            pltpu.VMEM((nf, tall + 2 * MARGIN, w), jnp.float32),
+            pltpu.VMEM((nf, deep, w), jnp.float32),
+            pltpu.VMEM((nf, deep, w), jnp.float32),
+            pltpu.VMEM((nf, deep, w), jnp.float32),
+            pltpu.VMEM((nlev, deep, w), jnp.float32),
+            pltpu.VMEM((deep, w), jnp.float32),
+            pltpu.VMEM((nf, deep, w), jnp.float32),
+            pltpu.VMEM((nf, deep, w), jnp.float32),
+            pltpu.VMEM((2, nf, tall, w), jnp.float32),
+            pltpu.SemaphoreType.DMA((2,)),
         ],
-        step_flops + 3 * step_flops // nlev,
-        2 * slab * nlev,
+        cost_estimate=pl.CostEstimate(
+            flops=step_flops + 3 * step_flops // nlev, bytes_accessed=2 * slab * nlev, transcendentals=0
+        ),
     )(main1, edges, from_west, from_east, rowvec)
 
 

time: 55.9 us -> 55.5 us (level)
  the two profiles are of different devices: /device:TPU:6 before, /device:TPU:16 now
where the time goes in v5:
time: 55.5 us; the launch traced here: 55 us
  Pallas kernels  30.7 us (55%)
  starting transfers between devices  12.8 us (23%)
  waiting for transfers between devices  6.45 us (12%)
  local copies, waits for them, and re-layouts  2.3 us (4%)
  other arithmetic  2.14 us (4%)
  between operations  0.72 us (1%)
    pallas_call x1, Pallas kernels, shards(): pl.pallas_call(_final_kernel, out_shape=(jax.ShapeDtypeStruct(thickness.s...  16.9 us
    pallas_call x1, Pallas kernels, shards(): pl.pallas_call(_main1_kernel, out_shape=jax.ShapeDtypeStruct((nf, nlev, d...  8.7 us
    ppermute x1, waiting for transfers between devices, shards(): from_south = lax.ppermute(top, 'lat', _shift_pairs(nlat, 1, False))  6.43 us
    ppermute x1, starting transfers between devices, shards(): from_east = lax.ppermute(edges, 'lon', _shift_pairs(nlon, -1, True))  5.72 us
    ppermute x1, starting transfers between devices, shards(): from_north = lax.ppermute(bottom, 'lat', _shift_pairs(nlat, -1, False))  4.44 us
    pallas_call x1, Pallas kernels, shards(): _vmem_call(_edge_inner_kernel, jax.ShapeDtypeStruct((nf, rows, w), jnp.fl...  2.86 us
    pallas_call x1, Pallas kernels, shards(): _vmem_call(_edge_kernel, jax.ShapeDtypeStruct((nf, tall, w), jnp.float32)...  2.23 us
    ppermute x1, starting transfers between devices, shards(): from_south = lax.ppermute(top, 'lat', _shift_pairs(nlat, 1, False))  1.92 us
  transfers between devices with their start and end apart: 5, of which 1 were waited for; matrix products, arithmetic and copies ran while one was open for 2% of the time, Pallas kernels for 21%

profile of v5, /device:TPU:16, one launch (start us, length us, event | category | flops | bytes accessed | tf_op | source)
XLA Modules:
  0.0 55.0 jit_solution(18415707827351116591)
XLA Ops:
  0.6 1.2 %broadcast_select_fusion = (f32[11,8,4,128]{3,2,1,0:T(4,128)S(1)}, f32[11,8,4,128]{3,2,1,0:T(4,128)S(1)}, f32[11,8,4,128]{3,2,1,0:T(4,128)S(1)}) fusion(pred[]{:T(512)S(6)} %eq.14, f32[8,8,32,128]{3,2,1,0:T(8,128)} %trc_ref.3, f32[2,8,32,128]{3,2,1,0:T(8,128)} %wind_ref.3, f32[1,8,32,128]{3,2,1,0:T(8,128)} %bitcast.1), kind=kLoop, calls=%fused_computation.5 | loop fusion | flops 225280 | bytes 1982465 | tf_op jit(solution)/shard_map/jit(_where)/select_n | solution.py:292
  1.8 0.7 %collective-permute-start = (f32[11,8,4,128]{3,2,1,0:T(4,128)S(1)}, f32[11,8,4,128]{3,2,1,0:T(4,128)S(1)}, u32[]{:S(2)}, u32[]{:S(2)}) collective-permute-start(f32[11,8,4,128]{3,2,1,0:T(4,128)S(1)} %get-tuple-element.3), channel_id=1, source_target_pairs={{0,16},{1,17},{2,18},{3,19},{4,20},{5,21},{6,22},{7,23},{8,24},{9,... | collective-permute-start | bytes 540680 | tf_op jit(solution)/shard_map/ppermute | solution.py:293
  2.5 4.4 %collective-permute-start.2 = (f32[11,8,4,128]{3,2,1,0:T(4,128)S(1)}, f32[11,8,4,128]{3,2,1,0:T(4,128)S(1)}, u32[]{:S(2)}, u32[]{:S(2)}) collective-permute-start(f32[11,8,4,128]{3,2,1,0:T(4,128)S(1)} %get-tuple-element.4), channel_id=1, source_target_pairs={{32,0},{64,32},{96,64},{128,96},{160,128},{192,160},{224,192},{33,... | collective-permute-start | bytes 540680 | tf_op jit(solution)/shard_map/ppermute | solution.py:286
  6.9 1.9 %collective-permute-start.1 = (f32[11,8,4,128]{3,2,1,0:T(4,128)S(1)}, f32[11,8,4,128]{3,2,1,0:T(4,128)S(1)}, u32[]{:S(2)}, u32[]{:S(2)}) collective-permute-start(f32[11,8,4,128]{3,2,1,0:T(4,128)S(1)} %get-tuple-element.5), channel_id=1, source_target_pairs={{0,32},{32,64},{64,96},{96,128},{128,160},{160,192},{192,224},{1,3... | collective-permute-start | bytes 540680 | tf_op jit(solution)/shard_map/ppermute | solution.py:285
  8.9 2.9 %shard_map.59.inner_ref = f32[11,32,128]{2,1,0:T(8,128)} custom-call(f32[8,32,128]{2,1,0:T(8,128)} %thk_ref.3, f32[2,8,32,128]{3,2,1,0:T(8,128)} %wind_ref.3, f32[8,8,32,128]{3,2,1,0:T(8,128)} %trc_ref.3), custom_call_target="tpu_custom_call" | custom-call | bytes 1441792 | tf_op jit(solution)/shard_map/pallas_call | solution.py:279
  11.8 0.0 collective-permute-done
  11.8 0.2 rev.4
  12.0 0.0 collective-permute-done.2
  12.0 6.4 %collective-permute-done.1 = f32[11,8,4,128]{3,2,1,0:T(4,128)S(1)} collective-permute-done((f32[11,8,4,128]{3,2,1,0:T(4,128)S(1)}, f32[11,8,4,128]{3,2,1,0:T(4,128)S(1)}, u32[]{:S(2)}, u32[]{:S(2)}) %collective-permute-start.1) | collective-permute-done | bytes 180256 | tf_op jit(solution)/shard_map/ppermute | solution.py:285
  18.4 0.9 %multiply_select_fusion = (f32[11,8,4,128]{3,2,1,0:T(4,128)}, f32[11,8,4,128]{3,2,1,0:T(4,128)}) fusion(f32[11,8,4,128]{3,2,1,0:T(4,128)S(1)} %collective-permute-done.2, f32[11,8,4,128]{3,2,1,0:T(4,128)S(1)} %rev.4, f32[11]{0:T(128)S(1)} %compare_select_fusion.1, pred[]{:T(512)S(6)} %eq.16, f32[11,8,4,128]{3,2,1,0:T(4,128)S(1)} %collective-permute-done.1, ...), kind=kLoop, calls=%fused_computation.3 | loop fusion | flops 135168 | bytes 901166 | tf_op jit(solution)/shard_map/jit(_where)/select_n | solution.py:297
  19.3 2.2 %shard_map.60.e_ref = f32[11,40,128]{2,1,0:T(8,128)} custom-call(f32[11,8,4,128]{3,2,1,0:T(4,128)} %get-tuple-element.7.south_ref.sall_ref, f32[11,32,128]{2,1,0:T(8,128)} %shard_map.59.inner_ref, f32[11,8,4,128]{3,2,1,0:T(4,128)} %get-tuple-element.6.north_ref.nall_ref), custom_call_target="tpu_custom_call" | custom-call | bytes 450560 | tf_op jit(solution)/shard_map/pallas_call | solution.py:300
  21.5 5.7 %collective-permute-start.4 = (f32[11,40,128]{2,1,0:T(8,128)}, f32[11,40,128]{2,1,0:T(8,128)S(1)}, u32[]{:S(2)}, u32[]{:S(2)}) collective-permute-start(f32[11,40,128]{2,1,0:T(8,128)} %shard_map.60.e_ref), channel_id=1, source_target_pairs={{0,31},{1,0},{2,1},{3,2},{4,3},{5,4},{6,5},{7,6},{8,7},{9,8},{10,9... | collective-permute-start | bytes 675848 | tf_op jit(solution)/shard_map/ppermute | solution.py:304
  27.3 0.0 collective-permute-start.3
  27.3 0.7 %broadcast_in_dim.28.rv_ref = f32[3,40,128]{2,1,0:T(8,128)} broadcast(f32[3,40]{1,0:T(4,128)S(1)} %pad_maximum_fusion.3), dimensions={0,1} | broadcast | bytes 61920 | tf_op jit(solution)/shard_map/broadcast_in_dim | solution.py:277
  28.0 8.7 %shard_map.58.s1_ref = f32[11,8,56,128]{3,2,1,0:T(8,128)} custom-call(f32[11,8,4,128]{3,2,1,0:T(4,128)} %get-tuple-element.7.south_ref.sall_ref, f32[8,32,128]{2,1,0:T(8,128)} %thk_ref.3, f32[2,8,32,128]{3,2,1,0:T(8,128)} %wind_ref.3, f32[8,8,32,128]{3,2,1,0:T(8,128)} %trc_ref.3, f32[11,8,4,128]{3,2,1,0:T(4,128)} %get-tuple-element.6.north_ref.nall_ref, ...), custom_call_target="tpu_custom_call" | custom-call | flops 27033600 | bytes 3604480 | tf_op jit(solution)/shard_map/pallas_call | solution.py:308
  36.7 0.0 collective-permute-done.4.ee_hbm
  36.8 0.0 copy-start
  36.8 0.0 collective-permute-done.3.ew_hbm
  36.8 0.7 %copy-done = f32[11,40,128]{2,1,0:T(8,128)} copy-done((f32[11,40,128]{2,1,0:T(8,128)}, f32[11,40,128]{2,1,0:T(8,128)S(1)}, u32[]{:S(2)}) %copy-start) | copy-done | bytes 225304
  37.5 0.0 copy-start.1
  37.5 0.7 %copy-done.1 = f32[11,40,128]{2,1,0:T(8,128)} copy-done((f32[11,40,128]{2,1,0:T(8,128)}, f32[11,40,128]{2,1,0:T(8,128)S(1)}, u32[]{:S(2)}) %copy-start.1) | copy-done | bytes 225304
  38.2 16.9 %shard_map.61 = (f32[8,32,128]{2,1,0:T(8,128)}, f32[2,8,32,128]{3,2,1,0:T(8,128)}, f32[8,8,32,128]{3,2,1,0:T(8,128)}) custom-call(f32[11,8,56,128]{3,2,1,0:T(8,128)} %shard_map.58.s1_ref, f32[11,40,128]{2,1,0:T(8,128)} %shard_map.60.e_ref, f32[11,40,128]{2,1,0:T(8,128)} %copy-done.1, f32[11,40,128]{2,1,0:T(8,128)} %copy-done, ...), custom_call_target="tpu_custom_call" | custom-call | flops 37171200 | bytes 3604480 | tf_op jit(solution)/shard_map/pallas_call | solution.py:335
  (4 shorter events, 0.1 us)
Async XLA Ops:
  1.8 10.0 %collective-permute-start = (f32[11,8,4,128]{3,2,1,0:T(4,128)S(1)}, f32[11,8,4,128]{3,2,1,0:T(4,128)S(1)}, u32[]{:S(2)}, u32[]{:S(2)}) collective-permute-start(f32[11,8,4,128]{3,2,1,0:T(4,128)S(1)} %get-tuple-element.3), channel_id=1, source_target_pairs={{0,16},{1,17},{2,18},{3,19},{4,20},{5,21},{6,22},{7,23},{8,24},{9,... | collective-permute-start | bytes 540680 | tf_op jit(solution)/shard_map/ppermute | solution.py:293
  2.5 9.5 %collective-permute-start.2 = (f32[11,8,4,128]{3,2,1,0:T(4,128)S(1)}, f32[11,8,4,128]{3,2,1,0:T(4,128)S(1)}, u32[]{:S(2)}, u32[]{:S(2)}) collective-permute-start(f32[11,8,4,128]{3,2,1,0:T(4,128)S(1)} %get-tuple-element.4), channel_id=1, source_target_pairs={{32,0},{64,32},{96,64},{128,96},{160,128},{192,160},{224,192},{33,... | collective-permute-start | bytes 540680 | tf_op jit(solution)/shard_map/ppermute | solution.py:286
  6.9 11.5 %collective-permute-start.1 = (f32[11,8,4,128]{3,2,1,0:T(4,128)S(1)}, f32[11,8,4,128]{3,2,1,0:T(4,128)S(1)}, u32[]{:S(2)}, u32[]{:S(2)}) collective-permute-start(f32[11,8,4,128]{3,2,1,0:T(4,128)S(1)} %get-tuple-element.5), channel_id=1, source_target_pairs={{0,32},{32,64},{64,96},{96,128},{128,160},{160,192},{192,224},{1,3... | collective-permute-start | bytes 540680 | tf_op jit(solution)/shard_map/ppermute | solution.py:285
  21.5 15.2 %collective-permute-start.4 = (f32[11,40,128]{2,1,0:T(8,128)}, f32[11,40,128]{2,1,0:T(8,128)S(1)}, u32[]{:S(2)}, u32[]{:S(2)}) collective-permute-start(f32[11,40,128]{2,1,0:T(8,128)} %shard_map.60.e_ref), channel_id=1, source_target_pairs={{0,31},{1,0},{2,1},{3,2},{4,3},{5,4},{6,5},{7,6},{8,7},{9,8},{10,9... | collective-permute-start | bytes 675848 | tf_op jit(solution)/shard_map/ppermute | solution.py:304
  27.3 9.5 %collective-permute-start.3 = (f32[11,40,128]{2,1,0:T(8,128)}, f32[11,40,128]{2,1,0:T(8,128)S(1)}, u32[]{:S(2)}, u32[]{:S(2)}) collective-permute-start(f32[11,40,128]{2,1,0:T(8,128)} %shard_map.60.e_ref), channel_id=1, source_target_pairs={{0,1},{1,2},{2,3},{3,4},{4,5},{5,6},{6,7},{7,8},{8,9},{9,10},{10,1... | collective-permute-start | bytes 675848 | tf_op jit(solution)/shard_map/ppermute | solution.py:303
  36.8 0.7 %copy-start = (f32[11,40,128]{2,1,0:T(8,128)}, f32[11,40,128]{2,1,0:T(8,128)S(1)}, u32[]{:S(2)}) copy-start(f32[11,40,128]{2,1,0:T(8,128)S(1)} %collective-permute-done.4.ee_hbm) | copy-start | bytes 675844
  37.5 0.7 %copy-start.1 = (f32[11,40,128]{2,1,0:T(8,128)}, f32[11,40,128]{2,1,0:T(8,128)S(1)}, u32[]{:S(2)}) copy-start(f32[11,40,128]{2,1,0:T(8,128)S(1)} %collective-permute-done.3.ew_hbm) | copy-start | bytes 675844

commit v6 on v5

--- a/solution.py
+++ b/solution.py
@@ -149,7 +149,7 @@
         sp_ref[f, bot] = north_ref[f, 0]
 
     def store(f, x):
-        o_ref[f, 0, win] = x
+        o_ref[0, f] = x
 
     _substep(
         lambda f, d: sp_ref[f, pl.ds(MARGIN + d, tall)],
@@ -162,8 +162,13 @@
 
 
 def _final_kernel(
-    s1_ref, e_ref, ew_hbm, ee_hbm, rv_ref, thk_ref, wind_ref, trc_ref, s_ref, g0_ref, g1_ref, g2_ref, p_ref, pg_ref, mf_ref, o2_ref, nb_ref, sem
+    s1_hbm, e_ref, ew_hbm, ee_hbm, rv_ref, thk_hbm, wind_hbm, trc_hbm,
+    s_ref, g0_ref, g1_ref, g2_ref, p_ref, pg_ref, mf_ref, o2_ref, nb_ref, sem, s1_ref, s1_sem, ob_ref, out_sem,
 ):
+    nlev, nf, _, w = s1_hbm.shape
+    s1_copies = [pltpu.make_async_copy(s1_hbm.at[lev], s1_ref.at[lev], s1_sem.at[lev]) for lev in range(nlev)]
+    for c in s1_copies:
+        c.start()
     copies = [pltpu.make_async_copy(src, nb_ref.at[i], sem.at[i]) for i, src in enumerate((ew_hbm, ee_hbm))]
     for c in copies:
         c.start()
@@ -171,7 +176,6 @@
         c.wait()
     ew_ref = nb_ref.at[0]
     ee_ref = nb_ref.at[1]
-    nf, nlev, _, w = s1_ref.shape
     rows = rv_ref.shape[1]
     inner = rows - 2 * HALO
     rv1 = (rv_ref[0], rv_ref[1], rv_ref[2])
@@ -195,10 +199,10 @@
         rv1,
         mf_ref,
     )
-    for f in range(nf):
-        g = g1_ref[f, win]
-        for lev in range(nlev):
-            s_ref[f, lev, win] = _fix_edges(s1_ref[f, lev, win], g, lev, lane)
+    for lev in range(nlev):
+        s1_copies[lev].wait()
+        for f in range(nf):
+            s_ref[f, lev, win] = _fix_edges(s1_ref[lev, f], g1_ref[f, win], lev, lane)
     for f in range(nf):
         g1_ref[f, win] = _pack_edges(lambda lev: s_ref[f, lev, win], nlev, rows, w, g1_ref[f, win])
     pg_ref[win] = _suffix_packed(g1_ref[0, win], group, nlev)
@@ -216,17 +220,20 @@
     )
     _potential(lambda lev: s_ref[0, lev, win], p_ref, nlev, rows)
     inner_rows = pl.ds(MARGIN + HALO, inner)
+    out_copies = []
     for lev in range(nlev):
 
         def store2(f, x, lev=lev):
             o2_ref[f, win] = _fix_edges(x, g2_ref[f, win], lev, lane)
-            x = o2_ref[f, inner_rows]
+            ob_ref[lev, f] = o2_ref[f, inner_rows]
             if f == 0:
-                thk_ref[lev] = x
+                dst = thk_hbm.at[lev]
             elif f < 3:
-                wind_ref[f - 1, lev] = x
+                dst = wind_hbm.at[f - 1, lev]
             else:
-                trc_ref[f - 3, lev] = x
+                dst = trc_hbm.at[f - 3, lev]
+            out_copies.append(pltpu.make_async_copy(ob_ref.at[lev, f], dst, out_sem.at[lev, f]))
+            out_copies[-1].start()
 
         _substep(
             lambda f, d, lev=lev: s_ref[f, lev, pl.ds(MARGIN + d, rows)],
@@ -236,6 +243,8 @@
             rv1,
             mf_ref,
         )
+    for c in out_copies:
+        c.wait()
 
 
 def _shift_pairs(n, d, closed):
@@ -307,7 +316,7 @@
     deep = tall + 2 * MARGIN
     main1 = pl.pallas_call(
         _main1_kernel,
-        out_shape=jax.ShapeDtypeStruct((nf, nlev, deep, w), jnp.float32),
+        out_shape=jax.ShapeDtypeStruct((nlev, nf, tall, w), jnp.float32),
         grid=(nlev,),
         in_specs=[
             pl.BlockSpec((nf, 1, HALO, w), lambda l: (0, l, 0, 0)),
@@ -320,7 +329,7 @@
             pl.BlockSpec((1, nlev, HALO, w), lambda l: (0, 0, 0, 0)),
             pl.BlockSpec((3, tall, w), lambda l: (0, 0, 0)),
         ],
-        out_specs=pl.BlockSpec((nf, 1, deep, w), lambda l: (0, l, 0, 0)),
+        out_specs=pl.BlockSpec((1, nf, tall, w), lambda l: (l, 0, 0, 0)),
         scratch_shapes=[
             pltpu.VMEM((nlev, deep, w), jnp.float32),
             pltpu.VMEM((nf, deep, w), jnp.float32),
@@ -339,8 +348,8 @@
             jax.ShapeDtypeStruct(winds.shape, jnp.float32),
             jax.ShapeDtypeStruct(tracer_mass.shape, jnp.float32),
         ),
-        in_specs=[vmem, vmem, anywhere, anywhere, vmem],
-        out_specs=(vmem, vmem, vmem),
+        in_specs=[anywhere, vmem, anywhere, anywhere, vmem],
+        out_specs=(anywhere, anywhere, anywhere),
         scratch_shapes=[
             pltpu.VMEM((nf, nlev, deep, w), jnp.float32),
             pltpu.VMEM((nf, deep, w), jnp.float32),
@@ -352,6 +361,10 @@
             pltpu.VMEM((nf, deep, w), jnp.float32),
             pltpu.VMEM((2, nf, tall, w), jnp.float32),
             pltpu.SemaphoreType.DMA((2,)),
+            pltpu.VMEM((nlev, nf, tall, w), jnp.float32),
+            pltpu.SemaphoreType.DMA((nlev,)),
+            pltpu.VMEM((nlev, nf, rows, w), jnp.float32),
+            pltpu.SemaphoreType.DMA((nlev, nf)),
         ],
         cost_estimate=pl.CostEstimate(
             flops=step_flops + 3 * step_flops // nlev, bytes_accessed=2 * slab * nlev, transcendentals=0

time: 55.5 us -> 55.9 us (level)
    pallas_call x1, Pallas kernels: 16.9 us -> 17.5 us  [shards(): pl.pallas_call(_final_kernel, out_shape=(jax.ShapeDtypeStruct(thickness.s...]
where the time goes in v6:
time: 55.9 us; the launch traced here: 55.5 us
  Pallas kernels  31.1 us (56%)
  starting transfers between devices  12.8 us (23%)
  waiting for transfers between devices  6.45 us (12%)
  local copies, waits for them, and re-layouts  2.29 us (4%)
  other arithmetic  2.14 us (4%)
  between operations  0.72 us (1%)
    pallas_call x1, Pallas kernels, shards(): pl.pallas_call(_final_kernel, out_shape=(jax.ShapeDtypeStruct(thickness.s...  17.5 us
    pallas_call x1, Pallas kernels, shards(): pl.pallas_call(_main1_kernel, out_shape=jax.ShapeDtypeStruct((nlev, nf, t...  8.54 us
    ppermute x1, waiting for transfers between devices, shards(): from_south = lax.ppermute(top, 'lat', _shift_pairs(nlat, 1, False))  6.43 us
    ppermute x1, starting transfers between devices, shards(): from_east = lax.ppermute(edges, 'lon', _shift_pairs(nlon, -1, True))  5.72 us
    ppermute x1, starting transfers between devices, shards(): from_north = lax.ppermute(bottom, 'lat', _shift_pairs(nlat, -1, False))  4.44 us
    pallas_call x1, Pallas kernels, shards(): _vmem_call(_edge_inner_kernel, jax.ShapeDtypeStruct((nf, rows, w), jnp.fl...  2.86 us
    pallas_call x1, Pallas kernels, shards(): _vmem_call(_edge_kernel, jax.ShapeDtypeStruct((nf, tall, w), jnp.float32)...  2.21 us
    ppermute x1, starting transfers between devices, shards(): from_south = lax.ppermute(top, 'lat', _shift_pairs(nlat, 1, False))  1.92 us
  transfers between devices with their start and end apart: 5, of which 1 were waited for; matrix products, arithmetic and copies ran while one was open for 2% of the time, Pallas kernels for 21%

profile of v6, /device:TPU:16, one launch (start us, length us, event | category | flops | bytes accessed | tf_op | source)
XLA Modules:
  0.0 55.5 jit_solution(15675105875712352938)
XLA Ops:
  0.6 1.2 %broadcast_select_fusion = (f32[11,8,4,128]{3,2,1,0:T(4,128)S(1)}, f32[11,8,4,128]{3,2,1,0:T(4,128)S(1)}, f32[11,8,4,128]{3,2,1,0:T(4,128)S(1)}) fusion(pred[]{:T(512)S(6)} %eq.14, f32[8,8,32,128]{3,2,1,0:T(8,128)} %trc_ref.3, f32[2,8,32,128]{3,2,1,0:T(8,128)} %wind_ref.3, f32[1,8,32,128]{3,2,1,0:T(8,128)} %bitcast.1), kind=kLoop, calls=%fused_computation.5 | loop fusion | flops 225280 | bytes 1982465 | tf_op jit(solution)/shard_map/jit(_where)/select_n | solution.py:301
  1.8 0.7 %collective-permute-start = (f32[11,8,4,128]{3,2,1,0:T(4,128)S(1)}, f32[11,8,4,128]{3,2,1,0:T(4,128)S(1)}, u32[]{:S(2)}, u32[]{:S(2)}) collective-permute-start(f32[11,8,4,128]{3,2,1,0:T(4,128)S(1)} %get-tuple-element.3), channel_id=1, source_target_pairs={{0,16},{1,17},{2,18},{3,19},{4,20},{5,21},{6,22},{7,23},{8,24},{9,... | collective-permute-start | bytes 540680 | tf_op jit(solution)/shard_map/ppermute | solution.py:302
  2.5 4.4 %collective-permute-start.2 = (f32[11,8,4,128]{3,2,1,0:T(4,128)S(1)}, f32[11,8,4,128]{3,2,1,0:T(4,128)S(1)}, u32[]{:S(2)}, u32[]{:S(2)}) collective-permute-start(f32[11,8,4,128]{3,2,1,0:T(4,128)S(1)} %get-tuple-element.4), channel_id=1, source_target_pairs={{32,0},{64,32},{96,64},{128,96},{160,128},{192,160},{224,192},{33,... | collective-permute-start | bytes 540680 | tf_op jit(solution)/shard_map/ppermute | solution.py:295
  6.9 1.9 %collective-permute-start.1 = (f32[11,8,4,128]{3,2,1,0:T(4,128)S(1)}, f32[11,8,4,128]{3,2,1,0:T(4,128)S(1)}, u32[]{:S(2)}, u32[]{:S(2)}) collective-permute-start(f32[11,8,4,128]{3,2,1,0:T(4,128)S(1)} %get-tuple-element.5), channel_id=1, source_target_pairs={{0,32},{32,64},{64,96},{96,128},{128,160},{160,192},{192,224},{1,3... | collective-permute-start | bytes 540680 | tf_op jit(solution)/shard_map/ppermute | solution.py:294
  8.9 2.9 %shard_map.59.inner_ref = f32[11,32,128]{2,1,0:T(8,128)} custom-call(f32[8,32,128]{2,1,0:T(8,128)} %thk_ref.3, f32[2,8,32,128]{3,2,1,0:T(8,128)} %wind_ref.3, f32[8,8,32,128]{3,2,1,0:T(8,128)} %trc_ref.3), custom_call_target="tpu_custom_call" | custom-call | bytes 1441792 | tf_op jit(solution)/shard_map/pallas_call | solution.py:288
  11.8 0.0 collective-permute-done
  11.8 0.2 rev.4
  12.0 0.0 collective-permute-done.2
  12.0 6.4 %collective-permute-done.1 = f32[11,8,4,128]{3,2,1,0:T(4,128)S(1)} collective-permute-done((f32[11,8,4,128]{3,2,1,0:T(4,128)S(1)}, f32[11,8,4,128]{3,2,1,0:T(4,128)S(1)}, u32[]{:S(2)}, u32[]{:S(2)}) %collective-permute-start.1) | collective-permute-done | bytes 180256 | tf_op jit(solution)/shard_map/ppermute | solution.py:294
  18.4 0.9 %multiply_select_fusion = (f32[11,8,4,128]{3,2,1,0:T(4,128)}, f32[11,8,4,128]{3,2,1,0:T(4,128)}) fusion(f32[11,8,4,128]{3,2,1,0:T(4,128)S(1)} %collective-permute-done.2, f32[11,8,4,128]{3,2,1,0:T(4,128)S(1)} %rev.4, f32[11]{0:T(128)S(1)} %compare_select_fusion.1, pred[]{:T(512)S(6)} %eq.16, f32[11,8,4,128]{3,2,1,0:T(4,128)S(1)} %collective-permute-done.1, ...), kind=kLoop, calls=%fused_computation.3 | loop fusion | flops 135168 | bytes 901166 | tf_op jit(solution)/shard_map/jit(_where)/select_n | solution.py:306
  19.3 2.2 %shard_map.60.e_ref = f32[11,40,128]{2,1,0:T(8,128)} custom-call(f32[11,8,4,128]{3,2,1,0:T(4,128)} %get-tuple-element.7.south_ref.sall_ref, f32[11,32,128]{2,1,0:T(8,128)} %shard_map.59.inner_ref, f32[11,8,4,128]{3,2,1,0:T(4,128)} %get-tuple-element.6.north_ref.nall_ref), custom_call_target="tpu_custom_call" | custom-call | bytes 450560 | tf_op jit(solution)/shard_map/pallas_call | solution.py:309
  21.5 5.7 %collective-permute-start.4 = (f32[11,40,128]{2,1,0:T(8,128)}, f32[11,40,128]{2,1,0:T(8,128)S(1)}, u32[]{:S(2)}, u32[]{:S(2)}) collective-permute-start(f32[11,40,128]{2,1,0:T(8,128)} %shard_map.60.e_ref), channel_id=1, source_target_pairs={{0,31},{1,0},{2,1},{3,2},{4,3},{5,4},{6,5},{7,6},{8,7},{9,8},{10,9... | collective-permute-start | bytes 675848 | tf_op jit(solution)/shard_map/ppermute | solution.py:313
  27.3 0.0 collective-permute-start.3
  27.3 0.7 %broadcast_in_dim.28.rv_ref = f32[3,40,128]{2,1,0:T(8,128)} broadcast(f32[3,40]{1,0:T(4,128)S(1)} %pad_maximum_fusion.3), dimensions={0,1} | broadcast | bytes 61920 | tf_op jit(solution)/shard_map/broadcast_in_dim | solution.py:286
  28.0 8.5 %shard_map.58.s1_hbm = f32[8,11,40,128]{3,2,1,0:T(8,128)} custom-call(f32[11,8,4,128]{3,2,1,0:T(4,128)} %get-tuple-element.7.south_ref.sall_ref, f32[8,32,128]{2,1,0:T(8,128)} %thk_ref.3, f32[2,8,32,128]{3,2,1,0:T(8,128)} %wind_ref.3, f32[8,8,32,128]{3,2,1,0:T(8,128)} %trc_ref.3, f32[11,8,4,128]{3,2,1,0:T(4,128)} %get-tuple-element.6.north_ref.nall_ref, ...), custom_call_target="tpu_custom_call" | custom-call | flops 27033600 | bytes 3604480 | tf_op jit(solution)/shard_map/pallas_call | solution.py:317
  36.6 0.0 collective-permute-done.4.ee_hbm
  36.6 0.0 copy-start
  36.6 0.0 collective-permute-done.3.ew_hbm
  36.6 0.7 %copy-done = f32[11,40,128]{2,1,0:T(8,128)} copy-done((f32[11,40,128]{2,1,0:T(8,128)}, f32[11,40,128]{2,1,0:T(8,128)S(1)}, u32[]{:S(2)}) %copy-start) | copy-done | bytes 225304
  37.3 0.0 copy-start.1
  37.3 0.7 %copy-done.1 = f32[11,40,128]{2,1,0:T(8,128)} copy-done((f32[11,40,128]{2,1,0:T(8,128)}, f32[11,40,128]{2,1,0:T(8,128)S(1)}, u32[]{:S(2)}) %copy-start.1) | copy-done | bytes 225304
  38.0 17.5 %shard_map.61 = (f32[8,32,128]{2,1,0:T(8,128)}, f32[2,8,32,128]{3,2,1,0:T(8,128)}, f32[8,8,32,128]{3,2,1,0:T(8,128)}) custom-call(f32[8,11,40,128]{3,2,1,0:T(8,128)} %shard_map.58.s1_hbm, f32[11,40,128]{2,1,0:T(8,128)} %shard_map.60.e_ref, f32[11,40,128]{2,1,0:T(8,128)} %copy-done.1, f32[11,40,128]{2,1,0:T(8,128)} %copy-done, ...), custom_call_target="tpu_custom_call" | custom-call | flops 37171200 | bytes 3604480 | tf_op jit(solution)/shard_map/pallas_call | solution.py:344
  (4 shorter events, 0.1 us)
Async XLA Ops:
  1.8 10.0 %collective-permute-start = (f32[11,8,4,128]{3,2,1,0:T(4,128)S(1)}, f32[11,8,4,128]{3,2,1,0:T(4,128)S(1)}, u32[]{:S(2)}, u32[]{:S(2)}) collective-permute-start(f32[11,8,4,128]{3,2,1,0:T(4,128)S(1)} %get-tuple-element.3), channel_id=1, source_target_pairs={{0,16},{1,17},{2,18},{3,19},{4,20},{5,21},{6,22},{7,23},{8,24},{9,... | collective-permute-start | bytes 540680 | tf_op jit(solution)/shard_map/ppermute | solution.py:302
  2.5 9.5 %collective-permute-start.2 = (f32[11,8,4,128]{3,2,1,0:T(4,128)S(1)}, f32[11,8,4,128]{3,2,1,0:T(4,128)S(1)}, u32[]{:S(2)}, u32[]{:S(2)}) collective-permute-start(f32[11,8,4,128]{3,2,1,0:T(4,128)S(1)} %get-tuple-element.4), channel_id=1, source_target_pairs={{32,0},{64,32},{96,64},{128,96},{160,128},{192,160},{224,192},{33,... | collective-permute-start | bytes 540680 | tf_op jit(solution)/shard_map/ppermute | solution.py:295
  6.9 11.5 %collective-permute-start.1 = (f32[11,8,4,128]{3,2,1,0:T(4,128)S(1)}, f32[11,8,4,128]{3,2,1,0:T(4,128)S(1)}, u32[]{:S(2)}, u32[]{:S(2)}) collective-permute-start(f32[11,8,4,128]{3,2,1,0:T(4,128)S(1)} %get-tuple-element.5), channel_id=1, source_target_pairs={{0,32},{32,64},{64,96},{96,128},{128,160},{160,192},{192,224},{1,3... | collective-permute-start | bytes 540680 | tf_op jit(solution)/shard_map/ppermute | solution.py:294
  21.5 15.0 %collective-permute-start.4 = (f32[11,40,128]{2,1,0:T(8,128)}, f32[11,40,128]{2,1,0:T(8,128)S(1)}, u32[]{:S(2)}, u32[]{:S(2)}) collective-permute-start(f32[11,40,128]{2,1,0:T(8,128)} %shard_map.60.e_ref), channel_id=1, source_target_pairs={{0,31},{1,0},{2,1},{3,2},{4,3},{5,4},{6,5},{7,6},{8,7},{9,8},{10,9... | collective-permute-start | bytes 675848 | tf_op jit(solution)/shard_map/ppermute | solution.py:313
  27.3 9.3 %collective-permute-start.3 = (f32[11,40,128]{2,1,0:T(8,128)}, f32[11,40,128]{2,1,0:T(8,128)S(1)}, u32[]{:S(2)}, u32[]{:S(2)}) collective-permute-start(f32[11,40,128]{2,1,0:T(8,128)} %shard_map.60.e_ref), channel_id=1, source_target_pairs={{0,1},{1,2},{2,3},{3,4},{4,5},{5,6},{6,7},{7,8},{8,9},{9,10},{10,1... | collective-permute-start | bytes 675848 | tf_op jit(solution)/shard_map/ppermute | solution.py:312
  36.6 0.7 %copy-start = (f32[11,40,128]{2,1,0:T(8,128)}, f32[11,40,128]{2,1,0:T(8,128)S(1)}, u32[]{:S(2)}) copy-start(f32[11,40,128]{2,1,0:T(8,128)S(1)} %collective-permute-done.4.ee_hbm) | copy-start | bytes 675844
  37.3 0.7 %copy-start.1 = (f32[11,40,128]{2,1,0:T(8,128)}, f32[11,40,128]{2,1,0:T(8,128)S(1)}, u32[]{:S(2)}) copy-start(f32[11,40,128]{2,1,0:T(8,128)S(1)} %collective-permute-done.3.ew_hbm) | copy-start | bytes 675844

commit v7 on v3

v7 whole, which is shorter than its diff:
```python
import math

import jax
import jax.numpy as jnp
from jax import lax
from jax.experimental import pallas as pl
from jax.experimental.pallas import tpu as pltpu
from jax.sharding import PartitionSpec as P

SUBSTEPS = 2
COUR = 0.25
GRAV = 1.0
FCOR = 1.0

HALO = 2 * SUBSTEPS
GW = 6 * HALO
MARGIN = 8


def _lroll(x, k):
    n = x.shape[-1]
    return pltpu.roll(x, k % n, x.ndim - 1)


def _face(pos, behind, centre, forward, beyond):
    p = jnp.where(pos, centre, forward)
    q = jnp.where(pos, forward, centre)
    r = jnp.where(pos, behind, beyond)
    return 5.0 * p + 2.0 * q - r


def _substep(load, store, nf, pot, rv, mf_ref):
    fcos, inv_acos, cor = rv
    u = load(1, 0)
    v = load(2, 0)
    n = u.shape[0]
    fs = (COUR * 0.5 / 6.0) * (u + _lroll(u, -1))
    ms = (COUR * 0.5 / 6.0) * (v + load(2, 1)) * fcos
    fpos = fs >= 0.0
    mpos = ms >= 0.0
    for f in range(nf):
        x = u if f == 1 else (v if f == 2 else load(f, 0))
        zf = fs * _face(fpos, _lroll(x, 1), x, _lroll(x, -1), _lroll(x, -2))
        mf = ms * _face(mpos, load(f, -1), x, load(f, 1), load(f, 2))
        mf_ref[f, pl.ds(MARGIN, n)] = mf
        new = x - (zf - _lroll(zf, 1)) - (mf - mf_ref[f, pl.ds(MARGIN - 1, n)]) * inv_acos
        if f == 1:
            p0 = pot(0)
            new = new - COUR * 0.5 * (_lroll(p0, -1) - _lroll(p0, 1)) + cor * v
        elif f == 2:
            new = new - COUR * 0.5 * (pot(1) - pot(-1)) - cor * u
        store(f, new)


def _slab_of(lev, per):
    return lev // per, lev % per


def _lanes(rows, w):
    lane = lax.broadcasted_iota(jnp.int32, (rows, w), 1)
    return lane, lane // GW, lane % GW


def _pack_own(get, nlev, rows, w, slab, init):
    per = w // GW
    lane, group, kk = _lanes(rows, w)
    lo_mask = (kk >= HALO) & (kk < 3 * HALO)
    hi_mask = (kk >= 3 * HALO) & (kk < 5 * HALO)
    g = init
    for lev in range(slab * per, min(nlev, (slab + 1) * per)):
        m = get(lev)
        base = GW * (lev - slab * per)
        g = jnp.where((group == lev - slab * per) & lo_mask, _lroll(m, base + HALO), g)
        g = jnp.where((group == lev - slab * per) & hi_mask, _lroll(m, base + 3 * HALO - (w - 2 * HALO)), g)
    return g


def _packed_potential(h, nlev, w, pg_ref, n):
    per = w // GW
    nslab = len(h)
    _, group, _ = _lanes(n, w)
    below = None
    for s in reversed(range(nslab)):
        ng = min(per, nlev - s * per)
        acc = h[s]
        k = 1
        while k < ng:
            acc = acc + jnp.where(group + k < ng, _lroll(acc, -GW * k), 0.0)
            k *= 2
        if below is not None:
            spread = below
            for g in range(1, ng):
                spread = jnp.where(group == g, _lroll(below, GW * g), spread)
            acc = acc + spread
        pg_ref[s, pl.ds(MARGIN, n)] = GRAV * acc
        below = jnp.where(group == 0, acc, 0.0)


def _edge_inner_kernel(thk_ref, wind_ref, trc_ref, e_ref):
    nlev, rows, w = thk_ref.shape
    nslab, nf = e_ref.shape[0], e_ref.shape[1]
    zeros = jnp.zeros((rows, w), jnp.float32)
    for s in range(nslab):
        for f in range(nf):
            if f == 0:
                get = lambda lev: thk_ref[lev]
            elif f < 3:
                get = lambda lev, f=f: wind_ref[f - 1, lev]
            else:
                get = lambda lev, f=f: trc_ref[f - 3, lev]
            e_ref[s, f] = _pack_own(get, nlev, rows, w, s, zeros)


def _edge_kernel(south_ref, inner_ref, north_ref, e_ref):
    nf, nlev, halo, w = south_ref.shape
    nslab, rows = inner_ref.shape[0], inner_ref.shape[2]
    zeros = jnp.zeros((halo, w), jnp.float32)
    for s in range(nslab):
        for f in range(nf):
            e_ref[s, f, pl.ds(0, halo)] = _pack_own(lambda lev: south_ref[f, lev], nlev, halo, w, s, zeros)
            e_ref[s, f, pl.ds(halo, rows)] = inner_ref[s, f]
            e_ref[s, f, pl.ds(halo + rows, halo)] = _pack_own(lambda lev: north_ref[f, lev], nlev, halo, w, s, zeros)


def _main_kernel(
    south_ref, thk_ref, wind_ref, trc_ref, north_ref, tall_ref, sall_ref, nall_ref, rv_ref,
    thk_o, wind_o, trc_o, p_ref, mf_ref, sp_ref, s1_ref,
):
    nf, _, halo, w = south_ref.shape
    nlev, rows = tall_ref.shape[0], tall_ref.shape[1]
    i = pl.program_id(0)
    tall = rows + 2 * halo
    win = pl.ds(MARGIN, tall)
    top = pl.ds(MARGIN, halo)
    mid = pl.ds(MARGIN + halo, rows)
    bot = pl.ds(MARGIN + halo + rows, halo)
    rv = (rv_ref[0], rv_ref[1], rv_ref[2])

    @pl.when(i == 0)
    def _():
        acc = None
        for l in reversed(range(nlev)):
            part = (sall_ref[0, l], tall_ref[l], nall_ref[0, l])
            acc = part if acc is None else tuple(x + y for x, y in zip(acc, part))
            p_ref[l, top] = GRAV * acc[0]
            p_ref[l, mid] = GRAV * acc[1]
            p_ref[l, bot] = GRAV * acc[2]

    @pl.when(i < nlev)
    def _():
        lev = i
        for f in range(nf):
            sp_ref[f, top] = south_ref[f, 0]
            if f == 0:
                sp_ref[f, mid] = thk_ref[0]
            elif f < 3:
                sp_ref[f, mid] = wind_ref[f - 1, 0]
            else:
                sp_ref[f, mid] = trc_ref[f - 3, 0]
            sp_ref[f, bot] = north_ref[f, 0]

        def store(f, x):
            s1_ref[f, lev, win] = x

        _substep(
            lambda f, d: sp_ref[f, pl.ds(MARGIN + d, tall)],
            store,
            nf,
            lambda d: p_ref[lev, pl.ds(MARGIN + d, tall)],
            rv,
            mf_ref,
        )

    @pl.when(i == nlev)
    def _():
        acc = None
        for l in reversed(range(nlev)):
            acc = s1_ref[0, l, win] if acc is None else acc + s1_ref[0, l, win]
            p_ref[l, win] = GRAV * acc

    @pl.when(i >= nlev)
    def _():
        lev = i - nlev

        def store(f, x):
            x = x[halo : halo + rows]
            if f == 0:
                thk_o[0] = x
            elif f < 3:
                wind_o[f - 1, 0] = x
            else:
                trc_o[f - 3, 0] = x

        _substep(
            lambda f, d: s1_ref[f, lev, pl.ds(MARGIN + d, tall)],
            store,
            nf,
            lambda d: p_ref[lev, pl.ds(MARGIN + d, tall)],
            rv,
            mf_ref,
        )


def _final_kernel(
    e_ref, ew_ref, ee_ref, rv_ref, thk_i, wind_i, trc_i, thk_o, wind_o, trc_o, g0_ref, g1_ref, pg_ref, mf_ref
):
    nslab, nf, tall, w = e_ref.shape
    nlev, rows = thk_i.shape[0], thk_i.shape[1]
    per = w // GW
    rv = (rv_ref[0], rv_ref[1], rv_ref[2])
    lane, group, kk = _lanes(tall, w)
    win = pl.ds(MARGIN, tall)
    for s in range(nslab):
        for f in range(nf):
            g0_ref[s, f, win] = jnp.where(
                kk < HALO,
                _lroll(ew_ref[s, f], -4 * HALO),
                jnp.where(kk >= 5 * HALO, _lroll(ee_ref[s, f], 4 * HALO), e_ref[s, f]),
            )
    for src, dst in ((g0_ref, g1_ref), (g1_ref, g0_ref)):
        _packed_potential([src[s, 0, win] for s in range(nslab)], nlev, w, pg_ref, tall)
        for s in range(nslab):

            def store(f, x, s=s, dst=dst):
                dst[s, f, win] = x

            _substep(
                lambda f, d, s=s, src=src: src[s, f, pl.ds(MARGIN + d, tall)],
                store,
                nf,
                lambda d, s=s: pg_ref[s, pl.ds(MARGIN + d, tall)],
                rv,
                mf_ref,
            )
    lane_o = lane[:rows]
    inner = pl.ds(MARGIN + HALO, rows)
    for lev in range(nlev):
        s, g = _slab_of(lev, per)
        for f in range(nf):
            strip = g0_ref[s, f, inner]
            lo = _lroll(strip, -(GW * g + HALO))
            hi = _lroll(strip, (w - HALO) - (GW * g + 4 * HALO))
            if f == 0:
                src, dst = thk_i.at[lev], thk_o.at[lev]
            elif f < 3:
                src, dst = wind_i.at[f - 1, lev], wind_o.at[f - 1, lev]
            else:
                src, dst = trc_i.at[f - 3, lev], trc_o.at[f - 3, lev]
            dst[...] = jnp.where(lane_o < HALO, lo, jnp.where(lane_o >= w - HALO, hi, src[...]))


def _shift_pairs(n, d, closed):
    return [(i, (i + d) % n) for i in range(n) if closed or 0 <= i + d < n]


def _vmem_call(kernel, out_shape, n_in, scratch, flops, nbytes):
    vmem = pl.BlockSpec(memory_space=pltpu.VMEM)
    return pl.pallas_call(
        kernel,
        out_shape=out_shape,
        in_specs=[vmem] * n_in,
        out_specs=tuple(vmem for _ in out_shape) if isinstance(out_shape, tuple) else vmem,
        scratch_shapes=scratch,
        cost_estimate=pl.CostEstimate(flops=flops, bytes_accessed=nbytes, transcendentals=0),
    )


def shards(thickness, winds, tracer_mass):
    fields = jnp.concatenate([thickness[None], winds, tracer_mass], 0)
    nf, nlev, rows, w = fields.shape
    nlat = lax.axis_size("lat")
    nlon = lax.axis_size("lon")
    band = lax.axis_index("lat")
    spacing = math.pi / (rows * nlat)
    tall = rows + 2 * HALO
    deep = tall + 2 * MARGIN
    per = w // GW
    nslab = -(-nlev // per)

    row_index = (jnp.arange(tall) + (band * rows - HALO)).astype(jnp.float32)
    center_lat = (row_index + 0.5) * spacing - 0.5 * math.pi
    face_lat = (row_index + 1.0) * spacing - 0.5 * math.pi
    center_cos = jnp.cos(center_lat)
    rowvec = jnp.stack(
        [
            jnp.abs(jnp.cos(face_lat)),
            1.0 / jnp.abs(center_cos),
            COUR * FCOR * jnp.sin(center_lat) * jnp.where(center_cos >= 0.0, 1.0, -1.0),
        ]
    )
    rowvec = jnp.broadcast_to(rowvec[:, :, None], (3, tall, w))

    inner_edges = _vmem_call(
        _edge_inner_kernel, jax.ShapeDtypeStruct((nslab, nf, rows, w), jnp.float32), 3, [], 0, nf * nlev * rows * w * 4
    )(thickness, winds, tracer_mass)

    top = fields[:, :, rows - HALO :]
    bottom = fields[:, :, :HALO]
    from_south = lax.ppermute(top, "lat", _shift_pairs(nlat, 1, False))
    from_north = lax.ppermute(bottom, "lat", _shift_pairs(nlat, -1, False))
    half = nlon // 2
    pole_pairs = []
    for b in (0, nlat - 1):
        for s in range(nlon):
            pole_pairs.append((b * nlon + s, b * nlon + (s + half) % nlon))
    pole_out = jnp.where(band == 0, bottom, top)
    pole_in = lax.ppermute(pole_out, ("lat", "lon"), pole_pairs)
    sign = jnp.where(jnp.arange(nf) == 2, -1.0, 1.0).astype(jnp.float32)[:, None, None, None]
    mirrored = jnp.flip(pole_in, 2) * sign
    south = jnp.where(band == 0, mirrored, from_south)
    north = jnp.where(band == nlat - 1, mirrored, from_north)

    slab = nf * tall * w * 4
    edges = _vmem_call(
        _edge_kernel, jax.ShapeDtypeStruct((nslab, nf, tall, w), jnp.float32), 3, [], 0, 2 * slab * nslab
    )(south, inner_edges, north)
    from_west = lax.ppermute(edges, "lon", _shift_pairs(nlon, 1, True))
    from_east = lax.ppermute(edges, "lon", _shift_pairs(nlon, -1, True))

    step_flops = 60 * nf * nlev * tall * w
    first = lambda i: jnp.minimum(i, nlev - 1)
    second = lambda i: jnp.maximum(i - nlev, 0)
    raw = pl.pallas_call(
        _main_kernel,
        out_shape=(
            jax.ShapeDtypeStruct(thickness.shape, jnp.float32),
            jax.ShapeDtypeStruct(winds.shape, jnp.float32),
            jax.ShapeDtypeStruct(tracer_mass.shape, jnp.float32),
        ),
        grid=(2 * nlev,),
        in_specs=[
            pl.BlockSpec((nf, 1, HALO, w), lambda i: (0, first(i), 0, 0)),
            pl.BlockSpec((1, rows, w), lambda i: (first(i), 0, 0)),
            pl.BlockSpec((2, 1, rows, w), lambda i: (0, first(i), 0, 0)),
            pl.BlockSpec((nf - 3, 1, rows, w), lambda i: (0, first(i), 0, 0)),
            pl.BlockSpec((nf, 1, HALO, w), lambda i: (0, first(i), 0, 0)),
            pl.BlockSpec((nlev, rows, w), lambda i: (0, 0, 0)),
            pl.BlockSpec((1, nlev, HALO, w), lambda i: (0, 0, 0, 0)),
            pl.BlockSpec((1, nlev, HALO, w), lambda i: (0, 0, 0, 0)),
            pl.BlockSpec((3, tall, w), lambda i: (0, 0, 0)),
        ],
        out_specs=(
            pl.BlockSpec((1, rows, w), lambda i: (second(i), 0, 0)),
            pl.BlockSpec((2, 1, rows, w), lambda i: (0, second(i), 0, 0)),
            pl.BlockSpec((nf - 3, 1, rows, w), lambda i: (0, second(i), 0, 0)),
        ),
        scratch_shapes=[
            pltpu.VMEM((nlev, deep, w), jnp.float32),
            pltpu.VMEM((nf, deep, w), jnp.float32),
            pltpu.VMEM((nf, deep, w), jnp.float32),
            pltpu.VMEM((nf, nlev, deep, w), jnp.float32),
        ],
        compiler_params=pltpu.CompilerParams(dimension_semantics=("arbitrary",)),
        cost_estimate=pl.CostEstimate(flops=2 * step_flops, bytes_accessed=2 * slab * nlev, transcendentals=0),
    )(south, thickness, winds, tracer_mass, north, thickness, south, north, rowvec)

    return _vmem_call(
        _final_kernel,
        (
            jax.ShapeDtypeStruct(thickness.shape, jnp.float32),
            jax.ShapeDtypeStruct(winds.shape, jnp.float32),
            jax.ShapeDtypeStruct(tracer_mass.shape, jnp.float32),
        ),
        7,
        [
            pltpu.VMEM((nslab, nf, deep, w), jnp.float32),
            pltpu.VMEM((nslab, nf, deep, w), jnp.float32),
            pltpu.VMEM((nslab, deep, w), jnp.float32),
            pltpu.VMEM((nf, deep, w), jnp.float32),
        ],
        4 * step_flops // nlev,
        4 * slab * nslab,
    )(edges, from_west, from_east, rowvec, *raw)


def solution(mesh):
    return jax.shard_map(
        shards,
        mesh=mesh,
        in_specs=(P(None, "lat", "lon"), P(None, None, "lat", "lon"), P(None, None, "lat", "lon")),
        out_specs=(P(None, "lat", "lon"), P(None, None, "lat", "lon"), P(None, None, "lat", "lon")),
        check_vma=False,
    )
```

time: 57.2 us -> 52.7 us (0.921)
  the two profiles are of different devices: /device:TPU:6 before, /device:TPU:16 now
where the time goes in v7:
time: 52.7 us; the launch traced here: 52.3 us
  Pallas kernels  28.4 us (54%)
  starting transfers between devices  12.8 us (24%)
  waiting for transfers between devices  6.45 us (12%)
  other arithmetic  2.16 us (4%)
  local copies, waits for them, and re-layouts  1.82 us (3%)
  between operations  0.73 us (1%)
    pallas_call x1, Pallas kernels, shards(): pl.pallas_call(_main_kernel, out_shape=(jax.ShapeDtypeStruct(thickness.sh...  14.9 us
    pallas_call x1, Pallas kernels, shards(): _vmem_call(_final_kernel, (jax.ShapeDtypeStruct(thickness.shape, jnp.floa...  8.23 us
    ppermute x1, waiting for transfers between devices, shards(): from_south = lax.ppermute(top, 'lat', _shift_pairs(nlat, 1, False))  6.44 us
    ppermute x1, starting transfers between devices, shards(): from_east = lax.ppermute(edges, 'lon', _shift_pairs(nlon, -1, True))  5.72 us
    ppermute x1, starting transfers between devices, shards(): from_north = lax.ppermute(bottom, 'lat', _shift_pairs(nlat, -1, False))  4.44 us
    pallas_call x1, Pallas kernels, shards(): _vmem_call(_edge_inner_kernel, jax.ShapeDtypeStruct((nslab, nf, rows, w),...  2.92 us
    pallas_call x1, Pallas kernels, shards(): _vmem_call(_edge_kernel, jax.ShapeDtypeStruct((nslab, nf, tall, w), jnp.f...  2.34 us
    ppermute x1, starting transfers between devices, shards(): from_south = lax.ppermute(top, 'lat', _shift_pairs(nlat, 1, False))  1.92 us
  transfers between devices with their start and end apart: 5, of which 1 were waited for; matrix products, arithmetic and copies ran while one was open for 2% of the time, Pallas kernels for 34%

profile of v7, /device:TPU:16, one launch (start us, length us, event | category | flops | bytes accessed | tf_op | source)
XLA Modules:
  0.0 52.3 jit_solution(3418154963384044216)
XLA Ops:
  0.6 1.2 %broadcast_select_fusion = (f32[11,8,4,128]{3,2,1,0:T(4,128)S(1)}, f32[11,8,4,128]{3,2,1,0:T(4,128)S(1)}, f32[11,8,4,128]{3,2,1,0:T(4,128)S(1)}) fusion(pred[]{:T(512)S(6)} %eq.14, f32[8,8,32,128]{3,2,1,0:T(8,128)} %trc_ref.3, f32[2,8,32,128]{3,2,1,0:T(8,128)} %wind_ref.3, f32[1,8,32,128]{3,2,1,0:T(8,128)} %bitcast.1), kind=kLoop, calls=%fused_computation.5 | loop fusion | flops 225280 | bytes 1982465 | tf_op jit(solution)/shard_map/jit(_where)/select_n | solution.py:306
  1.8 0.7 %collective-permute-start = (f32[11,8,4,128]{3,2,1,0:T(4,128)S(1)}, f32[11,8,4,128]{3,2,1,0:T(4,128)S(1)}, u32[]{:S(2)}, u32[]{:S(2)}) collective-permute-start(f32[11,8,4,128]{3,2,1,0:T(4,128)S(1)} %get-tuple-element.9), channel_id=1, source_target_pairs={{0,16},{1,17},{2,18},{3,19},{4,20},{5,21},{6,22},{7,23},{8,24},{9,... | collective-permute-start | bytes 540680 | tf_op jit(solution)/shard_map/ppermute | solution.py:307
  2.5 4.4 %collective-permute-start.2 = (f32[11,8,4,128]{3,2,1,0:T(4,128)S(1)}, f32[11,8,4,128]{3,2,1,0:T(4,128)S(1)}, u32[]{:S(2)}, u32[]{:S(2)}) collective-permute-start(f32[11,8,4,128]{3,2,1,0:T(4,128)S(1)} %get-tuple-element.10), channel_id=1, source_target_pairs={{32,0},{64,32},{96,64},{128,96},{160,128},{192,160},{224,192},{33,... | collective-permute-start | bytes 540680 | tf_op jit(solution)/shard_map/ppermute | solution.py:300
  6.9 1.9 %collective-permute-start.1 = (f32[11,8,4,128]{3,2,1,0:T(4,128)S(1)}, f32[11,8,4,128]{3,2,1,0:T(4,128)S(1)}, u32[]{:S(2)}, u32[]{:S(2)}) collective-permute-start(f32[11,8,4,128]{3,2,1,0:T(4,128)S(1)} %get-tuple-element.11), channel_id=1, source_target_pairs={{0,32},{32,64},{64,96},{96,128},{128,160},{160,192},{192,224},{1,3... | collective-permute-start | bytes 540680 | tf_op jit(solution)/shard_map/ppermute | solution.py:299
  8.9 2.9 %shard_map.58.inner_ref = f32[2,11,32,128]{3,2,1,0:T(8,128)} custom-call(f32[8,32,128]{2,1,0:T(8,128)} %tall_ref.1, f32[2,8,32,128]{3,2,1,0:T(8,128)} %wind_ref.3, f32[8,8,32,128]{3,2,1,0:T(8,128)} %trc_ref.3), custom_call_target="tpu_custom_call" | custom-call | bytes 1441792 | tf_op jit(solution)/shard_map/pallas_call | solution.py:293
  11.8 0.0 collective-permute-done
  11.8 0.2 rev.4
  12.0 0.0 collective-permute-done.2
  12.0 6.4 %collective-permute-done.1 = f32[11,8,4,128]{3,2,1,0:T(4,128)S(1)} collective-permute-done((f32[11,8,4,128]{3,2,1,0:T(4,128)S(1)}, f32[11,8,4,128]{3,2,1,0:T(4,128)S(1)}, u32[]{:S(2)}, u32[]{:S(2)}) %collective-permute-start.1) | collective-permute-done | bytes 180256 | tf_op jit(solution)/shard_map/ppermute | solution.py:299
  18.4 0.9 %multiply_select_fusion = (f32[11,8,4,128]{3,2,1,0:T(4,128)}, f32[11,8,4,128]{3,2,1,0:T(4,128)}) fusion(f32[11,8,4,128]{3,2,1,0:T(4,128)S(1)} %collective-permute-done.2, f32[11,8,4,128]{3,2,1,0:T(4,128)S(1)} %rev.4, f32[11]{0:T(128)S(1)} %compare_select_fusion.1, pred[]{:T(512)S(6)} %eq.16, f32[11,8,4,128]{3,2,1,0:T(4,128)S(1)} %collective-permute-done.1, ...), kind=kLoop, calls=%fused_computation.3 | loop fusion | flops 135168 | bytes 901166 | tf_op jit(solution)/shard_map/jit(_where)/select_n | solution.py:311
  19.3 2.3 %shard_map.59.e_ref = f32[2,11,40,128]{3,2,1,0:T(8,128)} custom-call(f32[11,8,4,128]{3,2,1,0:T(4,128)} %get-tuple-element.13.south_ref.sall_ref, f32[2,11,32,128]{3,2,1,0:T(8,128)} %shard_map.58.inner_ref, f32[11,8,4,128]{3,2,1,0:T(4,128)} %get-tuple-element.12.north_ref.nall_ref), custom_call_target="tpu_custom_call" | custom-call | bytes 901120 | tf_op jit(solution)/shard_map/pallas_call | solution.py:314
  21.7 5.7 %collective-permute-start.4 = (f32[2,11,40,128]{3,2,1,0:T(8,128)}, f32[2,11,40,128]{3,2,1,0:T(8,128)S(1)}, u32[]{:S(2)}, u32[]{:S(2)}) collective-permute-start(f32[2,11,40,128]{3,2,1,0:T(8,128)} %shard_map.59.e_ref), channel_id=1, source_target_pairs={{0,31},{1,0},{2,1},{3,2},{4,3},{5,4},{6,5},{7,6},{8,7},{9,8},{10,9... | collective-permute-start | bytes 1351688 | tf_op jit(solution)/shard_map/ppermute | solution.py:318
  27.4 0.0 collective-permute-start.3
  27.4 0.1 fusion
  27.5 0.7 %broadcast_in_dim.28.rv_ref = f32[3,40,128]{2,1,0:T(8,128)} broadcast(f32[3,40]{1,0:T(4,128)S(1)} %pad_maximum_fusion.3), dimensions={0,1} | broadcast | bytes 61920 | tf_op jit(solution)/shard_map/broadcast_in_dim | solution.py:291
  28.2 14.9 %shard_map.60 = (f32[8,32,128]{2,1,0:T(8,128)}, f32[2,8,32,128]{3,2,1,0:T(8,128)}, f32[8,8,32,128]{3,2,1,0:T(8,128)}) custom-call(f32[11,8,4,128]{3,2,1,0:T(4,128)} %get-tuple-element.13.south_ref.sall_ref, f32[8,32,128]{2,1,0:T(8,128)} %tall_ref.1, f32[2,8,32,128]{3,2,1,0:T(8,128)} %wind_ref.3, f32[8,8,32,128]{3,2,1,0:T(8,128)} %trc_ref.3, ...), custom_call_target="tpu_custom_call" | custom-call | flops 54067200 | bytes 3604480 | tf_op jit(solution)/shard_map/pallas_call | solution.py:323
  43.1 0.0 collective-permute-done.4.ee_ref
  43.2 0.0 copy-start
  43.2 0.0 collective-permute-done.3.ew_ref
  43.2 0.0 copy-start.1
  43.2 0.7 %copy-done = f32[2,11,40,128]{3,2,1,0:T(8,128)} copy-done((f32[2,11,40,128]{3,2,1,0:T(8,128)}, f32[2,11,40,128]{3,2,1,0:T(8,128)S(1)}, u32[]{:S(2)}) %copy-start) | copy-done | bytes 450584
  43.9 0.2 copy-done.1
  44.1 8.2 %shard_map.61 = (f32[8,32,128]{2,1,0:T(8,128)}, f32[2,8,32,128]{3,2,1,0:T(8,128)}, f32[8,8,32,128]{3,2,1,0:T(8,128)}) custom-call(f32[2,11,40,128]{3,2,1,0:T(8,128)} %shard_map.59.e_ref, f32[2,11,40,128]{3,2,1,0:T(8,128)} %copy-done.1, f32[2,11,40,128]{3,2,1,0:T(8,128)} %copy-done, f32[3,40,128]{2,1,0:T(8,128)} %broadcast_in_dim.28.rv_ref, ...), custom_call_target="tpu_custom_call" | custom-call | flops 13516800 | bytes 1802240 | tf_op jit(solution)/shard_map/pallas_call | solution.py:357
  (3 shorter events, 0.1 us)
Async XLA Ops:
  1.8 10.0 %collective-permute-start = (f32[11,8,4,128]{3,2,1,0:T(4,128)S(1)}, f32[11,8,4,128]{3,2,1,0:T(4,128)S(1)}, u32[]{:S(2)}, u32[]{:S(2)}) collective-permute-start(f32[11,8,4,128]{3,2,1,0:T(4,128)S(1)} %get-tuple-element.9), channel_id=1, source_target_pairs={{0,16},{1,17},{2,18},{3,19},{4,20},{5,21},{6,22},{7,23},{8,24},{9,... | collective-permute-start | bytes 540680 | tf_op jit(solution)/shard_map/ppermute | solution.py:307
  2.5 9.5 %collective-permute-start.2 = (f32[11,8,4,128]{3,2,1,0:T(4,128)S(1)}, f32[11,8,4,128]{3,2,1,0:T(4,128)S(1)}, u32[]{:S(2)}, u32[]{:S(2)}) collective-permute-start(f32[11,8,4,128]{3,2,1,0:T(4,128)S(1)} %get-tuple-element.10), channel_id=1, source_target_pairs={{32,0},{64,32},{96,64},{128,96},{160,128},{192,160},{224,192},{33,... | collective-permute-start | bytes 540680 | tf_op jit(solution)/shard_map/ppermute | solution.py:300
  6.9 11.5 %collective-permute-start.1 = (f32[11,8,4,128]{3,2,1,0:T(4,128)S(1)}, f32[11,8,4,128]{3,2,1,0:T(4,128)S(1)}, u32[]{:S(2)}, u32[]{:S(2)}) collective-permute-start(f32[11,8,4,128]{3,2,1,0:T(4,128)S(1)} %get-tuple-element.11), channel_id=1, source_target_pairs={{0,32},{32,64},{64,96},{96,128},{128,160},{160,192},{192,224},{1,3... | collective-permute-start | bytes 540680 | tf_op jit(solution)/shard_map/ppermute | solution.py:299
  21.7 21.5 %collective-permute-start.4 = (f32[2,11,40,128]{3,2,1,0:T(8,128)}, f32[2,11,40,128]{3,2,1,0:T(8,128)S(1)}, u32[]{:S(2)}, u32[]{:S(2)}) collective-permute-start(f32[2,11,40,128]{3,2,1,0:T(8,128)} %shard_map.59.e_ref), channel_id=1, source_target_pairs={{0,31},{1,0},{2,1},{3,2},{4,3},{5,4},{6,5},{7,6},{8,7},{9,8},{10,9... | collective-permute-start | bytes 1351688 | tf_op jit(solution)/shard_map/ppermute | solution.py:318
  27.4 15.8 %collective-permute-start.3 = (f32[2,11,40,128]{3,2,1,0:T(8,128)}, f32[2,11,40,128]{3,2,1,0:T(8,128)S(1)}, u32[]{:S(2)}, u32[]{:S(2)}) collective-permute-start(f32[2,11,40,128]{3,2,1,0:T(8,128)} %shard_map.59.e_ref), channel_id=1, source_target_pairs={{0,1},{1,2},{2,3},{3,4},{4,5},{5,6},{6,7},{7,8},{8,9},{9,10},{10,1... | collective-permute-start | bytes 1351688 | tf_op jit(solution)/shard_map/ppermute | solution.py:317
  43.2 0.8 %copy-start = (f32[2,11,40,128]{3,2,1,0:T(8,128)}, f32[2,11,40,128]{3,2,1,0:T(8,128)S(1)}, u32[]{:S(2)}) copy-start(f32[2,11,40,128]{3,2,1,0:T(8,128)S(1)} %collective-permute-done.4.ee_ref) | copy-start | bytes 1351684
  43.2 0.9 %copy-start.1 = (f32[2,11,40,128]{3,2,1,0:T(8,128)}, f32[2,11,40,128]{3,2,1,0:T(8,128)S(1)}, u32[]{:S(2)}) copy-start(f32[2,11,40,128]{3,2,1,0:T(8,128)S(1)} %collective-permute-done.3.ew_ref) | copy-start | bytes 1351684

commit v8 on v7

--- a/solution.py
+++ b/solution.py
@@ -96,7 +96,8 @@
         below = jnp.where(group == 0, acc, 0.0)
 
 
-def _edge_inner_kernel(thk_ref, wind_ref, trc_ref, e_ref):
+def _edge_inner_kernel(thk_ref, wind_ref, trc_ref, rvi_ref, e_ref, rv_ref):
+    rv_ref[...] = rvi_ref[...]
     nlev, rows, w = thk_ref.shape
     nslab, nf = e_ref.shape[0], e_ref.shape[1]
     zeros = jnp.zeros((rows, w), jnp.float32)
@@ -202,10 +203,21 @@
 
 
 def _final_kernel(
-    e_ref, ew_ref, ee_ref, rv_ref, thk_i, wind_i, trc_i, thk_o, wind_o, trc_o, g0_ref, g1_ref, pg_ref, mf_ref
+    e_ref, ew_ref, ee_ref, rv_ref, thk_i, wind_i, trc_i, thk_o, wind_o, trc_o, g0_ref, g1_ref, pg_ref, mf_ref,
+    buf_ref, in_sem, out_sem,
 ):
     nslab, nf, tall, w = e_ref.shape
     nlev, rows = thk_i.shape[0], thk_i.shape[1]
+
+    def hbm(refs, f, lev):
+        t, wd, tr = refs
+        return t.at[lev] if f == 0 else (wd.at[f - 1, lev] if f < 3 else tr.at[f - 3, lev])
+
+    ins = {}
+    for lev in range(nlev):
+        for f in range(nf):
+            ins[lev, f] = pltpu.make_async_copy(hbm((thk_i, wind_i, trc_i), f, lev), buf_ref.at[lev, f], in_sem.at[lev, f])
+            ins[lev, f].start()
     per = w // GW
     rv = (rv_ref[0], rv_ref[1], rv_ref[2])
     lane, group, kk = _lanes(tall, w)
@@ -234,19 +246,19 @@
             )
     lane_o = lane[:rows]
     inner = pl.ds(MARGIN + HALO, rows)
+    outs = []
     for lev in range(nlev):
         s, g = _slab_of(lev, per)
         for f in range(nf):
             strip = g0_ref[s, f, inner]
             lo = _lroll(strip, -(GW * g + HALO))
             hi = _lroll(strip, (w - HALO) - (GW * g + 4 * HALO))
-            if f == 0:
-                src, dst = thk_i.at[lev], thk_o.at[lev]
-            elif f < 3:
-                src, dst = wind_i.at[f - 1, lev], wind_o.at[f - 1, lev]
-            else:
-                src, dst = trc_i.at[f - 3, lev], trc_o.at[f - 3, lev]
-            dst[...] = jnp.where(lane_o < HALO, lo, jnp.where(lane_o >= w - HALO, hi, src[...]))
+            ins[lev, f].wait()
+            buf_ref[lev, f] = jnp.where(lane_o < HALO, lo, jnp.where(lane_o >= w - HALO, hi, buf_ref[lev, f]))
+            outs.append(pltpu.make_async_copy(buf_ref.at[lev, f], hbm((thk_o, wind_o, trc_o), f, lev), out_sem.at[lev, f]))
+            outs[-1].start()
+    for c in outs:
+        c.wait()
 
 
 def _shift_pairs(n, d, closed):
@@ -290,9 +302,14 @@
     )
     rowvec = jnp.broadcast_to(rowvec[:, :, None], (3, tall, w))
 
-    inner_edges = _vmem_call(
-        _edge_inner_kernel, jax.ShapeDtypeStruct((nslab, nf, rows, w), jnp.float32), 3, [], 0, nf * nlev * rows * w * 4
-    )(thickness, winds, tracer_mass)
+    inner_edges, rowvec = _vmem_call(
+        _edge_inner_kernel,
+        (jax.ShapeDtypeStruct((nslab, nf, rows, w), jnp.float32), jax.ShapeDtypeStruct(rowvec.shape, jnp.float32)),
+        4,
+        [],
+        0,
+        nf * nlev * rows * w * 4,
+    )(thickness, winds, tracer_mass, rowvec)
 
     top = fields[:, :, rows - HALO :]
     bottom = fields[:, :, :HALO]
@@ -354,22 +371,28 @@
         cost_estimate=pl.CostEstimate(flops=2 * step_flops, bytes_accessed=2 * slab * nlev, transcendentals=0),
     )(south, thickness, winds, tracer_mass, north, thickness, south, north, rowvec)
 
-    return _vmem_call(
+    vmem = pl.BlockSpec(memory_space=pltpu.VMEM)
+    anywhere = pl.BlockSpec(memory_space=pl.ANY)
+    return pl.pallas_call(
         _final_kernel,
-        (
+        out_shape=(
             jax.ShapeDtypeStruct(thickness.shape, jnp.float32),
             jax.ShapeDtypeStruct(winds.shape, jnp.float32),
             jax.ShapeDtypeStruct(tracer_mass.shape, jnp.float32),
         ),
-        7,
-        [
+        in_specs=[vmem] * 4 + [anywhere] * 3,
+        out_specs=(anywhere, anywhere, anywhere),
+        input_output_aliases={4: 0, 5: 1, 6: 2},
+        scratch_shapes=[
             pltpu.VMEM((nslab, nf, deep, w), jnp.float32),
             pltpu.VMEM((nslab, nf, deep, w), jnp.float32),
             pltpu.VMEM((nslab, deep, w), jnp.float32),
             pltpu.VMEM((nf, deep, w), jnp.float32),
+            pltpu.VMEM((nlev, nf, rows, w), jnp.float32),
+            pltpu.SemaphoreType.DMA((nlev, nf)),
+            pltpu.SemaphoreType.DMA((nlev, nf)),
         ],
-        4 * step_flops // nlev,
-        4 * slab * nslab,
+        cost_estimate=pl.CostEstimate(flops=4 * step_flops // nlev, bytes_accessed=4 * slab * nslab, transcendentals=0),
     )(edges, from_west, from_east, rowvec, *raw)
 
 

time: 52.7 us -> 58.5 us (1.11)
  Pallas kernels: 28.4 us -> 35 us
  waiting for transfers between devices: 6.45 us -> 5.6 us
    pallas_call x2, Pallas kernels: 11.2 us -> 17.8 us  [the longest x1 14.8 us: shards(): pl.pallas_call(_final_kernel, out_shape=(jax.ShapeDtypeStruct(thickness.s...]
    ppermute x1, waiting for transfers between devices: 6.44 us -> 5.59 us  [shards(): from_south = lax.ppermute(top, 'lat', _shift_pairs(nlat, 1, False))]
  transfers between devices with their start and end apart: 5 -> 5, of which waited for: 1 -> 1; matrix products, arithmetic and copies ran while one was open for 2% -> 2% of each run, Pallas kernels for 34% -> 31%
where the time goes in v8:
time: 58.5 us; the launch traced here: 58.1 us
  Pallas kernels  35 us (60%)
  starting transfers between devices  12.8 us (22%)
  waiting for transfers between devices  5.6 us (10%)
  other arithmetic  2.15 us (4%)
  local copies, waits for them, and re-layouts  1.84 us (3%)
  between operations  0.74 us (1%)
    pallas_call x1, Pallas kernels, shards(): pl.pallas_call(_main_kernel, out_shape=(jax.ShapeDtypeStruct(thickness.sh...  14.9 us
    pallas_call x1, Pallas kernels, shards(): pl.pallas_call(_final_kernel, out_shape=(jax.ShapeDtypeStruct(thickness.s...  14.8 us
    ppermute x1, starting transfers between devices, shards(): from_east = lax.ppermute(edges, 'lon', _shift_pairs(nlon, -1, True))  5.72 us
    ppermute x1, waiting for transfers between devices, shards(): from_south = lax.ppermute(top, 'lat', _shift_pairs(nlat, 1, False))  5.59 us
    ppermute x1, starting transfers between devices, shards(): from_north = lax.ppermute(bottom, 'lat', _shift_pairs(nlat, -1, False))  4.44 us
    pallas_call x1, Pallas kernels, shards(): _vmem_call(_edge_inner_kernel, (jax.ShapeDtypeStruct((nslab, nf, rows, w)...  2.92 us
    pallas_call x1, Pallas kernels, shards(): _vmem_call(_edge_kernel, jax.ShapeDtypeStruct((nslab, nf, tall, w), jnp.f...  2.32 us
    ppermute x1, starting transfers between devices, shards(): from_south = lax.ppermute(top, 'lat', _shift_pairs(nlat, 1, False))  1.92 us
  transfers between devices with their start and end apart: 5, of which 1 were waited for; matrix products, arithmetic and copies ran while one was open for 2% of the time, Pallas kernels for 31%

profile of v8, /device:TPU:16, one launch (start us, length us, event | category | flops | bytes accessed | tf_op | source)
XLA Modules:
  0.0 58.1 jit_solution(10726059727624882799)
XLA Ops:
  0.6 1.2 %broadcast_select_fusion = (f32[11,8,4,128]{3,2,1,0:T(4,128)S(1)}, f32[11,8,4,128]{3,2,1,0:T(4,128)S(1)}, f32[11,8,4,128]{3,2,1,0:T(4,128)S(1)}) fusion(pred[]{:T(512)S(6)} %eq.14, f32[8,8,32,128]{3,2,1,0:T(8,128)} %trc_ref.3, f32[2,8,32,128]{3,2,1,0:T(8,128)} %wind_ref.3, f32[1,8,32,128]{3,2,1,0:T(8,128)} %bitcast.1), kind=kLoop, calls=%fused_computation.5 | loop fusion | flops 225280 | bytes 1982465 | tf_op jit(solution)/shard_map/jit(_where)/select_n | solution.py:323
  1.8 0.7 %collective-permute-start = (f32[11,8,4,128]{3,2,1,0:T(4,128)S(1)}, f32[11,8,4,128]{3,2,1,0:T(4,128)S(1)}, u32[]{:S(2)}, u32[]{:S(2)}) collective-permute-start(f32[11,8,4,128]{3,2,1,0:T(4,128)S(1)} %get-tuple-element.13), channel_id=1, source_target_pairs={{0,16},{1,17},{2,18},{3,19},{4,20},{5,21},{6,22},{7,23},{8,24},{9,... | collective-permute-start | bytes 540680 | tf_op jit(solution)/shard_map/ppermute | solution.py:324
  2.5 4.4 %collective-permute-start.2 = (f32[11,8,4,128]{3,2,1,0:T(4,128)S(1)}, f32[11,8,4,128]{3,2,1,0:T(4,128)S(1)}, u32[]{:S(2)}, u32[]{:S(2)}) collective-permute-start(f32[11,8,4,128]{3,2,1,0:T(4,128)S(1)} %get-tuple-element.14), channel_id=1, source_target_pairs={{32,0},{64,32},{96,64},{128,96},{160,128},{192,160},{224,192},{33,... | collective-permute-start | bytes 540680 | tf_op jit(solution)/shard_map/ppermute | solution.py:317
  6.9 1.9 %collective-permute-start.1 = (f32[11,8,4,128]{3,2,1,0:T(4,128)S(1)}, f32[11,8,4,128]{3,2,1,0:T(4,128)S(1)}, u32[]{:S(2)}, u32[]{:S(2)}) collective-permute-start(f32[11,8,4,128]{3,2,1,0:T(4,128)S(1)} %get-tuple-element.15), channel_id=1, source_target_pairs={{0,32},{32,64},{64,96},{96,128},{128,160},{160,192},{192,224},{1,3... | collective-permute-start | bytes 540680 | tf_op jit(solution)/shard_map/ppermute | solution.py:316
  8.9 0.1 fusion
  9.0 0.7 %broadcast_in_dim.28.rvi_ref = f32[3,40,128]{2,1,0:T(8,128)} broadcast(f32[3,40]{1,0:T(4,128)S(1)} %pad_maximum_fusion.3), dimensions={0,1} | broadcast | bytes 61920 | tf_op jit(solution)/shard_map/broadcast_in_dim | solution.py:303
  9.7 2.9 %shard_map.58 = (f32[2,11,32,128]{3,2,1,0:T(8,128)}, f32[3,40,128]{2,1,0:T(8,128)}) custom-call(f32[8,32,128]{2,1,0:T(8,128)} %tall_ref.1, f32[2,8,32,128]{3,2,1,0:T(8,128)} %wind_ref.3, f32[8,8,32,128]{3,2,1,0:T(8,128)} %trc_ref.3, f32[3,40,128]{2,1,0:T(8,128)} %broadcast_in_dim.28.rvi_ref), custom_call_target="tpu_custom_call" | custom-call | bytes 1441792 | tf_op jit(solution)/shard_map/pallas_call | solution.py:305
  12.6 0.0 collective-permute-done
  12.6 0.2 rev.4
  12.8 0.0 collective-permute-done.2
  12.9 5.6 %collective-permute-done.1 = f32[11,8,4,128]{3,2,1,0:T(4,128)S(1)} collective-permute-done((f32[11,8,4,128]{3,2,1,0:T(4,128)S(1)}, f32[11,8,4,128]{3,2,1,0:T(4,128)S(1)}, u32[]{:S(2)}, u32[]{:S(2)}) %collective-permute-start.1) | collective-permute-done | bytes 180256 | tf_op jit(solution)/shard_map/ppermute | solution.py:316
  18.4 0.9 %multiply_select_fusion = (f32[11,8,4,128]{3,2,1,0:T(4,128)}, f32[11,8,4,128]{3,2,1,0:T(4,128)}) fusion(f32[11,8,4,128]{3,2,1,0:T(4,128)S(1)} %collective-permute-done.2, f32[11,8,4,128]{3,2,1,0:T(4,128)S(1)} %rev.4, f32[11]{0:T(128)S(1)} %compare_select_fusion.1, pred[]{:T(512)S(6)} %eq.16, f32[11,8,4,128]{3,2,1,0:T(4,128)S(1)} %collective-permute-done.1, ...), kind=kLoop, calls=%fused_computation.3 | loop fusion | flops 135168 | bytes 901166 | tf_op jit(solution)/shard_map/jit(_where)/select_n | solution.py:328
  19.3 2.3 %shard_map.59.e_ref = f32[2,11,40,128]{3,2,1,0:T(8,128)} custom-call(f32[11,8,4,128]{3,2,1,0:T(4,128)} %get-tuple-element.17.south_ref.sall_ref, f32[2,11,32,128]{3,2,1,0:T(8,128)} %get-tuple-element.8.inner_ref, f32[11,8,4,128]{3,2,1,0:T(4,128)} %get-tuple-element.16.north_ref.nall_ref), custom_call_target="tpu_custom_call" | custom-call | bytes 901120 | tf_op jit(solution)/shard_map/pallas_call | solution.py:331
  21.6 5.7 %collective-permute-start.4 = (f32[2,11,40,128]{3,2,1,0:T(8,128)}, f32[2,11,40,128]{3,2,1,0:T(8,128)S(1)}, u32[]{:S(2)}, u32[]{:S(2)}) collective-permute-start(f32[2,11,40,128]{3,2,1,0:T(8,128)} %shard_map.59.e_ref), channel_id=1, source_target_pairs={{0,31},{1,0},{2,1},{3,2},{4,3},{5,4},{6,5},{7,6},{8,7},{9,8},{10,9... | collective-permute-start | bytes 1351688 | tf_op jit(solution)/shard_map/ppermute | solution.py:335
  27.4 0.0 collective-permute-start.3
  27.4 14.9 %shard_map.60 = (f32[8,32,128]{2,1,0:T(8,128)}, f32[2,8,32,128]{3,2,1,0:T(8,128)}, f32[8,8,32,128]{3,2,1,0:T(8,128)}) custom-call(f32[11,8,4,128]{3,2,1,0:T(4,128)} %get-tuple-element.17.south_ref.sall_ref, f32[8,32,128]{2,1,0:T(8,128)} %tall_ref.1, f32[2,8,32,128]{3,2,1,0:T(8,128)} %wind_ref.3, f32[8,8,32,128]{3,2,1,0:T(8,128)} %trc_ref.3, ...), custom_call_target="tpu_custom_call" | custom-call | flops 54067200 | bytes 3604480 | tf_op jit(solution)/shard_map/pallas_call | solution.py:340
  42.3 0.0 collective-permute-done.4.ee_ref
  42.3 0.0 copy-start
  42.3 0.0 collective-permute-done.3.ew_ref
  42.3 0.0 copy-start.1
  42.3 0.7 %copy-done = f32[2,11,40,128]{3,2,1,0:T(8,128)} copy-done((f32[2,11,40,128]{3,2,1,0:T(8,128)}, f32[2,11,40,128]{3,2,1,0:T(8,128)S(1)}, u32[]{:S(2)}) %copy-start) | copy-done | bytes 450584
  43.1 0.2 copy-done.1
  43.2 14.8 %shard_map.61 = (f32[8,32,128]{2,1,0:T(8,128)}, f32[2,8,32,128]{3,2,1,0:T(8,128)}, f32[8,8,32,128]{3,2,1,0:T(8,128)}) custom-call(f32[2,11,40,128]{3,2,1,0:T(8,128)} %shard_map.59.e_ref, f32[2,11,40,128]{3,2,1,0:T(8,128)} %copy-done.1, f32[2,11,40,128]{3,2,1,0:T(8,128)} %copy-done, ...), custom_call_target="tpu_custom_call", output_to_operand_aliasing={{0}: (4, {}), {1}: (5, {}), {2}: (6, {})} | custom-call | flops 13516800 | bytes 1802240 | tf_op jit(solution)/shard_map/pallas_call | solution.py:376
  (3 shorter events, 0.1 us)
Async XLA Ops:
  1.8 10.8 %collective-permute-start = (f32[11,8,4,128]{3,2,1,0:T(4,128)S(1)}, f32[11,8,4,128]{3,2,1,0:T(4,128)S(1)}, u32[]{:S(2)}, u32[]{:S(2)}) collective-permute-start(f32[11,8,4,128]{3,2,1,0:T(4,128)S(1)} %get-tuple-element.13), channel_id=1, source_target_pairs={{0,16},{1,17},{2,18},{3,19},{4,20},{5,21},{6,22},{7,23},{8,24},{9,... | collective-permute-start | bytes 540680 | tf_op jit(solution)/shard_map/ppermute | solution.py:324
  2.5 10.4 %collective-permute-start.2 = (f32[11,8,4,128]{3,2,1,0:T(4,128)S(1)}, f32[11,8,4,128]{3,2,1,0:T(4,128)S(1)}, u32[]{:S(2)}, u32[]{:S(2)}) collective-permute-start(f32[11,8,4,128]{3,2,1,0:T(4,128)S(1)} %get-tuple-element.14), channel_id=1, source_target_pairs={{32,0},{64,32},{96,64},{128,96},{160,128},{192,160},{224,192},{33,... | collective-permute-start | bytes 540680 | tf_op jit(solution)/shard_map/ppermute | solution.py:317
  6.9 11.5 %collective-permute-start.1 = (f32[11,8,4,128]{3,2,1,0:T(4,128)S(1)}, f32[11,8,4,128]{3,2,1,0:T(4,128)S(1)}, u32[]{:S(2)}, u32[]{:S(2)}) collective-permute-start(f32[11,8,4,128]{3,2,1,0:T(4,128)S(1)} %get-tuple-element.15), channel_id=1, source_target_pairs={{0,32},{32,64},{64,96},{96,128},{128,160},{160,192},{192,224},{1,3... | collective-permute-start | bytes 540680 | tf_op jit(solution)/shard_map/ppermute | solution.py:316
  21.6 20.7 %collective-permute-start.4 = (f32[2,11,40,128]{3,2,1,0:T(8,128)}, f32[2,11,40,128]{3,2,1,0:T(8,128)S(1)}, u32[]{:S(2)}, u32[]{:S(2)}) collective-permute-start(f32[2,11,40,128]{3,2,1,0:T(8,128)} %shard_map.59.e_ref), channel_id=1, source_target_pairs={{0,31},{1,0},{2,1},{3,2},{4,3},{5,4},{6,5},{7,6},{8,7},{9,8},{10,9... | collective-permute-start | bytes 1351688 | tf_op jit(solution)/shard_map/ppermute | solution.py:335
  27.4 14.9 %collective-permute-start.3 = (f32[2,11,40,128]{3,2,1,0:T(8,128)}, f32[2,11,40,128]{3,2,1,0:T(8,128)S(1)}, u32[]{:S(2)}, u32[]{:S(2)}) collective-permute-start(f32[2,11,40,128]{3,2,1,0:T(8,128)} %shard_map.59.e_ref), channel_id=1, source_target_pairs={{0,1},{1,2},{2,3},{3,4},{4,5},{5,6},{6,7},{7,8},{8,9},{9,10},{10,1... | collective-permute-start | bytes 1351688 | tf_op jit(solution)/shard_map/ppermute | solution.py:334
  42.3 0.8 %copy-start = (f32[2,11,40,128]{3,2,1,0:T(8,128)}, f32[2,11,40,128]{3,2,1,0:T(8,128)S(1)}, u32[]{:S(2)}) copy-start(f32[2,11,40,128]{3,2,1,0:T(8,128)S(1)} %collective-permute-done.4.ee_ref) | copy-start | bytes 1351684
  42.3 0.9 %copy-start.1 = (f32[2,11,40,128]{3,2,1,0:T(8,128)}, f32[2,11,40,128]{3,2,1,0:T(8,128)S(1)}, u32[]{:S(2)}) copy-start(f32[2,11,40,128]{3,2,1,0:T(8,128)S(1)} %collective-permute-done.3.ew_ref) | copy-start | bytes 1351684

commit v9 on v7

--- a/solution.py
+++ b/solution.py
@@ -202,10 +202,15 @@
 
 
 def _final_kernel(
-    e_ref, ew_ref, ee_ref, rv_ref, thk_i, wind_i, trc_i, thk_o, wind_o, trc_o, g0_ref, g1_ref, pg_ref, mf_ref
+    e_ref, ew_ref, ee_ref, rv_ref, thk_h, wind_h, trc_h, thk_oh, wind_oh, trc_oh, g0_ref, g1_ref, pg_ref, mf_ref,
+    thk_i, wind_i, trc_i, sem,
 ):
     nslab, nf, tall, w = e_ref.shape
     nlev, rows = thk_i.shape[0], thk_i.shape[1]
+    ins = [pltpu.make_async_copy(h, v, sem.at[k]) for k, (h, v) in enumerate(zip((thk_h, wind_h, trc_h), (thk_i, wind_i, trc_i)))]
+    for c in ins:
+        c.start()
+    thk_o, wind_o, trc_o = thk_i, wind_i, trc_i
     per = w // GW
     rv = (rv_ref[0], rv_ref[1], rv_ref[2])
     lane, group, kk = _lanes(tall, w)
@@ -234,6 +239,8 @@
             )
     lane_o = lane[:rows]
     inner = pl.ds(MARGIN + HALO, rows)
+    for c in ins:
+        c.wait()
     for lev in range(nlev):
         s, g = _slab_of(lev, per)
         for f in range(nf):
@@ -247,6 +254,11 @@
             else:
                 src, dst = trc_i.at[f - 3, lev], trc_o.at[f - 3, lev]
             dst[...] = jnp.where(lane_o < HALO, lo, jnp.where(lane_o >= w - HALO, hi, src[...]))
+    outs = [pltpu.make_async_copy(v, h, sem.at[3 + k]) for k, (v, h) in enumerate(zip((thk_i, wind_i, trc_i), (thk_oh, wind_oh, trc_oh)))]
+    for c in outs:
+        c.start()
+    for c in outs:
+        c.wait()
 
 
 def _shift_pairs(n, d, closed):
@@ -354,22 +366,29 @@
         cost_estimate=pl.CostEstimate(flops=2 * step_flops, bytes_accessed=2 * slab * nlev, transcendentals=0),
     )(south, thickness, winds, tracer_mass, north, thickness, south, north, rowvec)
 
-    return _vmem_call(
+    vmem = pl.BlockSpec(memory_space=pltpu.VMEM)
+    anywhere = pl.BlockSpec(memory_space=pl.ANY)
+    return pl.pallas_call(
         _final_kernel,
-        (
+        out_shape=(
             jax.ShapeDtypeStruct(thickness.shape, jnp.float32),
             jax.ShapeDtypeStruct(winds.shape, jnp.float32),
             jax.ShapeDtypeStruct(tracer_mass.shape, jnp.float32),
         ),
-        7,
-        [
+        in_specs=[vmem] * 4 + [anywhere] * 3,
+        out_specs=(anywhere, anywhere, anywhere),
+        input_output_aliases={4: 0, 5: 1, 6: 2},
+        scratch_shapes=[
             pltpu.VMEM((nslab, nf, deep, w), jnp.float32),
             pltpu.VMEM((nslab, nf, deep, w), jnp.float32),
             pltpu.VMEM((nslab, deep, w), jnp.float32),
             pltpu.VMEM((nf, deep, w), jnp.float32),
+            pltpu.VMEM(thickness.shape, jnp.float32),
+            pltpu.VMEM(winds.shape, jnp.float32),
+            pltpu.VMEM(tracer_mass.shape, jnp.float32),
+            pltpu.SemaphoreType.DMA((6,)),
         ],
-        4 * step_flops // nlev,
-        4 * slab * nslab,
+        cost_estimate=pl.CostEstimate(flops=4 * step_flops // nlev, bytes_accessed=4 * slab * nslab, transcendentals=0),
     )(edges, from_west, from_east, rowvec, *raw)
 
 

time: 52.7 us -> 52.1 us (0.989)
  Pallas kernels: 28.4 us -> 27.8 us
    pallas_call x1, Pallas kernels: 8.23 us -> 7.65 us  [shards(): pl.pallas_call(_final_kernel, out_shape=(jax.ShapeDtypeStruct(thickness.s...]
where the time goes in v9:
time: 52.1 us; the launch traced here: 51.7 us
  Pallas kernels  27.8 us (53%)
  starting transfers between devices  12.8 us (25%)
  waiting for transfers between devices  6.45 us (12%)
  other arithmetic  2.15 us (4%)
  local copies, waits for them, and re-layouts  1.85 us (4%)
  between operations  0.73 us (1%)
    pallas_call x1, Pallas kernels, shards(): pl.pallas_call(_main_kernel, out_shape=(jax.ShapeDtypeStruct(thickness.sh...  14.9 us
    pallas_call x1, Pallas kernels, shards(): pl.pallas_call(_final_kernel, out_shape=(jax.ShapeDtypeStruct(thickness.s...  7.65 us
    ppermute x1, waiting for transfers between devices, shards(): from_south = lax.ppermute(top, 'lat', _shift_pairs(nlat, 1, False))  6.44 us
    ppermute x1, starting transfers between devices, shards(): from_east = lax.ppermute(edges, 'lon', _shift_pairs(nlon, -1, True))  5.72 us
    ppermute x1, starting transfers between devices, shards(): from_north = lax.ppermute(bottom, 'lat', _shift_pairs(nlat, -1, False))  4.44 us
    pallas_call x1, Pallas kernels, shards(): _vmem_call(_edge_inner_kernel, jax.ShapeDtypeStruct((nslab, nf, rows, w),...  2.92 us
    pallas_call x1, Pallas kernels, shards(): _vmem_call(_edge_kernel, jax.ShapeDtypeStruct((nslab, nf, tall, w), jnp.f...  2.31 us
    ppermute x1, starting transfers between devices, shards(): from_south = lax.ppermute(top, 'lat', _shift_pairs(nlat, 1, False))  1.92 us
  transfers between devices with their start and end apart: 5, of which 1 were waited for; matrix products, arithmetic and copies ran while one was open for 2% of the time, Pallas kernels for 34%

profile of v9, /device:TPU:16, one launch (start us, length us, event | category | flops | bytes accessed | tf_op | source)
XLA Modules:
  0.0 51.7 jit_solution(16595742339281229330)
XLA Ops:
  0.6 1.2 %broadcast_select_fusion = (f32[11,8,4,128]{3,2,1,0:T(4,128)S(1)}, f32[11,8,4,128]{3,2,1,0:T(4,128)S(1)}, f32[11,8,4,128]{3,2,1,0:T(4,128)S(1)}) fusion(pred[]{:T(512)S(6)} %eq.14, f32[8,8,32,128]{3,2,1,0:T(8,128)} %trc_ref.3, f32[2,8,32,128]{3,2,1,0:T(8,128)} %wind_ref.3, f32[1,8,32,128]{3,2,1,0:T(8,128)} %bitcast.1), kind=kLoop, calls=%fused_computation.5 | loop fusion | flops 225280 | bytes 1982465 | tf_op jit(solution)/shard_map/jit(_where)/select_n | solution.py:318
  1.8 0.7 %collective-permute-start = (f32[11,8,4,128]{3,2,1,0:T(4,128)S(1)}, f32[11,8,4,128]{3,2,1,0:T(4,128)S(1)}, u32[]{:S(2)}, u32[]{:S(2)}) collective-permute-start(f32[11,8,4,128]{3,2,1,0:T(4,128)S(1)} %get-tuple-element.9), channel_id=1, source_target_pairs={{0,16},{1,17},{2,18},{3,19},{4,20},{5,21},{6,22},{7,23},{8,24},{9,... | collective-permute-start | bytes 540680 | tf_op jit(solution)/shard_map/ppermute | solution.py:319
  2.5 4.4 %collective-permute-start.2 = (f32[11,8,4,128]{3,2,1,0:T(4,128)S(1)}, f32[11,8,4,128]{3,2,1,0:T(4,128)S(1)}, u32[]{:S(2)}, u32[]{:S(2)}) collective-permute-start(f32[11,8,4,128]{3,2,1,0:T(4,128)S(1)} %get-tuple-element.10), channel_id=1, source_target_pairs={{32,0},{64,32},{96,64},{128,96},{160,128},{192,160},{224,192},{33,... | collective-permute-start | bytes 540680 | tf_op jit(solution)/shard_map/ppermute | solution.py:312
  6.9 1.9 %collective-permute-start.1 = (f32[11,8,4,128]{3,2,1,0:T(4,128)S(1)}, f32[11,8,4,128]{3,2,1,0:T(4,128)S(1)}, u32[]{:S(2)}, u32[]{:S(2)}) collective-permute-start(f32[11,8,4,128]{3,2,1,0:T(4,128)S(1)} %get-tuple-element.11), channel_id=1, source_target_pairs={{0,32},{32,64},{64,96},{96,128},{128,160},{160,192},{192,224},{1,3... | collective-permute-start | bytes 540680 | tf_op jit(solution)/shard_map/ppermute | solution.py:311
  8.9 2.9 %shard_map.58.inner_ref = f32[2,11,32,128]{3,2,1,0:T(8,128)} custom-call(f32[8,32,128]{2,1,0:T(8,128)} %tall_ref.1, f32[2,8,32,128]{3,2,1,0:T(8,128)} %wind_ref.3, f32[8,8,32,128]{3,2,1,0:T(8,128)} %trc_ref.3), custom_call_target="tpu_custom_call" | custom-call | bytes 1441792 | tf_op jit(solution)/shard_map/pallas_call | solution.py:305
  11.8 0.0 collective-permute-done
  11.8 0.2 rev.4
  12.0 0.0 collective-permute-done.2
  12.0 6.4 %collective-permute-done.1 = f32[11,8,4,128]{3,2,1,0:T(4,128)S(1)} collective-permute-done((f32[11,8,4,128]{3,2,1,0:T(4,128)S(1)}, f32[11,8,4,128]{3,2,1,0:T(4,128)S(1)}, u32[]{:S(2)}, u32[]{:S(2)}) %collective-permute-start.1) | collective-permute-done | bytes 180256 | tf_op jit(solution)/shard_map/ppermute | solution.py:311
  18.4 0.9 %multiply_select_fusion = (f32[11,8,4,128]{3,2,1,0:T(4,128)}, f32[11,8,4,128]{3,2,1,0:T(4,128)}) fusion(f32[11,8,4,128]{3,2,1,0:T(4,128)S(1)} %collective-permute-done.2, f32[11,8,4,128]{3,2,1,0:T(4,128)S(1)} %rev.4, f32[11]{0:T(128)S(1)} %compare_select_fusion.1, pred[]{:T(512)S(6)} %eq.16, f32[11,8,4,128]{3,2,1,0:T(4,128)S(1)} %collective-permute-done.1, ...), kind=kLoop, calls=%fused_computation.3 | loop fusion | flops 135168 | bytes 901166 | tf_op jit(solution)/shard_map/jit(_where)/select_n | solution.py:323
  19.3 2.3 %shard_map.59.e_ref = f32[2,11,40,128]{3,2,1,0:T(8,128)} custom-call(f32[11,8,4,128]{3,2,1,0:T(4,128)} %get-tuple-element.13.south_ref.sall_ref, f32[2,11,32,128]{3,2,1,0:T(8,128)} %shard_map.58.inner_ref, f32[11,8,4,128]{3,2,1,0:T(4,128)} %get-tuple-element.12.north_ref.nall_ref), custom_call_target="tpu_custom_call" | custom-call | bytes 901120 | tf_op jit(solution)/shard_map/pallas_call | solution.py:326
  21.6 5.7 %collective-permute-start.4 = (f32[2,11,40,128]{3,2,1,0:T(8,128)}, f32[2,11,40,128]{3,2,1,0:T(8,128)S(1)}, u32[]{:S(2)}, u32[]{:S(2)}) collective-permute-start(f32[2,11,40,128]{3,2,1,0:T(8,128)} %shard_map.59.e_ref), channel_id=1, source_target_pairs={{0,31},{1,0},{2,1},{3,2},{4,3},{5,4},{6,5},{7,6},{8,7},{9,8},{10,9... | collective-permute-start | bytes 1351688 | tf_op jit(solution)/shard_map/ppermute | solution.py:330
  27.4 0.0 collective-permute-start.3
  27.4 0.1 fusion
  27.5 0.7 %broadcast_in_dim.28.rv_ref = f32[3,40,128]{2,1,0:T(8,128)} broadcast(f32[3,40]{1,0:T(4,128)S(1)} %pad_maximum_fusion.3), dimensions={0,1} | broadcast | bytes 61920 | tf_op jit(solution)/shard_map/broadcast_in_dim | solution.py:303
  28.2 14.9 %shard_map.60 = (f32[8,32,128]{2,1,0:T(8,128)}, f32[2,8,32,128]{3,2,1,0:T(8,128)}, f32[8,8,32,128]{3,2,1,0:T(8,128)}) custom-call(f32[11,8,4,128]{3,2,1,0:T(4,128)} %get-tuple-element.13.south_ref.sall_ref, f32[8,32,128]{2,1,0:T(8,128)} %tall_ref.1, f32[2,8,32,128]{3,2,1,0:T(8,128)} %wind_ref.3, f32[8,8,32,128]{3,2,1,0:T(8,128)} %trc_ref.3, ...), custom_call_target="tpu_custom_call" | custom-call | flops 54067200 | bytes 3604480 | tf_op jit(solution)/shard_map/pallas_call | solution.py:335
  43.1 0.0 collective-permute-done.4.ee_ref
  43.1 0.0 copy-start
  43.1 0.0 collective-permute-done.3.ew_ref
  43.1 0.0 copy-start.1
  43.1 0.8 %copy-done = f32[2,11,40,128]{3,2,1,0:T(8,128)} copy-done((f32[2,11,40,128]{3,2,1,0:T(8,128)}, f32[2,11,40,128]{3,2,1,0:T(8,128)S(1)}, u32[]{:S(2)}) %copy-start) | copy-done | bytes 450584
  43.9 0.2 copy-done.1
  44.1 7.7 %shard_map.61 = (f32[8,32,128]{2,1,0:T(8,128)}, f32[2,8,32,128]{3,2,1,0:T(8,128)}, f32[8,8,32,128]{3,2,1,0:T(8,128)}) custom-call(f32[2,11,40,128]{3,2,1,0:T(8,128)} %shard_map.59.e_ref, f32[2,11,40,128]{3,2,1,0:T(8,128)} %copy-done.1, f32[2,11,40,128]{3,2,1,0:T(8,128)} %copy-done, ...), custom_call_target="tpu_custom_call", output_to_operand_aliasing={{0}: (4, {}), {1}: (5, {}), {2}: (6, {})} | custom-call | flops 13516800 | bytes 1802240 | tf_op jit(solution)/shard_map/pallas_call | solution.py:371
  (3 shorter events, 0.1 us)
Async XLA Ops:
  1.8 10.0 %collective-permute-start = (f32[11,8,4,128]{3,2,1,0:T(4,128)S(1)}, f32[11,8,4,128]{3,2,1,0:T(4,128)S(1)}, u32[]{:S(2)}, u32[]{:S(2)}) collective-permute-start(f32[11,8,4,128]{3,2,1,0:T(4,128)S(1)} %get-tuple-element.9), channel_id=1, source_target_pairs={{0,16},{1,17},{2,18},{3,19},{4,20},{5,21},{6,22},{7,23},{8,24},{9,... | collective-permute-start | bytes 540680 | tf_op jit(solution)/shard_map/ppermute | solution.py:319
  2.5 9.5 %collective-permute-start.2 = (f32[11,8,4,128]{3,2,1,0:T(4,128)S(1)}, f32[11,8,4,128]{3,2,1,0:T(4,128)S(1)}, u32[]{:S(2)}, u32[]{:S(2)}) collective-permute-start(f32[11,8,4,128]{3,2,1,0:T(4,128)S(1)} %get-tuple-element.10), channel_id=1, source_target_pairs={{32,0},{64,32},{96,64},{128,96},{160,128},{192,160},{224,192},{33,... | collective-permute-start | bytes 540680 | tf_op jit(solution)/shard_map/ppermute | solution.py:312
  6.9 11.5 %collective-permute-start.1 = (f32[11,8,4,128]{3,2,1,0:T(4,128)S(1)}, f32[11,8,4,128]{3,2,1,0:T(4,128)S(1)}, u32[]{:S(2)}, u32[]{:S(2)}) collective-permute-start(f32[11,8,4,128]{3,2,1,0:T(4,128)S(1)} %get-tuple-element.11), channel_id=1, source_target_pairs={{0,32},{32,64},{64,96},{96,128},{128,160},{160,192},{192,224},{1,3... | collective-permute-start | bytes 540680 | tf_op jit(solution)/shard_map/ppermute | solution.py:311
  21.6 21.5 %collective-permute-start.4 = (f32[2,11,40,128]{3,2,1,0:T(8,128)}, f32[2,11,40,128]{3,2,1,0:T(8,128)S(1)}, u32[]{:S(2)}, u32[]{:S(2)}) collective-permute-start(f32[2,11,40,128]{3,2,1,0:T(8,128)} %shard_map.59.e_ref), channel_id=1, source_target_pairs={{0,31},{1,0},{2,1},{3,2},{4,3},{5,4},{6,5},{7,6},{8,7},{9,8},{10,9... | collective-permute-start | bytes 1351688 | tf_op jit(solution)/shard_map/ppermute | solution.py:330
  27.4 15.8 %collective-permute-start.3 = (f32[2,11,40,128]{3,2,1,0:T(8,128)}, f32[2,11,40,128]{3,2,1,0:T(8,128)S(1)}, u32[]{:S(2)}, u32[]{:S(2)}) collective-permute-start(f32[2,11,40,128]{3,2,1,0:T(8,128)} %shard_map.59.e_ref), channel_id=1, source_target_pairs={{0,1},{1,2},{2,3},{3,4},{4,5},{5,6},{6,7},{7,8},{8,9},{9,10},{10,1... | collective-permute-start | bytes 1351688 | tf_op jit(solution)/shard_map/ppermute | solution.py:329
  43.1 0.8 %copy-start = (f32[2,11,40,128]{3,2,1,0:T(8,128)}, f32[2,11,40,128]{3,2,1,0:T(8,128)S(1)}, u32[]{:S(2)}) copy-start(f32[2,11,40,128]{3,2,1,0:T(8,128)S(1)} %collective-permute-done.4.ee_ref) | copy-start | bytes 1351684
  43.1 0.9 %copy-start.1 = (f32[2,11,40,128]{3,2,1,0:T(8,128)}, f32[2,11,40,128]{3,2,1,0:T(8,128)S(1)}, u32[]{:S(2)}) copy-start(f32[2,11,40,128]{3,2,1,0:T(8,128)S(1)} %collective-permute-done.3.ew_ref) | copy-start | bytes 1351684

commit v10 on v9

--- a/solution.py
+++ b/solution.py
@@ -111,9 +111,25 @@
             e_ref[s, f] = _pack_own(get, nlev, rows, w, s, zeros)
 
 
-def _edge_kernel(south_ref, inner_ref, north_ref, e_ref):
-    nf, nlev, halo, w = south_ref.shape
+def _edge_kernel(
+    pole_at_ref, fs_ref, fn_ref, pole_ref, inner_ref, rvi_ref, e_ref, south_ref, north_ref, rv_ref
+):
+    nf, nlev, halo, w = fs_ref.shape
     nslab, rows = inner_ref.shape[0], inner_ref.shape[2]
+    tall = rv_ref.shape[1]
+    for k in range(rv_ref.shape[0]):
+        rv_ref[k] = jnp.broadcast_to(rvi_ref[k], (tall, w))
+    at_south = pole_at_ref[0] == 1
+    at_north = pole_at_ref[1] == 1
+    for f in range(nf):
+        for lev in range(nlev):
+            for k in range(halo):
+                mirrored = pole_ref[f, lev, pl.ds(halo - 1 - k, 1)]
+                if f == 2:
+                    mirrored = -mirrored
+                row = pl.ds(k, 1)
+                south_ref[f, lev, row] = jnp.where(at_south, mirrored, fs_ref[f, lev, row])
+                north_ref[f, lev, row] = jnp.where(at_north, mirrored, fn_ref[f, lev, row])
     zeros = jnp.zeros((halo, w), jnp.float32)
     for s in range(nslab):
         for f in range(nf):
@@ -300,7 +316,7 @@
             COUR * FCOR * jnp.sin(center_lat) * jnp.where(center_cos >= 0.0, 1.0, -1.0),
         ]
     )
-    rowvec = jnp.broadcast_to(rowvec[:, :, None], (3, tall, w))
+    rowvec = rowvec[:, :, None]
 
     inner_edges = _vmem_call(
         _edge_inner_kernel, jax.ShapeDtypeStruct((nslab, nf, rows, w), jnp.float32), 3, [], 0, nf * nlev * rows * w * 4
@@ -317,15 +333,22 @@
             pole_pairs.append((b * nlon + s, b * nlon + (s + half) % nlon))
     pole_out = jnp.where(band == 0, bottom, top)
     pole_in = lax.ppermute(pole_out, ("lat", "lon"), pole_pairs)
-    sign = jnp.where(jnp.arange(nf) == 2, -1.0, 1.0).astype(jnp.float32)[:, None, None, None]
-    mirrored = jnp.flip(pole_in, 2) * sign
-    south = jnp.where(band == 0, mirrored, from_south)
-    north = jnp.where(band == nlat - 1, mirrored, from_north)
+    pole_at = jnp.stack([band == 0, band == nlat - 1]).astype(jnp.int32)
 
     slab = nf * tall * w * 4
-    edges = _vmem_call(
-        _edge_kernel, jax.ShapeDtypeStruct((nslab, nf, tall, w), jnp.float32), 3, [], 0, 2 * slab * nslab
-    )(south, inner_edges, north)
+    vmem = pl.BlockSpec(memory_space=pltpu.VMEM)
+    edges, south, north, rowvec = pl.pallas_call(
+        _edge_kernel,
+        out_shape=(
+            jax.ShapeDtypeStruct((nslab, nf, tall, w), jnp.float32),
+            jax.ShapeDtypeStruct(top.shape, jnp.float32),
+            jax.ShapeDtypeStruct(top.shape, jnp.float32),
+            jax.ShapeDtypeStruct((3, tall, w), jnp.float32),
+        ),
+        in_specs=[pl.BlockSpec(memory_space=pltpu.SMEM)] + [vmem] * 5,
+        out_specs=(vmem, vmem, vmem, vmem),
+        cost_estimate=pl.CostEstimate(flops=0, bytes_accessed=2 * slab * nslab, transcendentals=0),
+    )(pole_at, from_south, from_north, pole_in, inner_edges, rowvec)
     from_west = lax.ppermute(edges, "lon", _shift_pairs(nlon, 1, True))
     from_east = lax.ppermute(edges, "lon", _shift_pairs(nlon, -1, True))
 

time: 52.1 us -> 51.2 us (0.983)
  waiting for transfers between devices: 6.45 us -> 5.16 us
    ppermute x1, waiting for transfers between devices: 6.44 us -> 5.15 us  [shards(): from_south = lax.ppermute(top, 'lat', _shift_pairs(nlat, 1, False))]
    select_n x2 -> x0, other arithmetic: 0.89 us -> none  [the longest x1 0.89 us: shards(): north = jnp.where(band == nlat - 1, mirrored, from_north)]
    convert_element_type x0 -> x1, other arithmetic: none -> 0.65 us  [shards(): pole_at = jnp.stack([band == 0, band == nlat - 1]).astype(jnp.int32)]
    unnamed x4 -> x10, local copies, waits for them, and re-layouts: 0.93 us -> 1.57 us
  transfers between devices with their start and end apart: 5 -> 5, of which waited for: 1 -> 1; matrix products, arithmetic and copies ran while one was open for 2% -> 3% of each run, Pallas kernels for 34% -> 35%
where the time goes in v10:
time: 51.2 us; the launch traced here: 50.8 us
  Pallas kernels  28 us (55%)
  starting transfers between devices  12.8 us (25%)
  waiting for transfers between devices  5.16 us (10%)
  local copies, waits for them, and re-layouts  2.3 us (4%)
  other arithmetic  1.91 us (4%)
  between operations  0.73 us (1%)
    pallas_call x1, Pallas kernels, shards(): pl.pallas_call(_main_kernel, out_shape=(jax.ShapeDtypeStruct(thickness.sh...  14.9 us
    pallas_call x1, Pallas kernels, shards(): pl.pallas_call(_final_kernel, out_shape=(jax.ShapeDtypeStruct(thickness.s...  7.65 us
    ppermute x1, starting transfers between devices, shards(): from_east = lax.ppermute(edges, 'lon', _shift_pairs(nlon, -1, True))  5.72 us
    ppermute x1, waiting for transfers between devices, shards(): from_south = lax.ppermute(top, 'lat', _shift_pairs(nlat, 1, False))  5.15 us
    ppermute x1, starting transfers between devices, shards(): from_north = lax.ppermute(bottom, 'lat', _shift_pairs(nlat, -1, False))  4.44 us
    pallas_call x1, Pallas kernels, shards(): _vmem_call(_edge_inner_kernel, jax.ShapeDtypeStruct((nslab, nf, rows, w),...  2.92 us
    pallas_call x1, Pallas kernels, shards(): pl.pallas_call(_edge_kernel, out_shape=(jax.ShapeDtypeStruct((nslab, nf,...  2.47 us
    ppermute x1, starting transfers between devices, shards(): from_south = lax.ppermute(top, 'lat', _shift_pairs(nlat, 1, False))  1.92 us
  transfers between devices with their start and end apart: 5, of which 1 were waited for; matrix products, arithmetic and copies ran while one was open for 3% of the time, Pallas kernels for 35%

profile of v10, /device:TPU:16, one launch (start us, length us, event | category | flops | bytes accessed | tf_op | source)
XLA Modules:
  0.0 50.8 jit_solution(14355426645511063646)
XLA Ops:
  0.6 1.2 %broadcast_select_fusion = (f32[11,8,4,128]{3,2,1,0:T(4,128)S(1)}, f32[11,8,4,128]{3,2,1,0:T(4,128)S(1)}, f32[11,8,4,128]{3,2,1,0:T(4,128)S(1)}) fusion(pred[]{:T(512)} %eq.7, f32[8,8,32,128]{3,2,1,0:T(8,128)} %trc_ref.3, f32[2,8,32,128]{3,2,1,0:T(8,128)} %wind_ref.3, f32[1,8,32,128]{3,2,1,0:T(8,128)} %bitcast.5), kind=kLoop, calls=%fused_computation.3 | loop fusion | flops 225280 | bytes 1982465 | tf_op jit(solution)/shard_map/jit(_where)/select_n | solution.py:334
  1.8 0.7 %collective-permute-start.2 = (f32[11,8,4,128]{3,2,1,0:T(4,128)S(1)}, f32[11,8,4,128]{3,2,1,0:T(4,128)S(1)}, u32[]{:S(2)}, u32[]{:S(2)}) collective-permute-start(f32[11,8,4,128]{3,2,1,0:T(4,128)S(1)} %get-tuple-element.17), channel_id=1, source_target_pairs={{0,16},{1,17},{2,18},{3,19},{4,20},{5,21},{6,22},{7,23},{8,24},{9,... | collective-permute-start | bytes 540680 | tf_op jit(solution)/shard_map/ppermute | solution.py:335
  2.5 4.4 %collective-permute-start.1 = (f32[11,8,4,128]{3,2,1,0:T(4,128)S(1)}, f32[11,8,4,128]{3,2,1,0:T(4,128)S(1)}, u32[]{:S(2)}, u32[]{:S(2)}) collective-permute-start(f32[11,8,4,128]{3,2,1,0:T(4,128)S(1)} %get-tuple-element.18), channel_id=1, source_target_pairs={{32,0},{64,32},{96,64},{128,96},{160,128},{192,160},{224,192},{33,... | collective-permute-start | bytes 540680 | tf_op jit(solution)/shard_map/ppermute | solution.py:328
  6.9 1.9 %collective-permute-start = (f32[11,8,4,128]{3,2,1,0:T(4,128)S(1)}, f32[11,8,4,128]{3,2,1,0:T(4,128)S(1)}, u32[]{:S(2)}, u32[]{:S(2)}) collective-permute-start(f32[11,8,4,128]{3,2,1,0:T(4,128)S(1)} %get-tuple-element.19), channel_id=1, source_target_pairs={{0,32},{32,64},{64,96},{96,128},{128,160},{160,192},{192,224},{1,3... | collective-permute-start | bytes 540680 | tf_op jit(solution)/shard_map/ppermute | solution.py:327
  8.9 0.1 fusion
  9.0 2.9 %shard_map.58.inner_ref = f32[2,11,32,128]{3,2,1,0:T(8,128)} custom-call(f32[8,32,128]{2,1,0:T(8,128)} %tall_ref.1, f32[2,8,32,128]{3,2,1,0:T(8,128)} %wind_ref.3, f32[8,8,32,128]{3,2,1,0:T(8,128)} %trc_ref.3), custom_call_target="tpu_custom_call" | custom-call | bytes 1441792 | tf_op jit(solution)/shard_map/pallas_call | solution.py:321
  11.9 0.7 %copy.9.rvi_ref = f32[3,40,1]{2,1,0:T(8,128)} copy(f32[3,40,1]{1,0,2:T(4,128)S(1)} %maximum_bitcast_fusion) | data formatting | bytes 960 | tf_op jit(solution)/shard_map/broadcast_in_dim | solution.py:319
  12.6 0.6 %add_convert_fusion.pole_at_ref = s32[2]{0:T(128)} fusion(pred[1]{0:T(512)(128)(4,1)} %bitcast.1, pred[1]{0:T(512)(128)(4,1)} %bitcast), kind=kLoop, calls=%fused_computation.5 | loop fusion | flops 4 | bytes 10 | tf_op jit(solution)/shard_map/convert_element_type | solution.py:336
  13.3 0.0 collective-permute-done.2.pole_ref
  13.3 0.0 copy-start.2
  13.3 0.0 collective-permute-done.1.fn_ref
  13.3 0.0 copy-start.3
  13.3 5.1 %collective-permute-done.fs_ref = f32[11,8,4,128]{3,2,1,0:T(4,128)S(1)} collective-permute-done((f32[11,8,4,128]{3,2,1,0:T(4,128)S(1)}, f32[11,8,4,128]{3,2,1,0:T(4,128)S(1)}, u32[]{:S(2)}, u32[]{:S(2)}) %collective-permute-start) | collective-permute-done | bytes 180256 | tf_op jit(solution)/shard_map/ppermute | solution.py:327
  18.4 0.0 copy-done.2
  18.4 0.0 copy-done.3
  18.5 0.0 copy-start.4
  18.5 0.7 %copy-done.4 = f32[11,8,4,128]{3,2,1,0:T(4,128)} copy-done((f32[11,8,4,128]{3,2,1,0:T(4,128)}, f32[11,8,4,128]{3,2,1,0:T(4,128)S(1)}, u32[]{:S(2)}) %copy-start.4) | copy-done | bytes 180248
  19.1 2.5 %shard_map.59 = (f32[2,11,40,128]{3,2,1,0:T(8,128)}, f32[11,8,4,128]{3,2,1,0:T(4,128)}, f32[11,8,4,128]{3,2,1,0:T(4,128)}, f32[3,40,128]{2,1,0:T(8,128)}) custom-call(s32[2]{0:T(128)} %add_convert_fusion.pole_at_ref, f32[11,8,4,128]{3,2,1,0:T(4,128)} %copy-done.4, f32[11,8,4,128]{3,2,1,0:T(4,128)} %copy-done.3, f32[11,8,4,128]{3,2,1,0:T(4,128)} %copy-done.2, ...), custom_call_target="tpu_custom_call" | custom-call | bytes 901120 | tf_op jit(solution)/shard_map/pallas_call | solution.py:340
  21.6 5.7 %collective-permute-start.4 = (f32[2,11,40,128]{3,2,1,0:T(8,128)}, f32[2,11,40,128]{3,2,1,0:T(8,128)S(1)}, u32[]{:S(2)}, u32[]{:S(2)}) collective-permute-start(f32[2,11,40,128]{3,2,1,0:T(8,128)} %get-tuple-element.10.e_ref), channel_id=1, source_target_pairs={{0,31},{1,0},{2,1},{3,2},{4,3},{5,4},{6,5},{7,6},{8,7},{9,8},{10,9... | collective-permute-start | bytes 1351688 | tf_op jit(solution)/shard_map/ppermute | solution.py:353
  27.3 0.0 collective-permute-start.3
  27.3 14.9 %shard_map.60 = (f32[8,32,128]{2,1,0:T(8,128)}, f32[2,8,32,128]{3,2,1,0:T(8,128)}, f32[8,8,32,128]{3,2,1,0:T(8,128)}) custom-call(f32[11,8,4,128]{3,2,1,0:T(4,128)} %get-tuple-element.12.south_ref.sall_ref, f32[8,32,128]{2,1,0:T(8,128)} %tall_ref.1, f32[2,8,32,128]{3,2,1,0:T(8,128)} %wind_ref.3, f32[8,8,32,128]{3,2,1,0:T(8,128)} %trc_ref.3, ...), custom_call_target="tpu_custom_call" | custom-call | flops 54067200 | bytes 3604480 | tf_op jit(solution)/shard_map/pallas_call | solution.py:358
  42.2 0.0 collective-permute-done.4.ee_ref
  42.3 0.0 copy-start
  42.3 0.0 collective-permute-done.3.ew_ref
  42.3 0.0 copy-start.1
  42.3 0.8 %copy-done = f32[2,11,40,128]{3,2,1,0:T(8,128)} copy-done((f32[2,11,40,128]{3,2,1,0:T(8,128)}, f32[2,11,40,128]{3,2,1,0:T(8,128)S(1)}, u32[]{:S(2)}) %copy-start) | copy-done | bytes 450584
  43.0 0.1 copy-done.1
  43.2 7.7 %shard_map.61 = (f32[8,32,128]{2,1,0:T(8,128)}, f32[2,8,32,128]{3,2,1,0:T(8,128)}, f32[8,8,32,128]{3,2,1,0:T(8,128)}) custom-call(f32[2,11,40,128]{3,2,1,0:T(8,128)} %get-tuple-element.10.e_ref, f32[2,11,40,128]{3,2,1,0:T(8,128)} %copy-done.1, f32[2,11,40,128]{3,2,1,0:T(8,128)} %copy-done, ...), custom_call_target="tpu_custom_call", output_to_operand_aliasing={{0}: (4, {}), {1}: (5, {}), {2}: (6, {})} | custom-call | flops 13516800 | bytes 1802240 | tf_op jit(solution)/shard_map/pallas_call | solution.py:394
  (2 shorter events, 0.1 us)
Async XLA Ops:
  1.8 11.5 %collective-permute-start.2 = (f32[11,8,4,128]{3,2,1,0:T(4,128)S(1)}, f32[11,8,4,128]{3,2,1,0:T(4,128)S(1)}, u32[]{:S(2)}, u32[]{:S(2)}) collective-permute-start(f32[11,8,4,128]{3,2,1,0:T(4,128)S(1)} %get-tuple-element.17), channel_id=1, source_target_pairs={{0,16},{1,17},{2,18},{3,19},{4,20},{5,21},{6,22},{7,23},{8,24},{9,... | collective-permute-start | bytes 540680 | tf_op jit(solution)/shard_map/ppermute | solution.py:335
  2.5 10.8 %collective-permute-start.1 = (f32[11,8,4,128]{3,2,1,0:T(4,128)S(1)}, f32[11,8,4,128]{3,2,1,0:T(4,128)S(1)}, u32[]{:S(2)}, u32[]{:S(2)}) collective-permute-start(f32[11,8,4,128]{3,2,1,0:T(4,128)S(1)} %get-tuple-element.18), channel_id=1, source_target_pairs={{32,0},{64,32},{96,64},{128,96},{160,128},{192,160},{224,192},{33,... | collective-permute-start | bytes 540680 | tf_op jit(solution)/shard_map/ppermute | solution.py:328
  6.9 11.5 %collective-permute-start = (f32[11,8,4,128]{3,2,1,0:T(4,128)S(1)}, f32[11,8,4,128]{3,2,1,0:T(4,128)S(1)}, u32[]{:S(2)}, u32[]{:S(2)}) collective-permute-start(f32[11,8,4,128]{3,2,1,0:T(4,128)S(1)} %get-tuple-element.19), channel_id=1, source_target_pairs={{0,32},{32,64},{64,96},{96,128},{128,160},{160,192},{192,224},{1,3... | collective-permute-start | bytes 540680 | tf_op jit(solution)/shard_map/ppermute | solution.py:327
  13.3 5.2 %copy-start.2 = (f32[11,8,4,128]{3,2,1,0:T(4,128)}, f32[11,8,4,128]{3,2,1,0:T(4,128)S(1)}, u32[]{:S(2)}) copy-start(f32[11,8,4,128]{3,2,1,0:T(4,128)S(1)} %collective-permute-done.2.pole_ref) | copy-start | bytes 540676
  13.3 5.2 %copy-start.3 = (f32[11,8,4,128]{3,2,1,0:T(4,128)}, f32[11,8,4,128]{3,2,1,0:T(4,128)S(1)}, u32[]{:S(2)}) copy-start(f32[11,8,4,128]{3,2,1,0:T(4,128)S(1)} %collective-permute-done.1.fn_ref) | copy-start | bytes 540676
  18.5 0.7 %copy-start.4 = (f32[11,8,4,128]{3,2,1,0:T(4,128)}, f32[11,8,4,128]{3,2,1,0:T(4,128)S(1)}, u32[]{:S(2)}) copy-start(f32[11,8,4,128]{3,2,1,0:T(4,128)S(1)} %collective-permute-done.fs_ref) | copy-start | bytes 540676
  21.6 20.7 %collective-permute-start.4 = (f32[2,11,40,128]{3,2,1,0:T(8,128)}, f32[2,11,40,128]{3,2,1,0:T(8,128)S(1)}, u32[]{:S(2)}, u32[]{:S(2)}) collective-permute-start(f32[2,11,40,128]{3,2,1,0:T(8,128)} %get-tuple-element.10.e_ref), channel_id=1, source_target_pairs={{0,31},{1,0},{2,1},{3,2},{4,3},{5,4},{6,5},{7,6},{8,7},{9,8},{10,9... | collective-permute-start | bytes 1351688 | tf_op jit(solution)/shard_map/ppermute | solution.py:353
  27.3 14.9 %collective-permute-start.3 = (f32[2,11,40,128]{3,2,1,0:T(8,128)}, f32[2,11,40,128]{3,2,1,0:T(8,128)S(1)}, u32[]{:S(2)}, u32[]{:S(2)}) collective-permute-start(f32[2,11,40,128]{3,2,1,0:T(8,128)} %get-tuple-element.10.e_ref), channel_id=1, source_target_pairs={{0,1},{1,2},{2,3},{3,4},{4,5},{5,6},{6,7},{7,8},{8,9},{9,10},{10,1... | collective-permute-start | bytes 1351688 | tf_op jit(solution)/shard_map/ppermute | solution.py:352
  42.3 0.8 %copy-start = (f32[2,11,40,128]{3,2,1,0:T(8,128)}, f32[2,11,40,128]{3,2,1,0:T(8,128)S(1)}, u32[]{:S(2)}) copy-start(f32[2,11,40,128]{3,2,1,0:T(8,128)S(1)} %collective-permute-done.4.ee_ref) | copy-start | bytes 1351684
  42.3 0.9 %copy-start.1 = (f32[2,11,40,128]{3,2,1,0:T(8,128)}, f32[2,11,40,128]{3,2,1,0:T(8,128)S(1)}, u32[]{:S(2)}) copy-start(f32[2,11,40,128]{3,2,1,0:T(8,128)S(1)} %collective-permute-done.3.ew_ref) | copy-start | bytes 1351684

commit v11 on v10

--- a/solution.py
+++ b/solution.py
@@ -142,8 +142,9 @@
     south_ref, thk_ref, wind_ref, trc_ref, north_ref, tall_ref, sall_ref, nall_ref, rv_ref,
     thk_o, wind_o, trc_o, p_ref, mf_ref, sp_ref, s1_ref,
 ):
-    nf, _, halo, w = south_ref.shape
+    nf, per, halo, w = south_ref.shape
     nlev, rows = tall_ref.shape[0], tall_ref.shape[1]
+    nb = nlev // per
     i = pl.program_id(0)
     tall = rows + 2 * halo
     win = pl.ds(MARGIN, tall)
@@ -162,59 +163,62 @@
             p_ref[l, mid] = GRAV * acc[1]
             p_ref[l, bot] = GRAV * acc[2]
 
-    @pl.when(i < nlev)
+    @pl.when(i < nb)
     def _():
-        lev = i
-        for f in range(nf):
-            sp_ref[f, top] = south_ref[f, 0]
-            if f == 0:
-                sp_ref[f, mid] = thk_ref[0]
-            elif f < 3:
-                sp_ref[f, mid] = wind_ref[f - 1, 0]
-            else:
-                sp_ref[f, mid] = trc_ref[f - 3, 0]
-            sp_ref[f, bot] = north_ref[f, 0]
-
-        def store(f, x):
-            s1_ref[f, lev, win] = x
-
-        _substep(
-            lambda f, d: sp_ref[f, pl.ds(MARGIN + d, tall)],
-            store,
-            nf,
-            lambda d: p_ref[lev, pl.ds(MARGIN + d, tall)],
-            rv,
-            mf_ref,
-        )
-
-    @pl.when(i == nlev)
+        for j in range(per):
+            lev = i * per + j
+            sp = sp_ref.at[j]
+            for f in range(nf):
+                sp[f, top] = south_ref[f, j]
+                if f == 0:
+                    sp[f, mid] = thk_ref[j]
+                elif f < 3:
+                    sp[f, mid] = wind_ref[f - 1, j]
+                else:
+                    sp[f, mid] = trc_ref[f - 3, j]
+                sp[f, bot] = north_ref[f, j]
+
+            def store(f, x, lev=lev):
+                s1_ref[f, lev, win] = x
+
+            _substep(
+                lambda f, d, sp=sp: sp[f, pl.ds(MARGIN + d, tall)],
+                store,
+                nf,
+                lambda d, lev=lev: p_ref[lev, pl.ds(MARGIN + d, tall)],
+                rv,
+                mf_ref.at[j],
+            )
+
+    @pl.when(i == nb)
     def _():
         acc = None
         for l in reversed(range(nlev)):
             acc = s1_ref[0, l, win] if acc is None else acc + s1_ref[0, l, win]
             p_ref[l, win] = GRAV * acc
 
-    @pl.when(i >= nlev)
+    @pl.when(i >= nb)
     def _():
-        lev = i - nlev
-
-        def store(f, x):
-            x = x[halo : halo + rows]
-            if f == 0:
-                thk_o[0] = x
-            elif f < 3:
-                wind_o[f - 1, 0] = x
-            else:
-                trc_o[f - 3, 0] = x
-
-        _substep(
-            lambda f, d: s1_ref[f, lev, pl.ds(MARGIN + d, tall)],
-            store,
-            nf,
-            lambda d: p_ref[lev, pl.ds(MARGIN + d, tall)],
-            rv,
-            mf_ref,
-        )
+        for j in range(per):
+            lev = (i - nb) * per + j
+
+            def store(f, x, j=j):
+                x = x[halo : halo + rows]
+                if f == 0:
+                    thk_o[j] = x
+                elif f < 3:
+                    wind_o[f - 1, j] = x
+                else:
+                    trc_o[f - 3, j] = x
+
+            _substep(
+                lambda f, d, lev=lev: s1_ref[f, lev, pl.ds(MARGIN + d, tall)],
+                store,
+                nf,
+                lambda d, lev=lev: p_ref[lev, pl.ds(MARGIN + d, tall)],
+                rv,
+                mf_ref.at[j],
+            )
 
 
 def _final_kernel(
@@ -353,8 +357,10 @@
     from_east = lax.ppermute(edges, "lon", _shift_pairs(nlon, -1, True))
 
     step_flops = 60 * nf * nlev * tall * w
-    first = lambda i: jnp.minimum(i, nlev - 1)
-    second = lambda i: jnp.maximum(i - nlev, 0)
+    per = 2 if nlev % 2 == 0 else 1
+    nb = nlev // per
+    first = lambda i: jnp.minimum(i, nb - 1)
+    second = lambda i: jnp.maximum(i - nb, 0)
     raw = pl.pallas_call(
         _main_kernel,
         out_shape=(
@@ -362,27 +368,27 @@
             jax.ShapeDtypeStruct(winds.shape, jnp.float32),
             jax.ShapeDtypeStruct(tracer_mass.shape, jnp.float32),
         ),
-        grid=(2 * nlev,),
+        grid=(2 * nb,),
         in_specs=[
-            pl.BlockSpec((nf, 1, HALO, w), lambda i: (0, first(i), 0, 0)),
-            pl.BlockSpec((1, rows, w), lambda i: (first(i), 0, 0)),
-            pl.BlockSpec((2, 1, rows, w), lambda i: (0, first(i), 0, 0)),
-            pl.BlockSpec((nf - 3, 1, rows, w), lambda i: (0, first(i), 0, 0)),
-            pl.BlockSpec((nf, 1, HALO, w), lambda i: (0, first(i), 0, 0)),
+            pl.BlockSpec((nf, per, HALO, w), lambda i: (0, first(i), 0, 0)),
+            pl.BlockSpec((per, rows, w), lambda i: (first(i), 0, 0)),
+            pl.BlockSpec((2, per, rows, w), lambda i: (0, first(i), 0, 0)),
+            pl.BlockSpec((nf - 3, per, rows, w), lambda i: (0, first(i), 0, 0)),
+            pl.BlockSpec((nf, per, HALO, w), lambda i: (0, first(i), 0, 0)),
             pl.BlockSpec((nlev, rows, w), lambda i: (0, 0, 0)),
             pl.BlockSpec((1, nlev, HALO, w), lambda i: (0, 0, 0, 0)),
             pl.BlockSpec((1, nlev, HALO, w), lambda i: (0, 0, 0, 0)),
             pl.BlockSpec((3, tall, w), lambda i: (0, 0, 0)),
         ],
         out_specs=(
-            pl.BlockSpec((1, rows, w), lambda i: (second(i), 0, 0)),
-            pl.BlockSpec((2, 1, rows, w), lambda i: (0, second(i), 0, 0)),
-            pl.BlockSpec((nf - 3, 1, rows, w), lambda i: (0, second(i), 0, 0)),
+            pl.BlockSpec((per, rows, w), lambda i: (second(i), 0, 0)),
+            pl.BlockSpec((2, per, rows, w), lambda i: (0, second(i), 0, 0)),
+            pl.BlockSpec((nf - 3, per, rows, w), lambda i: (0, second(i), 0, 0)),
         ),
         scratch_shapes=[
             pltpu.VMEM((nlev, deep, w), jnp.float32),
-            pltpu.VMEM((nf, deep, w), jnp.float32),
-            pltpu.VMEM((nf, deep, w), jnp.float32),
+            pltpu.VMEM((per, nf, deep, w), jnp.float32),
+            pltpu.VMEM((per, nf, deep, w), jnp.float32),
             pltpu.VMEM((nf, nlev, deep, w), jnp.float32),
         ],
         compiler_params=pltpu.CompilerParams(dimension_semantics=("arbitrary",)),

time: 51.2 us -> 52.3 us (1.021)
  Pallas kernels: 28 us -> 29.2 us
    pallas_call x1, Pallas kernels: 14.9 us -> 16.1 us  [shards(): pl.pallas_call(_main_kernel, out_shape=(jax.ShapeDtypeStruct(thickness.sh...]
  transfers between devices with their start and end apart: 5 -> 5, of which waited for: 1 -> 1; matrix products, arithmetic and copies ran while one was open for 3% -> 3% of each run, Pallas kernels for 35% -> 37%
where the time goes in v11:
time: 52.3 us; the launch traced here: 52 us
  Pallas kernels  29.2 us (56%)
  starting transfers between devices  12.8 us (24%)
  waiting for transfers between devices  5.16 us (10%)
  local copies, waits for them, and re-layouts  2.3 us (4%)
  other arithmetic  1.91 us (4%)
  between operations  0.73 us (1%)
    pallas_call x1, Pallas kernels, shards(): pl.pallas_call(_main_kernel, out_shape=(jax.ShapeDtypeStruct(thickness.sh...  16.1 us
    pallas_call x1, Pallas kernels, shards(): pl.pallas_call(_final_kernel, out_shape=(jax.ShapeDtypeStruct(thickness.s...  7.65 us
    ppermute x1, starting transfers between devices, shards(): from_east = lax.ppermute(edges, 'lon', _shift_pairs(nlon, -1, True))  5.72 us
    ppermute x1, waiting for transfers between devices, shards(): from_south = lax.ppermute(top, 'lat', _shift_pairs(nlat, 1, False))  5.15 us
    ppermute x1, starting transfers between devices, shards(): from_north = lax.ppermute(bottom, 'lat', _shift_pairs(nlat, -1, False))  4.44 us
    pallas_call x1, Pallas kernels, shards(): _vmem_call(_edge_inner_kernel, jax.ShapeDtypeStruct((nslab, nf, rows, w),...  2.92 us
    pallas_call x1, Pallas kernels, shards(): pl.pallas_call(_edge_kernel, out_shape=(jax.ShapeDtypeStruct((nslab, nf,...  2.47 us
    ppermute x1, starting transfers between devices, shards(): from_south = lax.ppermute(top, 'lat', _shift_pairs(nlat, 1, False))  1.92 us
  transfers between devices with their start and end apart: 5, of which 1 were waited for; matrix products, arithmetic and copies ran while one was open for 3% of the time, Pallas kernels for 37%

profile of v11, /device:TPU:16, one launch (start us, length us, event | category | flops | bytes accessed | tf_op | source)
XLA Modules:
  0.0 52.0 jit_solution(9153001009978100456)
XLA Ops:
  0.6 1.2 %broadcast_select_fusion = (f32[11,8,4,128]{3,2,1,0:T(4,128)S(1)}, f32[11,8,4,128]{3,2,1,0:T(4,128)S(1)}, f32[11,8,4,128]{3,2,1,0:T(4,128)S(1)}) fusion(pred[]{:T(512)} %eq.7, f32[8,8,32,128]{3,2,1,0:T(8,128)} %trc_ref.3, f32[2,8,32,128]{3,2,1,0:T(8,128)} %wind_ref.3, f32[1,8,32,128]{3,2,1,0:T(8,128)} %bitcast.5), kind=kLoop, calls=%fused_computation.3 | loop fusion | flops 225280 | bytes 1982465 | tf_op jit(solution)/shard_map/jit(_where)/select_n | solution.py:338
  1.8 0.7 %collective-permute-start.2 = (f32[11,8,4,128]{3,2,1,0:T(4,128)S(1)}, f32[11,8,4,128]{3,2,1,0:T(4,128)S(1)}, u32[]{:S(2)}, u32[]{:S(2)}) collective-permute-start(f32[11,8,4,128]{3,2,1,0:T(4,128)S(1)} %get-tuple-element.17), channel_id=1, source_target_pairs={{0,16},{1,17},{2,18},{3,19},{4,20},{5,21},{6,22},{7,23},{8,24},{9,... | collective-permute-start | bytes 540680 | tf_op jit(solution)/shard_map/ppermute | solution.py:339
  2.5 4.4 %collective-permute-start.1 = (f32[11,8,4,128]{3,2,1,0:T(4,128)S(1)}, f32[11,8,4,128]{3,2,1,0:T(4,128)S(1)}, u32[]{:S(2)}, u32[]{:S(2)}) collective-permute-start(f32[11,8,4,128]{3,2,1,0:T(4,128)S(1)} %get-tuple-element.18), channel_id=1, source_target_pairs={{32,0},{64,32},{96,64},{128,96},{160,128},{192,160},{224,192},{33,... | collective-permute-start | bytes 540680 | tf_op jit(solution)/shard_map/ppermute | solution.py:332
  6.9 1.9 %collective-permute-start = (f32[11,8,4,128]{3,2,1,0:T(4,128)S(1)}, f32[11,8,4,128]{3,2,1,0:T(4,128)S(1)}, u32[]{:S(2)}, u32[]{:S(2)}) collective-permute-start(f32[11,8,4,128]{3,2,1,0:T(4,128)S(1)} %get-tuple-element.19), channel_id=1, source_target_pairs={{0,32},{32,64},{64,96},{96,128},{128,160},{160,192},{192,224},{1,3... | collective-permute-start | bytes 540680 | tf_op jit(solution)/shard_map/ppermute | solution.py:331
  8.9 0.1 fusion
  9.0 2.9 %shard_map.58.inner_ref = f32[2,11,32,128]{3,2,1,0:T(8,128)} custom-call(f32[8,32,128]{2,1,0:T(8,128)} %tall_ref.1, f32[2,8,32,128]{3,2,1,0:T(8,128)} %wind_ref.3, f32[8,8,32,128]{3,2,1,0:T(8,128)} %trc_ref.3), custom_call_target="tpu_custom_call" | custom-call | bytes 1441792 | tf_op jit(solution)/shard_map/pallas_call | solution.py:325
  11.9 0.7 %copy.9.rvi_ref = f32[3,40,1]{2,1,0:T(8,128)} copy(f32[3,40,1]{1,0,2:T(4,128)S(1)} %maximum_bitcast_fusion) | data formatting | bytes 960 | tf_op jit(solution)/shard_map/broadcast_in_dim | solution.py:323
  12.6 0.6 %add_convert_fusion.pole_at_ref = s32[2]{0:T(128)} fusion(pred[1]{0:T(512)(128)(4,1)} %bitcast.1, pred[1]{0:T(512)(128)(4,1)} %bitcast), kind=kLoop, calls=%fused_computation.5 | loop fusion | flops 4 | bytes 10 | tf_op jit(solution)/shard_map/convert_element_type | solution.py:340
  13.3 0.0 collective-permute-done.2.pole_ref
  13.3 0.0 copy-start.2
  13.3 0.0 collective-permute-done.1.fn_ref
  13.3 0.0 copy-start.3
  13.3 5.1 %collective-permute-done.fs_ref = f32[11,8,4,128]{3,2,1,0:T(4,128)S(1)} collective-permute-done((f32[11,8,4,128]{3,2,1,0:T(4,128)S(1)}, f32[11,8,4,128]{3,2,1,0:T(4,128)S(1)}, u32[]{:S(2)}, u32[]{:S(2)}) %collective-permute-start) | collective-permute-done | bytes 180256 | tf_op jit(solution)/shard_map/ppermute | solution.py:331
  18.4 0.0 copy-done.2
  18.4 0.0 copy-done.3
  18.5 0.0 copy-start.4
  18.5 0.7 %copy-done.4 = f32[11,8,4,128]{3,2,1,0:T(4,128)} copy-done((f32[11,8,4,128]{3,2,1,0:T(4,128)}, f32[11,8,4,128]{3,2,1,0:T(4,128)S(1)}, u32[]{:S(2)}) %copy-start.4) | copy-done | bytes 180248
  19.1 2.5 %shard_map.59 = (f32[2,11,40,128]{3,2,1,0:T(8,128)}, f32[11,8,4,128]{3,2,1,0:T(4,128)}, f32[11,8,4,128]{3,2,1,0:T(4,128)}, f32[3,40,128]{2,1,0:T(8,128)}) custom-call(s32[2]{0:T(128)} %add_convert_fusion.pole_at_ref, f32[11,8,4,128]{3,2,1,0:T(4,128)} %copy-done.4, f32[11,8,4,128]{3,2,1,0:T(4,128)} %copy-done.3, f32[11,8,4,128]{3,2,1,0:T(4,128)} %copy-done.2, ...), custom_call_target="tpu_custom_call" | custom-call | bytes 901120 | tf_op jit(solution)/shard_map/pallas_call | solution.py:344
  21.6 5.7 %collective-permute-start.4 = (f32[2,11,40,128]{3,2,1,0:T(8,128)}, f32[2,11,40,128]{3,2,1,0:T(8,128)S(1)}, u32[]{:S(2)}, u32[]{:S(2)}) collective-permute-start(f32[2,11,40,128]{3,2,1,0:T(8,128)} %get-tuple-element.10.e_ref), channel_id=1, source_target_pairs={{0,31},{1,0},{2,1},{3,2},{4,3},{5,4},{6,5},{7,6},{8,7},{9,8},{10,9... | collective-permute-start | bytes 1351688 | tf_op jit(solution)/shard_map/ppermute | solution.py:357
  27.3 0.0 collective-permute-start.3
  27.3 16.1 %shard_map.60 = (f32[8,32,128]{2,1,0:T(8,128)}, f32[2,8,32,128]{3,2,1,0:T(8,128)}, f32[8,8,32,128]{3,2,1,0:T(8,128)}) custom-call(f32[11,8,4,128]{3,2,1,0:T(4,128)} %get-tuple-element.12.south_ref.sall_ref, f32[8,32,128]{2,1,0:T(8,128)} %tall_ref.1, f32[2,8,32,128]{3,2,1,0:T(8,128)} %wind_ref.3, f32[8,8,32,128]{3,2,1,0:T(8,128)} %trc_ref.3, ...), custom_call_target="tpu_custom_call" | custom-call | flops 54067200 | bytes 3604480 | tf_op jit(solution)/shard_map/pallas_call | solution.py:364
  43.5 0.0 collective-permute-done.4.ee_ref
  43.5 0.0 copy-start
  43.5 0.0 collective-permute-done.3.ew_ref
  43.5 0.0 copy-start.1
  43.5 0.8 %copy-done = f32[2,11,40,128]{3,2,1,0:T(8,128)} copy-done((f32[2,11,40,128]{3,2,1,0:T(8,128)}, f32[2,11,40,128]{3,2,1,0:T(8,128)S(1)}, u32[]{:S(2)}) %copy-start) | copy-done | bytes 450584
  44.2 0.1 copy-done.1
  44.4 7.7 %shard_map.61 = (f32[8,32,128]{2,1,0:T(8,128)}, f32[2,8,32,128]{3,2,1,0:T(8,128)}, f32[8,8,32,128]{3,2,1,0:T(8,128)}) custom-call(f32[2,11,40,128]{3,2,1,0:T(8,128)} %get-tuple-element.10.e_ref, f32[2,11,40,128]{3,2,1,0:T(8,128)} %copy-done.1, f32[2,11,40,128]{3,2,1,0:T(8,128)} %copy-done, ...), custom_call_target="tpu_custom_call", output_to_operand_aliasing={{0}: (4, {}), {1}: (5, {}), {2}: (6, {})} | custom-call | flops 13516800 | bytes 1802240 | tf_op jit(solution)/shard_map/pallas_call | solution.py:400
  (2 shorter events, 0.1 us)
Async XLA Ops:
  1.8 11.5 %collective-permute-start.2 = (f32[11,8,4,128]{3,2,1,0:T(4,128)S(1)}, f32[11,8,4,128]{3,2,1,0:T(4,128)S(1)}, u32[]{:S(2)}, u32[]{:S(2)}) collective-permute-start(f32[11,8,4,128]{3,2,1,0:T(4,128)S(1)} %get-tuple-element.17), channel_id=1, source_target_pairs={{0,16},{1,17},{2,18},{3,19},{4,20},{5,21},{6,22},{7,23},{8,24},{9,... | collective-permute-start | bytes 540680 | tf_op jit(solution)/shard_map/ppermute | solution.py:339
  2.5 10.8 %collective-permute-start.1 = (f32[11,8,4,128]{3,2,1,0:T(4,128)S(1)}, f32[11,8,4,128]{3,2,1,0:T(4,128)S(1)}, u32[]{:S(2)}, u32[]{:S(2)}) collective-permute-start(f32[11,8,4,128]{3,2,1,0:T(4,128)S(1)} %get-tuple-element.18), channel_id=1, source_target_pairs={{32,0},{64,32},{96,64},{128,96},{160,128},{192,160},{224,192},{33,... | collective-permute-start | bytes 540680 | tf_op jit(solution)/shard_map/ppermute | solution.py:332
  6.9 11.5 %collective-permute-start = (f32[11,8,4,128]{3,2,1,0:T(4,128)S(1)}, f32[11,8,4,128]{3,2,1,0:T(4,128)S(1)}, u32[]{:S(2)}, u32[]{:S(2)}) collective-permute-start(f32[11,8,4,128]{3,2,1,0:T(4,128)S(1)} %get-tuple-element.19), channel_id=1, source_target_pairs={{0,32},{32,64},{64,96},{96,128},{128,160},{160,192},{192,224},{1,3... | collective-permute-start | bytes 540680 | tf_op jit(solution)/shard_map/ppermute | solution.py:331
  13.3 5.2 %copy-start.2 = (f32[11,8,4,128]{3,2,1,0:T(4,128)}, f32[11,8,4,128]{3,2,1,0:T(4,128)S(1)}, u32[]{:S(2)}) copy-start(f32[11,8,4,128]{3,2,1,0:T(4,128)S(1)} %collective-permute-done.2.pole_ref) | copy-start | bytes 540676
  13.3 5.2 %copy-start.3 = (f32[11,8,4,128]{3,2,1,0:T(4,128)}, f32[11,8,4,128]{3,2,1,0:T(4,128)S(1)}, u32[]{:S(2)}) copy-start(f32[11,8,4,128]{3,2,1,0:T(4,128)S(1)} %collective-permute-done.1.fn_ref) | copy-start | bytes 540676
  18.5 0.7 %copy-start.4 = (f32[11,8,4,128]{3,2,1,0:T(4,128)}, f32[11,8,4,128]{3,2,1,0:T(4,128)S(1)}, u32[]{:S(2)}) copy-start(f32[11,8,4,128]{3,2,1,0:T(4,128)S(1)} %collective-permute-done.fs_ref) | copy-start | bytes 540676
  21.6 21.9 %collective-permute-start.4 = (f32[2,11,40,128]{3,2,1,0:T(8,128)}, f32[2,11,40,128]{3,2,1,0:T(8,128)S(1)}, u32[]{:S(2)}, u32[]{:S(2)}) collective-permute-start(f32[2,11,40,128]{3,2,1,0:T(8,128)} %get-tuple-element.10.e_ref), channel_id=1, source_target_pairs={{0,31},{1,0},{2,1},{3,2},{4,3},{5,4},{6,5},{7,6},{8,7},{9,8},{10,9... | collective-permute-start | bytes 1351688 | tf_op jit(solution)/shard_map/ppermute | solution.py:357
  27.3 16.1 %collective-permute-start.3 = (f32[2,11,40,128]{3,2,1,0:T(8,128)}, f32[2,11,40,128]{3,2,1,0:T(8,128)S(1)}, u32[]{:S(2)}, u32[]{:S(2)}) collective-permute-start(f32[2,11,40,128]{3,2,1,0:T(8,128)} %get-tuple-element.10.e_ref), channel_id=1, source_target_pairs={{0,1},{1,2},{2,3},{3,4},{4,5},{5,6},{6,7},{7,8},{8,9},{9,10},{10,1... | collective-permute-start | bytes 1351688 | tf_op jit(solution)/shard_map/ppermute | solution.py:356
  43.5 0.8 %copy-start = (f32[2,11,40,128]{3,2,1,0:T(8,128)}, f32[2,11,40,128]{3,2,1,0:T(8,128)S(1)}, u32[]{:S(2)}) copy-start(f32[2,11,40,128]{3,2,1,0:T(8,128)S(1)} %collective-permute-done.4.ee_ref) | copy-start | bytes 1351684
  43.5 0.9 %copy-start.1 = (f32[2,11,40,128]{3,2,1,0:T(8,128)}, f32[2,11,40,128]{3,2,1,0:T(8,128)S(1)}, u32[]{:S(2)}) copy-start(f32[2,11,40,128]{3,2,1,0:T(8,128)S(1)} %collective-permute-done.3.ew_ref) | copy-start | bytes 1351684

commit v12 on v10

--- a/solution.py
+++ b/solution.py
@@ -199,7 +199,8 @@
         lev = i - nlev
 
         def store(f, x):
-            x = x[halo : halo + rows]
+            sp_ref[f, win] = x
+            x = sp_ref[f, mid]
             if f == 0:
                 thk_o[0] = x
             elif f < 3:

time: 51.2 us -> 51.4 us (level)
  no operation moved by 1% of the time
where the time goes in v12:
time: 51.4 us; the launch traced here: 51 us
  Pallas kernels  28.1 us (55%)
  starting transfers between devices  12.8 us (25%)
  waiting for transfers between devices  5.16 us (10%)
  local copies, waits for them, and re-layouts  2.3 us (4%)
  other arithmetic  1.91 us (4%)
  between operations  0.73 us (1%)
    pallas_call x1, Pallas kernels, shards(): pl.pallas_call(_main_kernel, out_shape=(jax.ShapeDtypeStruct(thickness.sh...  15.1 us
    pallas_call x1, Pallas kernels, shards(): pl.pallas_call(_final_kernel, out_shape=(jax.ShapeDtypeStruct(thickness.s...  7.65 us
    ppermute x1, starting transfers between devices, shards(): from_east = lax.ppermute(edges, 'lon', _shift_pairs(nlon, -1, True))  5.72 us
    ppermute x1, waiting for transfers between devices, shards(): from_south = lax.ppermute(top, 'lat', _shift_pairs(nlat, 1, False))  5.15 us
    ppermute x1, starting transfers between devices, shards(): from_north = lax.ppermute(bottom, 'lat', _shift_pairs(nlat, -1, False))  4.44 us
    pallas_call x1, Pallas kernels, shards(): _vmem_call(_edge_inner_kernel, jax.ShapeDtypeStruct((nslab, nf, rows, w),...  2.92 us
    pallas_call x1, Pallas kernels, shards(): pl.pallas_call(_edge_kernel, out_shape=(jax.ShapeDtypeStruct((nslab, nf,...  2.47 us
    ppermute x1, starting transfers between devices, shards(): from_south = lax.ppermute(top, 'lat', _shift_pairs(nlat, 1, False))  1.92 us
  transfers between devices with their start and end apart: 5, of which 1 were waited for; matrix products, arithmetic and copies ran while one was open for 3% of the time, Pallas kernels for 35%

profile of v12, /device:TPU:16, one launch (start us, length us, event | category | flops | bytes accessed | tf_op | source)
XLA Modules:
  0.0 51.0 jit_solution(8956742523355942695)
XLA Ops:
  0.6 1.2 %broadcast_select_fusion = (f32[11,8,4,128]{3,2,1,0:T(4,128)S(1)}, f32[11,8,4,128]{3,2,1,0:T(4,128)S(1)}, f32[11,8,4,128]{3,2,1,0:T(4,128)S(1)}) fusion(pred[]{:T(512)} %eq.7, f32[8,8,32,128]{3,2,1,0:T(8,128)} %trc_ref.3, f32[2,8,32,128]{3,2,1,0:T(8,128)} %wind_ref.3, f32[1,8,32,128]{3,2,1,0:T(8,128)} %bitcast.5), kind=kLoop, calls=%fused_computation.3 | loop fusion | flops 225280 | bytes 1982465 | tf_op jit(solution)/shard_map/jit(_where)/select_n | solution.py:335
  1.8 0.7 %collective-permute-start.2 = (f32[11,8,4,128]{3,2,1,0:T(4,128)S(1)}, f32[11,8,4,128]{3,2,1,0:T(4,128)S(1)}, u32[]{:S(2)}, u32[]{:S(2)}) collective-permute-start(f32[11,8,4,128]{3,2,1,0:T(4,128)S(1)} %get-tuple-element.17), channel_id=1, source_target_pairs={{0,16},{1,17},{2,18},{3,19},{4,20},{5,21},{6,22},{7,23},{8,24},{9,... | collective-permute-start | bytes 540680 | tf_op jit(solution)/shard_map/ppermute | solution.py:336
  2.5 4.4 %collective-permute-start.1 = (f32[11,8,4,128]{3,2,1,0:T(4,128)S(1)}, f32[11,8,4,128]{3,2,1,0:T(4,128)S(1)}, u32[]{:S(2)}, u32[]{:S(2)}) collective-permute-start(f32[11,8,4,128]{3,2,1,0:T(4,128)S(1)} %get-tuple-element.18), channel_id=1, source_target_pairs={{32,0},{64,32},{96,64},{128,96},{160,128},{192,160},{224,192},{33,... | collective-permute-start | bytes 540680 | tf_op jit(solution)/shard_map/ppermute | solution.py:329
  6.9 1.9 %collective-permute-start = (f32[11,8,4,128]{3,2,1,0:T(4,128)S(1)}, f32[11,8,4,128]{3,2,1,0:T(4,128)S(1)}, u32[]{:S(2)}, u32[]{:S(2)}) collective-permute-start(f32[11,8,4,128]{3,2,1,0:T(4,128)S(1)} %get-tuple-element.19), channel_id=1, source_target_pairs={{0,32},{32,64},{64,96},{96,128},{128,160},{160,192},{192,224},{1,3... | collective-permute-start | bytes 540680 | tf_op jit(solution)/shard_map/ppermute | solution.py:328
  8.9 0.1 fusion
  9.0 2.9 %shard_map.58.inner_ref = f32[2,11,32,128]{3,2,1,0:T(8,128)} custom-call(f32[8,32,128]{2,1,0:T(8,128)} %tall_ref.1, f32[2,8,32,128]{3,2,1,0:T(8,128)} %wind_ref.3, f32[8,8,32,128]{3,2,1,0:T(8,128)} %trc_ref.3), custom_call_target="tpu_custom_call" | custom-call | bytes 1441792 | tf_op jit(solution)/shard_map/pallas_call | solution.py:322
  11.9 0.7 %copy.9.rvi_ref = f32[3,40,1]{2,1,0:T(8,128)} copy(f32[3,40,1]{1,0,2:T(4,128)S(1)} %maximum_bitcast_fusion) | data formatting | bytes 960 | tf_op jit(solution)/shard_map/broadcast_in_dim | solution.py:320
  12.6 0.6 %add_convert_fusion.pole_at_ref = s32[2]{0:T(128)} fusion(pred[1]{0:T(512)(128)(4,1)} %bitcast.1, pred[1]{0:T(512)(128)(4,1)} %bitcast), kind=kLoop, calls=%fused_computation.5 | loop fusion | flops 4 | bytes 10 | tf_op jit(solution)/shard_map/convert_element_type | solution.py:337
  13.3 0.0 collective-permute-done.2.pole_ref
  13.3 0.0 copy-start.2
  13.3 0.0 collective-permute-done.1.fn_ref
  13.3 0.0 copy-start.3
  13.3 5.1 %collective-permute-done.fs_ref = f32[11,8,4,128]{3,2,1,0:T(4,128)S(1)} collective-permute-done((f32[11,8,4,128]{3,2,1,0:T(4,128)S(1)}, f32[11,8,4,128]{3,2,1,0:T(4,128)S(1)}, u32[]{:S(2)}, u32[]{:S(2)}) %collective-permute-start) | collective-permute-done | bytes 180256 | tf_op jit(solution)/shard_map/ppermute | solution.py:328
  18.4 0.0 copy-done.2
  18.4 0.0 copy-done.3
  18.5 0.0 copy-start.4
  18.5 0.7 %copy-done.4 = f32[11,8,4,128]{3,2,1,0:T(4,128)} copy-done((f32[11,8,4,128]{3,2,1,0:T(4,128)}, f32[11,8,4,128]{3,2,1,0:T(4,128)S(1)}, u32[]{:S(2)}) %copy-start.4) | copy-done | bytes 180248
  19.1 2.5 %shard_map.59 = (f32[2,11,40,128]{3,2,1,0:T(8,128)}, f32[11,8,4,128]{3,2,1,0:T(4,128)}, f32[11,8,4,128]{3,2,1,0:T(4,128)}, f32[3,40,128]{2,1,0:T(8,128)}) custom-call(s32[2]{0:T(128)} %add_convert_fusion.pole_at_ref, f32[11,8,4,128]{3,2,1,0:T(4,128)} %copy-done.4, f32[11,8,4,128]{3,2,1,0:T(4,128)} %copy-done.3, f32[11,8,4,128]{3,2,1,0:T(4,128)} %copy-done.2, ...), custom_call_target="tpu_custom_call" | custom-call | bytes 901120 | tf_op jit(solution)/shard_map/pallas_call | solution.py:341
  21.6 5.7 %collective-permute-start.4 = (f32[2,11,40,128]{3,2,1,0:T(8,128)}, f32[2,11,40,128]{3,2,1,0:T(8,128)S(1)}, u32[]{:S(2)}, u32[]{:S(2)}) collective-permute-start(f32[2,11,40,128]{3,2,1,0:T(8,128)} %get-tuple-element.10.e_ref), channel_id=1, source_target_pairs={{0,31},{1,0},{2,1},{3,2},{4,3},{5,4},{6,5},{7,6},{8,7},{9,8},{10,9... | collective-permute-start | bytes 1351688 | tf_op jit(solution)/shard_map/ppermute | solution.py:354
  27.3 0.0 collective-permute-start.3
  27.3 15.1 %shard_map.60 = (f32[8,32,128]{2,1,0:T(8,128)}, f32[2,8,32,128]{3,2,1,0:T(8,128)}, f32[8,8,32,128]{3,2,1,0:T(8,128)}) custom-call(f32[11,8,4,128]{3,2,1,0:T(4,128)} %get-tuple-element.12.south_ref.sall_ref, f32[8,32,128]{2,1,0:T(8,128)} %tall_ref.1, f32[2,8,32,128]{3,2,1,0:T(8,128)} %wind_ref.3, f32[8,8,32,128]{3,2,1,0:T(8,128)} %trc_ref.3, ...), custom_call_target="tpu_custom_call" | custom-call | flops 54067200 | bytes 3604480 | tf_op jit(solution)/shard_map/pallas_call | solution.py:359
  42.4 0.0 collective-permute-done.4.ee_ref
  42.4 0.0 copy-start
  42.4 0.0 collective-permute-done.3.ew_ref
  42.5 0.0 copy-start.1
  42.5 0.8 %copy-done = f32[2,11,40,128]{3,2,1,0:T(8,128)} copy-done((f32[2,11,40,128]{3,2,1,0:T(8,128)}, f32[2,11,40,128]{3,2,1,0:T(8,128)S(1)}, u32[]{:S(2)}) %copy-start) | copy-done | bytes 450584
  43.2 0.1 copy-done.1
  43.3 7.7 %shard_map.61 = (f32[8,32,128]{2,1,0:T(8,128)}, f32[2,8,32,128]{3,2,1,0:T(8,128)}, f32[8,8,32,128]{3,2,1,0:T(8,128)}) custom-call(f32[2,11,40,128]{3,2,1,0:T(8,128)} %get-tuple-element.10.e_ref, f32[2,11,40,128]{3,2,1,0:T(8,128)} %copy-done.1, f32[2,11,40,128]{3,2,1,0:T(8,128)} %copy-done, ...), custom_call_target="tpu_custom_call", output_to_operand_aliasing={{0}: (4, {}), {1}: (5, {}), {2}: (6, {})} | custom-call | flops 13516800 | bytes 1802240 | tf_op jit(solution)/shard_map/pallas_call | solution.py:395
  (2 shorter events, 0.1 us)
Async XLA Ops:
  1.8 11.5 %collective-permute-start.2 = (f32[11,8,4,128]{3,2,1,0:T(4,128)S(1)}, f32[11,8,4,128]{3,2,1,0:T(4,128)S(1)}, u32[]{:S(2)}, u32[]{:S(2)}) collective-permute-start(f32[11,8,4,128]{3,2,1,0:T(4,128)S(1)} %get-tuple-element.17), channel_id=1, source_target_pairs={{0,16},{1,17},{2,18},{3,19},{4,20},{5,21},{6,22},{7,23},{8,24},{9,... | collective-permute-start | bytes 540680 | tf_op jit(solution)/shard_map/ppermute | solution.py:336
  2.5 10.8 %collective-permute-start.1 = (f32[11,8,4,128]{3,2,1,0:T(4,128)S(1)}, f32[11,8,4,128]{3,2,1,0:T(4,128)S(1)}, u32[]{:S(2)}, u32[]{:S(2)}) collective-permute-start(f32[11,8,4,128]{3,2,1,0:T(4,128)S(1)} %get-tuple-element.18), channel_id=1, source_target_pairs={{32,0},{64,32},{96,64},{128,96},{160,128},{192,160},{224,192},{33,... | collective-permute-start | bytes 540680 | tf_op jit(solution)/shard_map/ppermute | solution.py:329
  6.9 11.5 %collective-permute-start = (f32[11,8,4,128]{3,2,1,0:T(4,128)S(1)}, f32[11,8,4,128]{3,2,1,0:T(4,128)S(1)}, u32[]{:S(2)}, u32[]{:S(2)}) collective-permute-start(f32[11,8,4,128]{3,2,1,0:T(4,128)S(1)} %get-tuple-element.19), channel_id=1, source_target_pairs={{0,32},{32,64},{64,96},{96,128},{128,160},{160,192},{192,224},{1,3... | collective-permute-start | bytes 540680 | tf_op jit(solution)/shard_map/ppermute | solution.py:328
  13.3 5.2 %copy-start.2 = (f32[11,8,4,128]{3,2,1,0:T(4,128)}, f32[11,8,4,128]{3,2,1,0:T(4,128)S(1)}, u32[]{:S(2)}) copy-start(f32[11,8,4,128]{3,2,1,0:T(4,128)S(1)} %collective-permute-done.2.pole_ref) | copy-start | bytes 540676
  13.3 5.2 %copy-start.3 = (f32[11,8,4,128]{3,2,1,0:T(4,128)}, f32[11,8,4,128]{3,2,1,0:T(4,128)S(1)}, u32[]{:S(2)}) copy-start(f32[11,8,4,128]{3,2,1,0:T(4,128)S(1)} %collective-permute-done.1.fn_ref) | copy-start | bytes 540676
  18.5 0.7 %copy-start.4 = (f32[11,8,4,128]{3,2,1,0:T(4,128)}, f32[11,8,4,128]{3,2,1,0:T(4,128)S(1)}, u32[]{:S(2)}) copy-start(f32[11,8,4,128]{3,2,1,0:T(4,128)S(1)} %collective-permute-done.fs_ref) | copy-start | bytes 540676
  21.6 20.8 %collective-permute-start.4 = (f32[2,11,40,128]{3,2,1,0:T(8,128)}, f32[2,11,40,128]{3,2,1,0:T(8,128)S(1)}, u32[]{:S(2)}, u32[]{:S(2)}) collective-permute-start(f32[2,11,40,128]{3,2,1,0:T(8,128)} %get-tuple-element.10.e_ref), channel_id=1, source_target_pairs={{0,31},{1,0},{2,1},{3,2},{4,3},{5,4},{6,5},{7,6},{8,7},{9,8},{10,9... | collective-permute-start | bytes 1351688 | tf_op jit(solution)/shard_map/ppermute | solution.py:354
  27.3 15.1 %collective-permute-start.3 = (f32[2,11,40,128]{3,2,1,0:T(8,128)}, f32[2,11,40,128]{3,2,1,0:T(8,128)S(1)}, u32[]{:S(2)}, u32[]{:S(2)}) collective-permute-start(f32[2,11,40,128]{3,2,1,0:T(8,128)} %get-tuple-element.10.e_ref), channel_id=1, source_target_pairs={{0,1},{1,2},{2,3},{3,4},{4,5},{5,6},{6,7},{7,8},{8,9},{9,10},{10,1... | collective-permute-start | bytes 1351688 | tf_op jit(solution)/shard_map/ppermute | solution.py:353
  42.4 0.8 %copy-start = (f32[2,11,40,128]{3,2,1,0:T(8,128)}, f32[2,11,40,128]{3,2,1,0:T(8,128)S(1)}, u32[]{:S(2)}) copy-start(f32[2,11,40,128]{3,2,1,0:T(8,128)S(1)} %collective-permute-done.4.ee_ref) | copy-start | bytes 1351684
  42.5 0.9 %copy-start.1 = (f32[2,11,40,128]{3,2,1,0:T(8,128)}, f32[2,11,40,128]{3,2,1,0:T(8,128)S(1)}, u32[]{:S(2)}) copy-start(f32[2,11,40,128]{3,2,1,0:T(8,128)S(1)} %collective-permute-done.3.ew_ref) | copy-start | bytes 1351684

commit v13 on v10

--- a/solution.py
+++ b/solution.py
@@ -111,16 +111,15 @@
             e_ref[s, f] = _pack_own(get, nlev, rows, w, s, zeros)
 
 
-def _edge_kernel(
-    pole_at_ref, fs_ref, fn_ref, pole_ref, inner_ref, rvi_ref, e_ref, south_ref, north_ref, rv_ref
-):
+def _edge_kernel(fs_ref, fn_ref, pole_ref, inner_ref, rvi_ref, e_ref, south_ref, north_ref, rv_ref):
     nf, nlev, halo, w = fs_ref.shape
     nslab, rows = inner_ref.shape[0], inner_ref.shape[2]
     tall = rv_ref.shape[1]
     for k in range(rv_ref.shape[0]):
         rv_ref[k] = jnp.broadcast_to(rvi_ref[k], (tall, w))
-    at_south = pole_at_ref[0] == 1
-    at_north = pole_at_ref[1] == 1
+    band = lax.axis_index("lat")
+    at_south = band == 0
+    at_north = band == lax.axis_size("lat") - 1
     for f in range(nf):
         for lev in range(nlev):
             for k in range(halo):
@@ -333,8 +332,6 @@
             pole_pairs.append((b * nlon + s, b * nlon + (s + half) % nlon))
     pole_out = jnp.where(band == 0, bottom, top)
     pole_in = lax.ppermute(pole_out, ("lat", "lon"), pole_pairs)
-    pole_at = jnp.stack([band == 0, band == nlat - 1]).astype(jnp.int32)
-
     slab = nf * tall * w * 4
     vmem = pl.BlockSpec(memory_space=pltpu.VMEM)
     edges, south, north, rowvec = pl.pallas_call(
@@ -345,10 +342,10 @@
             jax.ShapeDtypeStruct(top.shape, jnp.float32),
             jax.ShapeDtypeStruct((3, tall, w), jnp.float32),
         ),
-        in_specs=[pl.BlockSpec(memory_space=pltpu.SMEM)] + [vmem] * 5,
+        in_specs=[vmem] * 5,
         out_specs=(vmem, vmem, vmem, vmem),
         cost_estimate=pl.CostEstimate(flops=0, bytes_accessed=2 * slab * nslab, transcendentals=0),
-    )(pole_at, from_south, from_north, pole_in, inner_edges, rowvec)
+    )(from_south, from_north, pole_in, inner_edges, rowvec)
     from_west = lax.ppermute(edges, "lon", _shift_pairs(nlon, 1, True))
     from_east = lax.ppermute(edges, "lon", _shift_pairs(nlon, -1, True))
 

time: 51.2 us -> 51.2 us (level)
  other arithmetic: 1.91 us -> 1.27 us
  waiting for transfers between devices: 5.16 us -> 5.8 us
    convert_element_type x1 -> x0, other arithmetic: 0.65 us -> none  [shards(): pole_at = jnp.stack([band == 0, band == nlat - 1]).astype(jnp.int32)]
    ppermute x1, waiting for transfers between devices: 5.15 us -> 5.79 us  [shards(): from_south = lax.ppermute(top, 'lat', _shift_pairs(nlat, 1, False))]
  transfers between devices with their start and end apart: 5 -> 5, of which waited for: 1 -> 1; matrix products, arithmetic and copies ran while one was open for 3% -> 2% of each run, Pallas kernels for 35% -> 35%
where the time goes in v13:
time: 51.2 us; the launch traced here: 50.8 us
  Pallas kernels  28 us (55%)
  starting transfers between devices  12.8 us (25%)
  waiting for transfers between devices  5.8 us (11%)
  local copies, waits for them, and re-layouts  2.3 us (4%)
  other arithmetic  1.27 us (2%)
  between operations  0.72 us (1%)
    pallas_call x1, Pallas kernels, shards(): pl.pallas_call(_main_kernel, out_shape=(jax.ShapeDtypeStruct(thickness.sh...  14.9 us
    pallas_call x1, Pallas kernels, shards(): pl.pallas_call(_final_kernel, out_shape=(jax.ShapeDtypeStruct(thickness.s...  7.65 us
    ppermute x1, waiting for transfers between devices, shards(): from_south = lax.ppermute(top, 'lat', _shift_pairs(nlat, 1, False))  5.79 us
    ppermute x1, starting transfers between devices, shards(): from_east = lax.ppermute(edges, 'lon', _shift_pairs(nlon, -1, True))  5.72 us
    ppermute x1, starting transfers between devices, shards(): from_north = lax.ppermute(bottom, 'lat', _shift_pairs(nlat, -1, False))  4.44 us
    pallas_call x1, Pallas kernels, shards(): _vmem_call(_edge_inner_kernel, jax.ShapeDtypeStruct((nslab, nf, rows, w),...  2.92 us
    pallas_call x1, Pallas kernels, shards(): pl.pallas_call(_edge_kernel, out_shape=(jax.ShapeDtypeStruct((nslab, nf,...  2.47 us
    ppermute x1, starting transfers between devices, shards(): from_south = lax.ppermute(top, 'lat', _shift_pairs(nlat, 1, False))  1.92 us
  transfers between devices with their start and end apart: 5, of which 1 were waited for; matrix products, arithmetic and copies ran while one was open for 2% of the time, Pallas kernels for 35%

profile of v13, /device:TPU:16, one launch (start us, length us, event | category | flops | bytes accessed | tf_op | source)
XLA Modules:
  0.0 50.8 jit_solution(9243095527733138623)
XLA Ops:
  0.6 1.2 %broadcast_select_fusion = (f32[11,8,4,128]{3,2,1,0:T(4,128)S(1)}, f32[11,8,4,128]{3,2,1,0:T(4,128)S(1)}, f32[11,8,4,128]{3,2,1,0:T(4,128)S(1)}) fusion(pred[]{:T(512)S(6)} %eq.3, f32[8,8,32,128]{3,2,1,0:T(8,128)} %trc_ref.3, f32[2,8,32,128]{3,2,1,0:T(8,128)} %wind_ref.3, f32[1,8,32,128]{3,2,1,0:T(8,128)} %bitcast.3), kind=kLoop, calls=%fused_computation.3 | loop fusion | flops 225280 | bytes 1982465 | tf_op jit(solution)/shard_map/jit(_where)/select_n | solution.py:333
  1.8 0.7 %collective-permute-start.2 = (f32[11,8,4,128]{3,2,1,0:T(4,128)S(1)}, f32[11,8,4,128]{3,2,1,0:T(4,128)S(1)}, u32[]{:S(2)}, u32[]{:S(2)}) collective-permute-start(f32[11,8,4,128]{3,2,1,0:T(4,128)S(1)} %get-tuple-element.17), channel_id=1, source_target_pairs={{0,16},{1,17},{2,18},{3,19},{4,20},{5,21},{6,22},{7,23},{8,24},{9,... | collective-permute-start | bytes 540680 | tf_op jit(solution)/shard_map/ppermute | solution.py:334
  2.5 4.4 %collective-permute-start.1 = (f32[11,8,4,128]{3,2,1,0:T(4,128)S(1)}, f32[11,8,4,128]{3,2,1,0:T(4,128)S(1)}, u32[]{:S(2)}, u32[]{:S(2)}) collective-permute-start(f32[11,8,4,128]{3,2,1,0:T(4,128)S(1)} %get-tuple-element.18), channel_id=1, source_target_pairs={{32,0},{64,32},{96,64},{128,96},{160,128},{192,160},{224,192},{33,... | collective-permute-start | bytes 540680 | tf_op jit(solution)/shard_map/ppermute | solution.py:327
  6.9 1.9 %collective-permute-start = (f32[11,8,4,128]{3,2,1,0:T(4,128)S(1)}, f32[11,8,4,128]{3,2,1,0:T(4,128)S(1)}, u32[]{:S(2)}, u32[]{:S(2)}) collective-permute-start(f32[11,8,4,128]{3,2,1,0:T(4,128)S(1)} %get-tuple-element.19), channel_id=1, source_target_pairs={{0,32},{32,64},{64,96},{96,128},{128,160},{160,192},{192,224},{1,3... | collective-permute-start | bytes 540680 | tf_op jit(solution)/shard_map/ppermute | solution.py:326
  8.9 2.9 %shard_map.58.inner_ref = f32[2,11,32,128]{3,2,1,0:T(8,128)} custom-call(f32[8,32,128]{2,1,0:T(8,128)} %tall_ref.1, f32[2,8,32,128]{3,2,1,0:T(8,128)} %wind_ref.3, f32[8,8,32,128]{3,2,1,0:T(8,128)} %trc_ref.3), custom_call_target="tpu_custom_call" | custom-call | bytes 1441792 | tf_op jit(solution)/shard_map/pallas_call | solution.py:320
  11.8 0.1 cosine_abs_fusion
  11.9 0.7 %copy.9.rvi_ref = f32[3,40,1]{2,1,0:T(8,128)} copy(f32[3,40,1]{1,0,2:T(4,128)S(1)} %maximum_bitcast_fusion) | data formatting | bytes 960 | tf_op jit(solution)/shard_map/broadcast_in_dim | solution.py:318
  12.6 0.0 collective-permute-done.2.pole_ref
  12.6 0.0 copy-start.2
  12.6 0.0 collective-permute-done.1.fn_ref
  12.6 0.0 copy-start.3
  12.7 5.8 %collective-permute-done.fs_ref = f32[11,8,4,128]{3,2,1,0:T(4,128)S(1)} collective-permute-done((f32[11,8,4,128]{3,2,1,0:T(4,128)S(1)}, f32[11,8,4,128]{3,2,1,0:T(4,128)S(1)}, u32[]{:S(2)}, u32[]{:S(2)}) %collective-permute-start) | collective-permute-done | bytes 180256 | tf_op jit(solution)/shard_map/ppermute | solution.py:326
  18.4 0.0 copy-done.2
  18.4 0.0 copy-done.3
  18.5 0.0 copy-start.4
  18.5 0.7 %copy-done.4 = f32[11,8,4,128]{3,2,1,0:T(4,128)} copy-done((f32[11,8,4,128]{3,2,1,0:T(4,128)}, f32[11,8,4,128]{3,2,1,0:T(4,128)S(1)}, u32[]{:S(2)}) %copy-start.4) | copy-done | bytes 180248
  19.1 2.5 %shard_map.59 = (f32[2,11,40,128]{3,2,1,0:T(8,128)}, f32[11,8,4,128]{3,2,1,0:T(4,128)}, f32[11,8,4,128]{3,2,1,0:T(4,128)}, f32[3,40,128]{2,1,0:T(8,128)}) custom-call(f32[11,8,4,128]{3,2,1,0:T(4,128)} %copy-done.4, f32[11,8,4,128]{3,2,1,0:T(4,128)} %copy-done.3, f32[11,8,4,128]{3,2,1,0:T(4,128)} %copy-done.2, f32[2,11,32,128]{3,2,1,0:T(8,128)} %shard_map.58.inner_ref, ...), custom_call_target="tpu_custom_call" | custom-call | bytes 901120 | tf_op jit(solution)/shard_map/pallas_call | solution.py:337
  21.6 5.7 %collective-permute-start.4 = (f32[2,11,40,128]{3,2,1,0:T(8,128)}, f32[2,11,40,128]{3,2,1,0:T(8,128)S(1)}, u32[]{:S(2)}, u32[]{:S(2)}) collective-permute-start(f32[2,11,40,128]{3,2,1,0:T(8,128)} %get-tuple-element.10.e_ref), channel_id=1, source_target_pairs={{0,31},{1,0},{2,1},{3,2},{4,3},{5,4},{6,5},{7,6},{8,7},{9,8},{10,9... | collective-permute-start | bytes 1351688 | tf_op jit(solution)/shard_map/ppermute | solution.py:350
  27.3 0.0 collective-permute-start.3
  27.3 14.9 %shard_map.60 = (f32[8,32,128]{2,1,0:T(8,128)}, f32[2,8,32,128]{3,2,1,0:T(8,128)}, f32[8,8,32,128]{3,2,1,0:T(8,128)}) custom-call(f32[11,8,4,128]{3,2,1,0:T(4,128)} %get-tuple-element.12.south_ref.sall_ref, f32[8,32,128]{2,1,0:T(8,128)} %tall_ref.1, f32[2,8,32,128]{3,2,1,0:T(8,128)} %wind_ref.3, f32[8,8,32,128]{3,2,1,0:T(8,128)} %trc_ref.3, ...), custom_call_target="tpu_custom_call" | custom-call | flops 54067200 | bytes 3604480 | tf_op jit(solution)/shard_map/pallas_call | solution.py:355
  42.2 0.0 collective-permute-done.4.ee_ref
  42.3 0.0 copy-start
  42.3 0.0 collective-permute-done.3.ew_ref
  42.3 0.0 copy-start.1
  42.3 0.8 %copy-done = f32[2,11,40,128]{3,2,1,0:T(8,128)} copy-done((f32[2,11,40,128]{3,2,1,0:T(8,128)}, f32[2,11,40,128]{3,2,1,0:T(8,128)S(1)}, u32[]{:S(2)}) %copy-start) | copy-done | bytes 450584
  43.0 0.1 copy-done.1
  43.2 7.7 %shard_map.61 = (f32[8,32,128]{2,1,0:T(8,128)}, f32[2,8,32,128]{3,2,1,0:T(8,128)}, f32[8,8,32,128]{3,2,1,0:T(8,128)}) custom-call(f32[2,11,40,128]{3,2,1,0:T(8,128)} %get-tuple-element.10.e_ref, f32[2,11,40,128]{3,2,1,0:T(8,128)} %copy-done.1, f32[2,11,40,128]{3,2,1,0:T(8,128)} %copy-done, ...), custom_call_target="tpu_custom_call", output_to_operand_aliasing={{0}: (4, {}), {1}: (5, {}), {2}: (6, {})} | custom-call | flops 13516800 | bytes 1802240 | tf_op jit(solution)/shard_map/pallas_call | solution.py:391
  (2 shorter events, 0.1 us)
Async XLA Ops:
  1.8 10.8 %collective-permute-start.2 = (f32[11,8,4,128]{3,2,1,0:T(4,128)S(1)}, f32[11,8,4,128]{3,2,1,0:T(4,128)S(1)}, u32[]{:S(2)}, u32[]{:S(2)}) collective-permute-start(f32[11,8,4,128]{3,2,1,0:T(4,128)S(1)} %get-tuple-element.17), channel_id=1, source_target_pairs={{0,16},{1,17},{2,18},{3,19},{4,20},{5,21},{6,22},{7,23},{8,24},{9,... | collective-permute-start | bytes 540680 | tf_op jit(solution)/shard_map/ppermute | solution.py:334
  2.5 10.2 %collective-permute-start.1 = (f32[11,8,4,128]{3,2,1,0:T(4,128)S(1)}, f32[11,8,4,128]{3,2,1,0:T(4,128)S(1)}, u32[]{:S(2)}, u32[]{:S(2)}) collective-permute-start(f32[11,8,4,128]{3,2,1,0:T(4,128)S(1)} %get-tuple-element.18), channel_id=1, source_target_pairs={{32,0},{64,32},{96,64},{128,96},{160,128},{192,160},{224,192},{33,... | collective-permute-start | bytes 540680 | tf_op jit(solution)/shard_map/ppermute | solution.py:327
  6.9 11.5 %collective-permute-start = (f32[11,8,4,128]{3,2,1,0:T(4,128)S(1)}, f32[11,8,4,128]{3,2,1,0:T(4,128)S(1)}, u32[]{:S(2)}, u32[]{:S(2)}) collective-permute-start(f32[11,8,4,128]{3,2,1,0:T(4,128)S(1)} %get-tuple-element.19), channel_id=1, source_target_pairs={{0,32},{32,64},{64,96},{96,128},{128,160},{160,192},{192,224},{1,3... | collective-permute-start | bytes 540680 | tf_op jit(solution)/shard_map/ppermute | solution.py:326
  12.6 5.8 %copy-start.2 = (f32[11,8,4,128]{3,2,1,0:T(4,128)}, f32[11,8,4,128]{3,2,1,0:T(4,128)S(1)}, u32[]{:S(2)}) copy-start(f32[11,8,4,128]{3,2,1,0:T(4,128)S(1)} %collective-permute-done.2.pole_ref) | copy-start | bytes 540676
  12.6 5.8 %copy-start.3 = (f32[11,8,4,128]{3,2,1,0:T(4,128)}, f32[11,8,4,128]{3,2,1,0:T(4,128)S(1)}, u32[]{:S(2)}) copy-start(f32[11,8,4,128]{3,2,1,0:T(4,128)S(1)} %collective-permute-done.1.fn_ref) | copy-start | bytes 540676
  18.5 0.7 %copy-start.4 = (f32[11,8,4,128]{3,2,1,0:T(4,128)}, f32[11,8,4,128]{3,2,1,0:T(4,128)S(1)}, u32[]{:S(2)}) copy-start(f32[11,8,4,128]{3,2,1,0:T(4,128)S(1)} %collective-permute-done.fs_ref) | copy-start | bytes 540676
  21.6 20.7 %collective-permute-start.4 = (f32[2,11,40,128]{3,2,1,0:T(8,128)}, f32[2,11,40,128]{3,2,1,0:T(8,128)S(1)}, u32[]{:S(2)}, u32[]{:S(2)}) collective-permute-start(f32[2,11,40,128]{3,2,1,0:T(8,128)} %get-tuple-element.10.e_ref), channel_id=1, source_target_pairs={{0,31},{1,0},{2,1},{3,2},{4,3},{5,4},{6,5},{7,6},{8,7},{9,8},{10,9... | collective-permute-start | bytes 1351688 | tf_op jit(solution)/shard_map/ppermute | solution.py:350
  27.3 14.9 %collective-permute-start.3 = (f32[2,11,40,128]{3,2,1,0:T(8,128)}, f32[2,11,40,128]{3,2,1,0:T(8,128)S(1)}, u32[]{:S(2)}, u32[]{:S(2)}) collective-permute-start(f32[2,11,40,128]{3,2,1,0:T(8,128)} %get-tuple-element.10.e_ref), channel_id=1, source_target_pairs={{0,1},{1,2},{2,3},{3,4},{4,5},{5,6},{6,7},{7,8},{8,9},{9,10},{10,1... | collective-permute-start | bytes 1351688 | tf_op jit(solution)/shard_map/ppermute | solution.py:349
  42.3 0.8 %copy-start = (f32[2,11,40,128]{3,2,1,0:T(8,128)}, f32[2,11,40,128]{3,2,1,0:T(8,128)S(1)}, u32[]{:S(2)}) copy-start(f32[2,11,40,128]{3,2,1,0:T(8,128)S(1)} %collective-permute-done.4.ee_ref) | copy-start | bytes 1351684
  42.3 0.9 %copy-start.1 = (f32[2,11,40,128]{3,2,1,0:T(8,128)}, f32[2,11,40,128]{3,2,1,0:T(8,128)S(1)}, u32[]{:S(2)}) copy-start(f32[2,11,40,128]{3,2,1,0:T(8,128)S(1)} %collective-permute-done.3.ew_ref) | copy-start | bytes 1351684
